TPU v7x, 512 devices: a whole 4x8x8 slice. The times are simulated.
512 devices in a mesh: blk: 64 (over x, z, y_hi), dp: 8 (over y_lo, core).
Axes of the slice: x: 4, y: 8 (y_hi: 2, y_lo: 4; y = y_hi * 4 + y_lo), z: 8, core: 2. Of those that a mesh axis runs over, the one named last changes fastest.
Arguments:
- input_field: bfloat16 [262144, 2048], P('blk', 'dp'), may hold values from -6 to 6
- target_field: bfloat16 [262144, 2048], P('blk', 'dp'), may hold values from -6 to 6
- first_factor: bfloat16 [256, 1024, 256], P('dp', 'blk'), may hold values from -0.375 to 0.375
- second_factor: bfloat16 [256, 1024, 256], P('dp', 'blk'), may hold values from -0.375 to 0.375
Outputs:
- first_grad: bfloat16 [256, 1024, 256], P('dp', 'blk')
- second_grad: bfloat16 [256, 1024, 256], P('dp', 'blk')
All inputs are finite; a program needn't handle non-finite values.
Results may differ from a plain program's by a relative error of at most 0.012.
Values may be sent and summed in bfloat16 or wider, within the bound.
No kernel may reach another device: no remote copies, remote signals or barrier semaphores. Data moves between devices by JAX's collectives and lax.ppermute only.
A program may use at most 64 MiB of HBM per device.

v0:
```python
import math

import jax
import jax.numpy as jnp
from jax import lax
from jax.sharding import PartitionSpec as P

NB = 1024
BS = 256


tanh_scale = 0.7978845608028654
cubic_coef = 0.044715


def gelu_value(values):
    inner = jnp.tanh(tanh_scale * (values + cubic_coef * values * values * values))
    return 0.5 * values * (1.0 + inner)


def gelu_slope(values):
    inner = jnp.tanh(tanh_scale * (values + cubic_coef * values * values * values))
    return 0.5 * (1.0 + inner) + 0.5 * values * (1.0 - inner * inner) * tanh_scale * (
        1.0 + 3.0 * cubic_coef * values * values
    )


def shards(input_field, target_field, first_factor, second_factor):
    block_count = first_factor.shape[1]
    block_size = first_factor.shape[2]
    second_rows_local = second_factor.shape[0]
    row_count = input_field.shape[1]
    replica_count = lax.axis_size("dp")
    group_count = NB // BS
    inner_count = block_count // group_count
    scale_factor = 1.0 / math.sqrt(row_count * replica_count)
    inputs = input_field.reshape(block_count, block_size, row_count)
    first_full = lax.all_gather(first_factor, "dp", axis=0, tiled=True)
    pre_act = jnp.einsum("bkr,kbi->bir", inputs, first_full, preferred_element_type=jnp.float32)
    activated = gelu_value(pre_act).astype(jnp.bfloat16)
    received = lax.all_to_all(activated, "blk", split_axis=1, concat_axis=0, tiled=True)
    permuted = received.reshape(group_count, block_size, inner_count, row_count)
    targets = target_field.reshape(inner_count, group_count, block_size, row_count)
    piece_rows = lax.all_gather(second_factor, "dp", axis=0, tiled=True)
    count = piece_rows.shape[0]
    permuted_part = permuted
    split_part = piece_rows.reshape(count, inner_count, group_count, block_size)
    predicted = jnp.einsum(
        "gcir,cigj->igjr", permuted_part, split_part, preferred_element_type=jnp.float32
    )
    residual = ((predicted - targets.astype(jnp.float32)) * scale_factor).astype(jnp.bfloat16)
    piece_rows = lax.all_gather(second_factor, "dp", axis=0, tiled=True)
    count = piece_rows.shape[0]
    split_part = piece_rows.reshape(count, inner_count, group_count, block_size)
    permuted_grad = jnp.einsum(
        "cigj,igjr->gcir", split_part, residual, preferred_element_type=jnp.float32
    ).astype(jnp.bfloat16)
    permuted_part = permuted
    term = jnp.einsum(
        "gcir,igjr->cigj", permuted_part, residual, preferred_element_type=jnp.float32
    )
    second_out = lax.psum_scatter(
        term.reshape(second_rows_local * lax.axis_size("dp"), block_count, block_size).astype(
            jnp.bfloat16
        ),
        "dp",
        scatter_dimension=0,
        tiled=True,
    )
    sending = permuted_grad.reshape(group_count * block_size, inner_count, row_count)
    activated_grad = lax.all_to_all(sending, "blk", split_axis=0, concat_axis=1, tiled=True)
    pre_grad = (activated_grad.astype(jnp.float32) * gelu_slope(pre_act)).astype(jnp.bfloat16)
    first_sum = lax.psum_scatter(
        jnp.einsum("bkr,bir->kbi", inputs, pre_grad, preferred_element_type=jnp.float32).astype(
            jnp.bfloat16
        ),
        "dp",
        scatter_dimension=0,
        tiled=True,
    )
    return (first_sum, second_out)


def solution(mesh):
    return jax.shard_map(
        shards,
        mesh=mesh,
        in_specs=(P("blk", "dp"), P("blk", "dp"), P("dp", "blk", None), P("dp", "blk", None)),
        out_specs=(P("dp", "blk", None), P("dp", "blk", None)),
        check_vma=False,
    )
```

profile of v0, /device:TPU:1, one launch (start us, length us, event | category | flops | bytes accessed | tf_op | source)
XLA Modules:
  0.0 306.6 jit_solution(16598214252673159265)
XLA Ops:
  7.2 0.0 copy-start
  7.2 0.0 all-gather.3.cloned.1.call-start
  7.2 1.9 copy.40
  9.1 0.0 all-gather.3.cloned.1.call-update
  9.1 47.4 %all-gather.3.cloned.1.call-done = bf16[256,16,256]{2,0,1:T(8,128)(2,1)} async-done(((bf16[32,16,256]{2,0,1:T(8,128)(2,1)}), bf16[256,16,256]{2,0,1:T(8,128)(2,1)}) %all-gather.3.cloned.1.call-update) | async-done | bytes 2097168 | tf_op jit(solution)/shard_map/all_gather | solution.py:38
  56.5 0.0 copy-done
  56.5 5.2 %multiply_convert_fusion = (bf16[16,256,256]{2,1,0:T(8,128)(2,1)S(1)}, f32[16,256,256]{2,1,0:T(8,128)}) fusion(bf16[256,16,256]{2,0,1:T(8,128)(2,1)} %all-gather.3.cloned.1.call-done, bf16[16,256,256]{2,1,0:T(8,128)(2,1)S(1)} %bitcast.33), kind=kOutput, calls=%fused_computation.13 | convolution fusion | flops 546308096 | bytes 10485760 | tf_op jit(solution)/shard_map/bkr,kbi->bir/dot_general | solution.py:39
  61.8 2.5 copy.41
  64.3 13.7 %all-to-all-start = ((bf16[16,256,256]{2,0,1:T(8,128)(2,1)}), bf16[16,256,256]{2,0,1:T(8,128)(2,1)}, u32[]{:S(2)}, u32[]{:S(2)}) async-start(bf16[16,256,256]{2,0,1:T(8,128)(2,1)} %copy.41), calls=%async_computation | async-start | bytes 4194304 | tf_op jit(solution)/shard_map/all_to_all | solution.py:41
  78.0 0.0 all-gather.5.cloned.1.call-start
  78.0 0.7 all-gather.5.cloned.1.call-update
  78.7 4.6 %copy.45 = f32[4,4,256,256]{2,3,1,0:T(8,128)} copy(bf16[4,4,256,256]{3,2,1,0:T(8,128)(2,1)} %bitcast.42) | data formatting | bytes 6291456 | tf_op jit(solution)/shard_map/convert_element_type | solution.py:51
  83.3 63.7 %all-gather.5.cloned.1.call-done = bf16[256,16,256]{2,1,0:T(8,128)(2,1)} async-done(((bf16[32,16,256]{2,1,0:T(8,128)(2,1)}), bf16[256,16,256]{2,1,0:T(8,128)(2,1)}) %all-gather.5.cloned.1.call-update) | async-done | bytes 2097168 | tf_op jit(solution)/shard_map/all_gather | solution.py:44
  147.0 3.6 %copy.43 = bf16[256,16,256]{2,0,1:T(8,128)(2,1)} copy(bf16[256,16,256]{2,1,0:T(8,128)(2,1)} %all-gather.5.cloned.1.call-done) | data formatting | bytes 4194304 | tf_op jit(solution)/shard_map/all_gather | solution.py:44
  150.6 0.0 all-to-all-done
  150.6 0.0 copy-start.2
  150.6 1.9 copy.42
  152.5 0.0 copy-start.1
  152.5 0.9 copy-done.2
  153.4 0.0 copy-start.4
  153.4 2.8 fusion.8
  156.2 0.0 copy-done.1
  156.2 0.0 copy-done.4
  156.2 0.0 copy-start.3
  156.3 0.7 convert_bitcast_fusion.2
  157.0 0.1 copy.48
  157.2 0.4 copy-done.3
  157.6 3.0 copy.49
  160.6 11.6 %all-to-all-start.1 = ((bf16[1024,4,256]{2,1,0:T(4,128)(2,1)}), bf16[1024,4,256]{2,1,0:T(4,128)(2,1)}, u32[]{:S(2)}, u32[]{:S(2)}) async-start(bf16[1024,4,256]{2,1,0:T(4,128)(2,1)} %copy.49), calls=%async_computation.1 | async-start | bytes 4194304 | tf_op jit(solution)/shard_map/all_to_all | solution.py:71
  172.2 0.0 reduce-scatter.5.cloned.1.call-start
  172.2 4.3 %convolution_convert_fusion = bf16[4,4,256,256]{3,2,1,0:T(8,128)(2,1)} fusion(bf16[4,4,256,256]{2,3,1,0:T(8,128)(2,1)} %copy-done.3, bf16[4,256,4,256]{3,1,0,2:T(8,128)(2,1)} %bitcast.36), kind=kOutput, calls=%fused_computation.20 | convolution fusion | flops 537919488 | bytes 6291456 | tf_op jit(solution)/shard_map/gcir,igjr->cigj/dot_general | solution.py:59
  176.5 4.5 %copy.54 = bf16[256,16,256]{2,1,0:T(8,128)(2,1)} copy(bf16[256,16,256]{0,2,1:T(8,128)(2,1)} %bitcast.39) | data formatting | bytes 4194304 | tf_op jit(solution)/shard_map/convert_element_type | solution.py:63
  181.1 0.0 reduce-scatter.5.cloned.1.call-update
  181.1 0.2 reduce-scatter.3.cloned.1.call-start
  181.3 41.3 %all-to-all-done.1 = bf16[1024,4,256]{2,1,0:T(4,128)(2,1)} async-done(((bf16[1024,4,256]{2,1,0:T(4,128)(2,1)}), bf16[1024,4,256]{2,1,0:T(4,128)(2,1)}, u32[]{:S(2)}, u32[]{:S(2)}) %all-to-all-start.1) | async-done | bytes 2097184 | tf_op jit(solution)/shard_map/all_to_all | solution.py:71
  222.7 1.9 copy.50
  224.6 0.6 convert_bitcast_fusion
  225.1 4.7 %copy.51 = f32[16,64,4,256]{3,2,1,0:T(4,128)} copy(f32[16,64,4,256]{3,0,1,2:T(8,128)S(1)} %convert_bitcast_fusion) | data formatting | bytes 8388608 | tf_op jit(solution)/shard_map/convert_element_type | solution.py:72
  229.8 5.4 %reshape.32 = f32[16,256,256]{2,1,0:T(8,128)} reshape(f32[16,64,4,256]{3,2,1,0:T(4,128)} %copy.51) | data formatting | bytes 8388608 | tf_op jit(solution)/shard_map/convert_element_type | solution.py:72
  235.2 7.8 %convert_bitcast_fusion.1 = bf16[256,16,256]{0,2,1:T(8,128)(2,1)} fusion(bf16[16,256,256]{2,1,0:T(8,128)(2,1)S(1)} %bitcast.34, f32[16,256,256]{2,1,0:T(8,128)} %reshape.32, f32[16,256,256]{2,1,0:T(8,128)} %get-tuple-element.7), kind=kOutput, calls=%fused_computation.17 | convolution fusion | flops 557842432 | bytes 12582912 | tf_op jit(solution)/shard_map/bkr,bir->kbi/dot_general | solution.py:74
  243.0 4.6 %copy.52 = bf16[256,16,256]{2,1,0:T(8,128)(2,1)} copy(bf16[256,16,256]{0,2,1:T(8,128)(2,1)} %convert_bitcast_fusion.1) | data formatting | bytes 4194304 | tf_op jit(solution)/shard_map/convert_element_type | solution.py:74
  247.5 0.0 reduce-scatter.3.cloned.1.call-update
  247.5 0.0 reduce-scatter.5.cloned.1.call-done
  247.6 52.5 %reduce-scatter.3.cloned.1.call-done = bf16[32,16,256]{2,1,0:T(8,128)(2,1)} async-done(((bf16[256,16,256]{2,1,0:T(8,128)(2,1)}), bf16[32,16,256]{2,1,0:T(8,128)(2,1)}) %reduce-scatter.3.cloned.1.call-update) | async-done | bytes 262160 | tf_op jit(solution)/shard_map/reduce_scatter | solution.py:73
Async XLA Ops:
  7.2 49.4 %copy-start = (bf16[4096,256]{1,0:T(8,128)(2,1)S(1)}, bf16[4096,256]{1,0:T(8,128)(2,1)}, u32[]{:S(2)}) copy-start(bf16[4096,256]{1,0:T(8,128)(2,1)} %param.4) | copy-start | bytes 6291460
  7.2 49.4 %all-gather.3.cloned.1.call-start = ((), (), s32[]{:S(2)}) async-start(), calls=%async_computation.4 | async-start | bytes 2359296 | tf_op jit(solution)/shard_map/all_gather | solution.py:38
  64.3 86.3 %all-to-all-start = ((bf16[16,256,256]{2,0,1:T(8,128)(2,1)}), bf16[16,256,256]{2,0,1:T(8,128)(2,1)}, u32[]{:S(2)}, u32[]{:S(2)}) async-start(bf16[16,256,256]{2,0,1:T(8,128)(2,1)} %copy.41), calls=%async_computation | async-start | bytes 4194304 | tf_op jit(solution)/shard_map/all_to_all | solution.py:41
  78.0 69.0 %all-gather.5.cloned.1.call-start = ((), (), s32[]{:S(2)}) async-start(), calls=%async_computation.5 | async-start | bytes 2359296 | tf_op jit(solution)/shard_map/all_gather | solution.py:44
  150.6 2.8 copy-start.2
  152.5 3.7 %copy-start.1 = (bf16[64,16,4,256]{3,1,0,2:T(8,128)(2,1)}, bf16[64,16,4,256]{3,1,0,2:T(8,128)(2,1)S(1)}, u32[]{:S(2)}) copy-start(bf16[64,16,4,256]{3,1,0,2:T(8,128)(2,1)S(1)} %copy.42) | copy-start | bytes 6291460
  153.4 2.8 copy-start.4
  156.2 1.3 copy-start.3
  160.6 62.1 %all-to-all-start.1 = ((bf16[1024,4,256]{2,1,0:T(4,128)(2,1)}), bf16[1024,4,256]{2,1,0:T(4,128)(2,1)}, u32[]{:S(2)}, u32[]{:S(2)}) async-start(bf16[1024,4,256]{2,1,0:T(4,128)(2,1)} %copy.49), calls=%async_computation.1 | async-start | bytes 4194304 | tf_op jit(solution)/shard_map/all_to_all | solution.py:71
  172.2 75.4 %reduce-scatter.5.cloned.1.call-start = ((), (), s32[]{:S(2)}) async-start(), calls=%async_computation.7 | async-start | bytes 2359296 | tf_op jit(solution)/shard_map/reduce_scatter | solution.py:62
  181.1 119.0 %reduce-scatter.3.cloned.1.call-start = ((), (), s32[]{:S(2)}) async-start(), calls=%async_computation.6 | async-start | bytes 2359296 | tf_op jit(solution)/shard_map/reduce_scatter | solution.py:73
Sparse Core Ops, SparseCore 0:
  10.7 45.8 all-gather.2
  80.9 66.0 all-gather.4
  181.2 58.4 reduce-scatter.4
  247.7 52.3 reduce-scatter.2
where the time goes:
time: 309 us; the launch traced here: 307 us
  waiting for transfers between devices  206 us (67%)
  local copies, waits for them, and re-layouts  40 us (13%)
  starting transfers between devices  25.7 us (8%)
  matrix products  20.8 us (7%)
  between operations  13.9 us (4%)
    all_gather x1, waiting for transfers between devices, shards(): piece_rows = lax.all_gather(second_factor, 'dp', axis=0, tiled=True)  63.7 us
    reduce_scatter x1, waiting for transfers between devices, shards(): lax.psum_scatter(jnp.einsum('bkr,bir->kbi', inputs, pre_grad, preferred_e...  52.5 us
    all_gather x1, waiting for transfers between devices, shards(): first_full = lax.all_gather(first_factor, 'dp', axis=0, tiled=True)  47.4 us
    all_to_all x1, waiting for transfers between devices, shards(): lax.all_to_all(sending, 'blk', split_axis=0, concat_axis=1, tiled=True)  41.3 us
    all_to_all x1, starting transfers between devices, shards(): lax.all_to_all(activated, 'blk', split_axis=1, concat_axis=0, tiled=True)  13.7 us
    all_to_all x1, starting transfers between devices, shards(): lax.all_to_all(sending, 'blk', split_axis=0, concat_axis=1, tiled=True)  11.6 us
    convert_element_type x2, local copies, waits for them, and re-layouts, shards(): activated_grad.astype(jnp.float32) * gelu_slope(pre_act)  10 us
    dot_general x1, matrix products, shards(): jnp.einsum('bkr,bir->kbi', inputs, pre_grad, preferred_element_type=jnp.f...  7.77 us
  transfers between devices with their start and end apart: 6, of which 4 were waited for; matrix products, arithmetic and copies ran while one was open for 14% of the time, Pallas kernels for 0%

commit v1 on v0

v1 whole, which is shorter than its diff:
```python
import math

import jax
import jax.numpy as jnp
from jax import lax
from jax.experimental.layout import Layout, with_layout_constraint
from jax.sharding import Mesh
from jax.sharding import PartitionSpec as P

NB = 1024
BS = 256


tanh_scale = 0.7978845608028654
cubic_coef = 0.044715


def gelu_value(values):
    inner = jnp.tanh(tanh_scale * (values + cubic_coef * values * values * values))
    return 0.5 * values * (1.0 + inner)


def gelu_slope(values):
    inner = jnp.tanh(tanh_scale * (values + cubic_coef * values * values * values))
    return 0.5 * (1.0 + inner) + 0.5 * values * (1.0 - inner * inner) * tanh_scale * (
        1.0 + 3.0 * cubic_coef * values * values
    )


def gather_rows(piece):
    n_core = lax.axis_size("core")
    n_ylo = lax.axis_size("ylo")
    along = lax.all_gather(piece, "ylo", axis=0, tiled=True)
    both = lax.all_gather(along, "core", axis=0, tiled=False)
    rows = piece.shape[0]
    both = both.reshape((n_core, n_ylo, rows) + piece.shape[1:])
    both = jnp.swapaxes(both, 0, 1)
    return both.reshape((n_ylo * n_core * rows,) + piece.shape[1:])


def scatter_rows(term):
    n_core = lax.axis_size("core")
    me = lax.axis_index("core")
    other = lax.rem(me + 1, n_core)
    sent = lax.dynamic_index_in_dim(term, other, 0, keepdims=False)
    kept = lax.dynamic_index_in_dim(term, me, 0, keepdims=False)
    got = lax.ppermute(sent, "core", [(c, (c + 1) % n_core) for c in range(n_core)])
    half = (kept.astype(jnp.float32) + got.astype(jnp.float32)).astype(jnp.bfloat16)
    half = with_layout_constraint(half, Layout(tuple(range(half.ndim))))
    part = lax.psum_scatter(half, "ylo", scatter_dimension=0, tiled=True)
    return part.reshape(part.shape[1:])


def shards(input_field, target_field, first_factor, second_factor):
    block_count = first_factor.shape[1]
    block_size = first_factor.shape[2]
    row_count = input_field.shape[1]
    replica_count = lax.axis_size("ylo") * lax.axis_size("core")
    group_count = NB // BS
    inner_count = block_count // group_count
    scale_factor = 1.0 / math.sqrt(row_count * replica_count)
    inputs = input_field.reshape(block_count, block_size, row_count)
    first_full = gather_rows(first_factor)
    second_full = gather_rows(second_factor)
    pre_act = jnp.einsum("bkr,kbi->bir", inputs, first_full, preferred_element_type=jnp.float32)
    activated = gelu_value(pre_act).astype(jnp.bfloat16)
    received = lax.all_to_all(activated, "blk", split_axis=1, concat_axis=0, tiled=True)
    permuted = received.reshape(group_count, block_size, inner_count, row_count)
    targets = target_field.reshape(inner_count, group_count, block_size, row_count)
    count = second_full.shape[0]
    split_part = second_full.reshape(count, inner_count, group_count, block_size)
    predicted = jnp.einsum(
        "gcir,cigj->igjr", permuted, split_part, preferred_element_type=jnp.float32
    )
    residual = ((predicted - targets.astype(jnp.float32)) * scale_factor).astype(jnp.bfloat16)
    permuted_grad = jnp.einsum(
        "cigj,igjr->gcir", split_part, residual, preferred_element_type=jnp.float32
    ).astype(jnp.bfloat16)
    n_core = lax.axis_size("core")
    n_ylo = lax.axis_size("ylo")
    kk = block_size // (n_core * n_ylo)
    permuted_cm = permuted.reshape(group_count, n_ylo, n_core, kk, inner_count, row_count)
    term = jnp.einsum(
        "gyxcir,igjr->xycigj", permuted_cm, residual, preferred_element_type=jnp.float32
    )
    second_out = scatter_rows(
        term.reshape(n_core, n_ylo, kk, block_count, block_size).astype(jnp.bfloat16)
    )
    sending = permuted_grad.reshape(group_count * block_size, inner_count, row_count)
    activated_grad = lax.all_to_all(sending, "blk", split_axis=0, concat_axis=1, tiled=True)
    pre_grad = (activated_grad.astype(jnp.float32) * gelu_slope(pre_act)).astype(jnp.bfloat16)
    inputs_cm = inputs.reshape(block_count, n_ylo, n_core, kk, row_count)
    first_sum = scatter_rows(
        jnp.einsum(
            "byxkr,bir->xykbi", inputs_cm, pre_grad, preferred_element_type=jnp.float32
        ).astype(jnp.bfloat16)
    )
    return (first_sum, second_out)


def solution(mesh):
    n_blk, n_dp = mesh.devices.shape
    n_core = 2
    split_mesh = Mesh(
        mesh.devices.reshape(n_blk, n_dp // n_core, n_core), ("blk", "ylo", "core")
    )
    dp = ("ylo", "core")
    return jax.shard_map(
        shards,
        mesh=split_mesh,
        in_specs=(P("blk", dp), P("blk", dp), P(dp, "blk", None), P(dp, "blk", None)),
        out_specs=(P(dp, "blk", None), P(dp, "blk", None)),
        check_vma=False,
    )
```

time: 309 us -> 345 us (1.12)
  waiting for transfers between devices: 206 us -> 238 us
  starting transfers between devices: 25.7 us -> 38.3 us
  local copies, waits for them, and re-layouts: 40 us -> 33.2 us
  matrix products: 20.8 us -> 17 us
    all_gather x2 -> x4, waiting for transfers between devices: 111 us -> 147 us  [the longest x2 97.9 us: gather_rows(): along = lax.all_gather(piece, 'ylo', axis=0, tiled=True)]
    convert_element_type x2 -> x0, local copies, waits for them, and re-layouts: 9.11 us -> none  [the longest x1 4.56 us: shards(): jnp.einsum('bkr,bir->kbi', inputs, pre_grad, preferred_element_type=jnp.f...]
    ppermute x0 -> x2, starting transfers between devices: none -> 8.48 us  [scatter_rows(): lax.ppermute(sent, 'core', [(c, (c + 1) % n_core) for c in range(n_core)])]
    reduce_scatter x2, waiting for transfers between devices: 52.6 us -> 45.4 us  [scatter_rows(): part = lax.psum_scatter(half, 'ylo', scatter_dimension=0, tiled=True)]
    ppermute x0 -> x2, waiting for transfers between devices: none -> 4.53 us  [scatter_rows(): lax.ppermute(sent, 'core', [(c, (c + 1) % n_core) for c in range(n_core)])]
    all_gather x1 -> x0, local copies, waits for them, and re-layouts: 3.63 us -> none  [shards(): piece_rows = lax.all_gather(second_factor, 'dp', axis=0, tiled=True)]
    reshape x0 -> x1, local copies, waits for them, and re-layouts: none -> 3.61 us  [gather_rows(): both = both.reshape((n_core, n_ylo, rows) + piece.shape[1:])]
  transfers between devices with their start and end apart: 6 -> 10, of which waited for: 4 -> 8; matrix products, arithmetic and copies ran while one was open for 14% -> 10% of each run, Pallas kernels for 0% -> 0%
where the time goes in v1:
time: 345 us; the launch traced here: 344 us
  waiting for transfers between devices  238 us (69%)
  starting transfers between devices  38.3 us (11%)
  local copies, waits for them, and re-layouts  33.2 us (10%)
  matrix products  17 us (5%)
  between operations  14.3 us (4%)
  other arithmetic  3.7 us (1%)
    all_gather x2, waiting for transfers between devices, gather_rows(): along = lax.all_gather(piece, 'ylo', axis=0, tiled=True)  97.9 us
    all_gather x2, waiting for transfers between devices, gather_rows(): both = lax.all_gather(along, 'core', axis=0, tiled=False)  48.9 us
    reduce_scatter x2, waiting for transfers between devices, scatter_rows(): part = lax.psum_scatter(half, 'ylo', scatter_dimension=0, tiled=True)  45.4 us
    all_to_all x1, waiting for transfers between devices, shards(): lax.all_to_all(sending, 'blk', split_axis=0, concat_axis=1, tiled=True)  39.7 us
    all_to_all x1, starting transfers between devices, shards(): lax.all_to_all(activated, 'blk', split_axis=1, concat_axis=0, tiled=True)  14.7 us
    all_to_all x1, starting transfers between devices, shards(): lax.all_to_all(sending, 'blk', split_axis=0, concat_axis=1, tiled=True)  14.7 us
    convert_element_type x2, local copies, waits for them, and re-layouts, shards(): activated_grad.astype(jnp.float32) * gelu_slope(pre_act)  10.1 us
    ppermute x2, starting transfers between devices, scatter_rows(): lax.ppermute(sent, 'core', [(c, (c + 1) % n_core) for c in range(n_core)])  8.48 us
  transfers between devices with their start and end apart: 10, of which 8 were waited for; matrix products, arithmetic and copies ran while one was open for 10% of the time, Pallas kernels for 0%

profile of v1, /device:TPU:1, one launch (start us, length us, event | category | flops | bytes accessed | tf_op | source)
XLA Modules:
  0.0 344.4 jit_solution(17482573426429803015)
XLA Ops:
  7.2 0.0 copy-start
  7.2 0.0 all-gather.7.cloned.1.call-start
  7.2 0.7 all-gather.7.cloned.1.call-update
  7.9 0.0 all-gather.11.cloned.1.call-start
  8.0 43.6 %all-gather.7.cloned.1.call-done = bf16[128,16,256]{2,1,0:T(8,128)(2,1)} async-done(((bf16[32,16,256]{2,1,0:T(8,128)(2,1)}), bf16[128,16,256]{2,1,0:T(8,128)(2,1)}) %all-gather.7.cloned.1.call-update) | async-done | bytes 1048592 | tf_op jit(solution)/shard_map/all_gather | solution.py:33
  51.5 0.0 all-gather.11.cloned.1.call-update
  51.5 21.6 %all-gather.11.cloned.1.call-done = bf16[256,16,256]{2,1,0:T(8,128)(2,1)} async-done(((bf16[128,16,256]{2,1,0:T(8,128)(2,1)}), bf16[256,16,256]{2,1,0:T(8,128)(2,1)}) %all-gather.11.cloned.1.call-update) | async-done | bytes 2097168 | tf_op jit(solution)/shard_map/all_gather | solution.py:34
  73.1 1.8 copy.54
  74.9 0.0 copy-done
  74.9 4.1 %multiply_convert_fusion = (bf16[16,256,256]{2,1,0:T(8,128)(2,1)S(1)}, f32[16,256,256]{2,1,0:T(8,128)}) fusion(bf16[16,256,256]{2,1,0:T(8,128)(2,1)S(1)} %bitcast.70, bf16[256,16,256]{2,1,0:T(8,128)(2,1)S(1)} %bitcast.82), kind=kOutput, calls=%fused_computation.14 | convolution fusion | flops 546308096 | bytes 10485760 | tf_op jit(solution)/shard_map/bkr,kbi->bir/dot_general | solution.py:65
  79.0 2.5 copy.56
  81.5 14.7 %all-to-all-start = ((bf16[16,256,256]{2,0,1:T(8,128)(2,1)}), bf16[16,256,256]{2,0,1:T(8,128)(2,1)}, u32[]{:S(2)}, u32[]{:S(2)}) async-start(bf16[16,256,256]{2,0,1:T(8,128)(2,1)} %copy.56), calls=%async_computation | async-start | bytes 4194304 | tf_op jit(solution)/shard_map/all_to_all | solution.py:67
  96.2 0.0 all-gather.9.cloned.1.call-start
  96.3 0.7 all-gather.9.cloned.1.call-update
  97.0 0.0 all-gather.13.cloned.1.call-start
  97.0 54.4 %all-gather.9.cloned.1.call-done = bf16[128,16,256]{2,1,0:T(8,128)(2,1)} async-done(((bf16[32,16,256]{2,1,0:T(8,128)(2,1)}), bf16[128,16,256]{2,1,0:T(8,128)(2,1)}) %all-gather.9.cloned.1.call-update) | async-done | bytes 1048592 | tf_op jit(solution)/shard_map/all_gather | solution.py:33
  151.4 0.0 all-gather.13.cloned.1.call-update
  151.4 4.6 %copy.60 = f32[4,4,256,256]{2,3,1,0:T(8,128)} copy(bf16[4,4,256,256]{3,2,1,0:T(8,128)(2,1)} %bitcast.78) | data formatting | bytes 6291456 | tf_op jit(solution)/shard_map/convert_element_type | solution.py:75
  156.0 27.4 %all-gather.13.cloned.1.call-done = bf16[256,16,256]{2,1,0:T(8,128)(2,1)} async-done(((bf16[128,16,256]{2,1,0:T(8,128)(2,1)}), bf16[256,16,256]{2,1,0:T(8,128)(2,1)}) %all-gather.13.cloned.1.call-update) | async-done | bytes 2097168 | tf_op jit(solution)/shard_map/all_gather | solution.py:34
  183.4 3.6 %copy.58 = bf16[2,4,32,16,256]{4,2,0,1,3:T(8,128)(2,1)} copy(bf16[2,4,32,16,256]{4,3,2,1,0:T(8,128)(2,1)} %bitcast.80) | data formatting | bytes 4194304 | tf_op jit(solution)/shard_map/reshape | solution.py:36
  187.0 0.0 all-to-all-done
  187.0 0.0 copy-start.1
  187.0 1.9 copy.57
  188.9 0.0 copy-start.2
  188.9 0.9 copy-done.1
  189.8 0.0 copy-start.3
  189.8 2.8 fusion.8
  192.6 0.0 copy-done.2
  192.6 0.0 copy-done.3
  192.6 0.0 copy-start.4
  192.6 0.7 convert_bitcast_fusion.1
  193.4 0.6 copy-done.4
  194.0 0.1 copy.63
  194.1 3.0 copy.64
  197.1 14.7 %all-to-all-start.1 = ((bf16[1024,4,256]{2,1,0:T(4,128)(2,1)}), bf16[1024,4,256]{2,1,0:T(4,128)(2,1)}, u32[]{:S(2)}, u32[]{:S(2)}) async-start(bf16[1024,4,256]{2,1,0:T(4,128)(2,1)} %copy.64), calls=%async_computation.1 | async-start | bytes 4194304 | tf_op jit(solution)/shard_map/all_to_all | solution.py:90
  211.8 0.2 reduce-scatter.5.cloned.1.call-start
  212.0 2.9 fusion.25
  215.0 0.2 constant_dynamic-slice_fusion.1
  215.2 0.6 copy.99
  215.8 2.4 collective-permute-start.1
  218.2 2.3 collective-permute-done.1
  220.5 1.8 fusion.11
  222.3 0.0 reduce-scatter.5.cloned.1.call-update
  222.3 0.0 reduce-scatter.3.cloned.1.call-start
  222.4 39.7 %all-to-all-done.1 = bf16[1024,4,256]{2,1,0:T(4,128)(2,1)} async-done(((bf16[1024,4,256]{2,1,0:T(4,128)(2,1)}), bf16[1024,4,256]{2,1,0:T(4,128)(2,1)}, u32[]{:S(2)}, u32[]{:S(2)}) %all-to-all-start.1) | async-done | bytes 2097184 | tf_op jit(solution)/shard_map/all_to_all | solution.py:90
  262.1 1.9 copy.65
  264.0 0.6 convert_bitcast_fusion
  264.6 4.7 %copy.66 = f32[16,64,4,256]{3,2,1,0:T(4,128)} copy(f32[16,64,4,256]{3,0,1,2:T(8,128)S(1)} %convert_bitcast_fusion) | data formatting | bytes 8388608 | tf_op jit(solution)/shard_map/convert_element_type | solution.py:91
  269.2 5.4 %reshape.52 = f32[16,256,256]{2,1,0:T(8,128)} reshape(f32[16,64,4,256]{3,2,1,0:T(4,128)} %copy.66) | data formatting | bytes 8388608 | tf_op jit(solution)/shard_map/convert_element_type | solution.py:91
  274.6 6.4 %fusion.13 = bf16[16,256,4,2,32]{1,4,3,2,0:T(8,128)(2,1)S(1)} fusion(bf16[16,4,2,32,256]{4,3,2,1,0:T(8,128)(2,1)S(1)} %bitcast.71, f32[16,256,256]{2,1,0:T(8,128)} %reshape.52, f32[16,256,256]{2,1,0:T(8,128)} %get-tuple-element.5), kind=kOutput, calls=%fused_computation.21 | convolution fusion | flops 556793856 | bytes 12582912 | tf_op jit(solution)/shard_map/byxkr,bir->xykbi/dot_general | solution.py:94
  281.1 1.3 copy.96
  282.4 0.1 dynamic-slice_bitcast_fusion
  282.4 6.1 %collective-permute-start = (bf16[4,32,16,256]{3,2,1,0:T(8,128)(2,1)S(1)}, bf16[4,32,16,256]{3,2,1,0:T(8,128)(2,1)S(1)}, u32[]{:S(2)}, u32[]{:S(2)}) collective-permute-start(bf16[4,32,16,256]{3,2,1,0:T(8,128)(2,1)S(1)} %dynamic-slice_bitcast_fusion), channel_id=1, source_target_pairs={{0,1},{1,0},{2,3},{3,2},{4,5},{5,4},{6,7},{7,6},{8,9},{9,8},{10,11... | collective-permute-start | bytes 3145736 | tf_op jit(solution)/shard_map/ppermute | solution.py:47
  288.5 2.3 collective-permute-done
  290.8 1.3 fusion.12
  292.1 0.0 reduce-scatter.3.cloned.1.call-update
  292.1 0.0 reduce-scatter.5.cloned.1.call-done
  292.2 45.4 %reduce-scatter.3.cloned.1.call-done = bf16[1,32,16,256]{3,2,1,0:T(8,128)(2,1)} async-done(((bf16[4,32,16,256]{3,2,1,0:T(8,128)(2,1)}), bf16[1,32,16,256]{3,2,1,0:T(8,128)(2,1)}) %reduce-scatter.3.cloned.1.call-update) | async-done | bytes 262160 | tf_op jit(solution)/shard_map/reduce_scatter | solution.py:50
Async XLA Ops:
  7.2 67.8 %copy-start = (bf16[4096,256]{1,0:T(8,128)(2,1)S(1)}, bf16[4096,256]{1,0:T(8,128)(2,1)}, u32[]{:S(2)}) copy-start(bf16[4096,256]{1,0:T(8,128)(2,1)} %param.4) | copy-start | bytes 6291460
  7.2 44.4 %all-gather.7.cloned.1.call-start = ((), (), s32[]{:S(2)}) async-start(), calls=%async_computation.4 | async-start | bytes 1310720 | tf_op jit(solution)/shard_map/all_gather | solution.py:33
  7.9 65.2 %all-gather.11.cloned.1.call-start = ((), (), s32[]{:S(2)}) async-start(), calls=%async_computation.8 | async-start | bytes 3145728 | tf_op jit(solution)/shard_map/all_gather | solution.py:34
  81.5 105.4 %all-to-all-start = ((bf16[16,256,256]{2,0,1:T(8,128)(2,1)}), bf16[16,256,256]{2,0,1:T(8,128)(2,1)}, u32[]{:S(2)}, u32[]{:S(2)}) async-start(bf16[16,256,256]{2,0,1:T(8,128)(2,1)} %copy.56), calls=%async_computation | async-start | bytes 4194304 | tf_op jit(solution)/shard_map/all_to_all | solution.py:67
  96.2 55.1 %all-gather.9.cloned.1.call-start = ((), (), s32[]{:S(2)}) async-start(), calls=%async_computation.5 | async-start | bytes 1310720 | tf_op jit(solution)/shard_map/all_gather | solution.py:33
  97.0 86.4 %all-gather.13.cloned.1.call-start = ((), (), s32[]{:S(2)}) async-start(), calls=%async_computation.9 | async-start | bytes 3145728 | tf_op jit(solution)/shard_map/all_gather | solution.py:34
  187.0 2.8 copy-start.1
  188.9 3.7 %copy-start.2 = (bf16[64,16,4,256]{3,1,0,2:T(8,128)(2,1)}, bf16[64,16,4,256]{3,1,0,2:T(8,128)(2,1)S(1)}, u32[]{:S(2)}) copy-start(bf16[64,16,4,256]{3,1,0,2:T(8,128)(2,1)S(1)} %copy.57) | copy-start | bytes 6291460
  189.8 2.8 copy-start.3
  192.6 1.3 copy-start.4
  197.1 65.0 %all-to-all-start.1 = ((bf16[1024,4,256]{2,1,0:T(4,128)(2,1)}), bf16[1024,4,256]{2,1,0:T(4,128)(2,1)}, u32[]{:S(2)}, u32[]{:S(2)}) async-start(bf16[1024,4,256]{2,1,0:T(4,128)(2,1)} %copy.64), calls=%async_computation.1 | async-start | bytes 4194304 | tf_op jit(solution)/shard_map/all_to_all | solution.py:90
  211.8 80.4 %reduce-scatter.5.cloned.1.call-start = ((), (), s32[]{:S(2)}) async-start(), calls=%async_computation.7 | async-start | bytes 1310720 | tf_op jit(solution)/shard_map/reduce_scatter | solution.py:50
  215.8 4.7 %collective-permute-start.1 = (bf16[4,32,16,256]{3,2,1,0:T(8,128)(2,1)S(1)}, bf16[4,32,16,256]{3,2,1,0:T(8,128)(2,1)S(1)}, u32[]{:S(2)}, u32[]{:S(2)}) collective-permute-start(bf16[4,32,16,256]{3,2,1,0:T(8,128)(2,1)S(1)} %bitcast.83), channel_id=1, source_target_pairs={{0,1},{1,0},{2,3},{3,2},{4,5},{5,4},{6,7},{7,6},{8,9},{9,8},{10,11... | collective-permute-start | bytes 3145736 | tf_op jit(solution)/shard_map/ppermute | solution.py:47
  222.3 115.2 %reduce-scatter.3.cloned.1.call-start = ((), (), s32[]{:S(2)}) async-start(), calls=%async_computation.6 | async-start | bytes 1310720 | tf_op jit(solution)/shard_map/reduce_scatter | solution.py:50
  282.4 8.3 %collective-permute-start = (bf16[4,32,16,256]{3,2,1,0:T(8,128)(2,1)S(1)}, bf16[4,32,16,256]{3,2,1,0:T(8,128)(2,1)S(1)}, u32[]{:S(2)}, u32[]{:S(2)}) collective-permute-start(bf16[4,32,16,256]{3,2,1,0:T(8,128)(2,1)S(1)} %dynamic-slice_bitcast_fusion), channel_id=1, source_target_pairs={{0,1},{1,0},{2,3},{3,2},{4,5},{5,4},{6,7},{7,6},{8,9},{9,8},{10,11... | collective-permute-start | bytes 3145736 | tf_op jit(solution)/shard_map/ppermute | solution.py:47
Sparse Core Ops, SparseCore 0:
  10.1 41.3 all-gather.6
  53.6 19.4 all-gather.10
  99.2 52.1 all-gather.8
  153.3 29.9 all-gather.12
  222.4 50.1 reduce-scatter.4
  292.3 45.2 reduce-scatter.2

commit v2 on v1

--- a/solution.py
+++ b/solution.py
@@ -3,7 +3,6 @@
 import jax
 import jax.numpy as jnp
 from jax import lax
-from jax.experimental.layout import Layout, with_layout_constraint
 from jax.sharding import Mesh
 from jax.sharding import PartitionSpec as P
 
@@ -27,28 +26,51 @@
     )
 
 
+def line_pairs(n, step):
+    return [(i, i + step) for i in range(n) if 0 <= i + step < n]
+
+
+def swap_pairs(n):
+    return [(c, (c + 1) % n) for c in range(n)]
+
+
 def gather_rows(piece):
     n_core = lax.axis_size("core")
     n_ylo = lax.axis_size("ylo")
-    along = lax.all_gather(piece, "ylo", axis=0, tiled=True)
-    both = lax.all_gather(along, "core", axis=0, tiled=False)
-    rows = piece.shape[0]
-    both = both.reshape((n_core, n_ylo, rows) + piece.shape[1:])
-    both = jnp.swapaxes(both, 0, 1)
-    return both.reshape((n_ylo * n_core * rows,) + piece.shape[1:])
+    y = lax.axis_index("ylo")
+    c = lax.axis_index("core")
+    right = [piece]
+    left = [piece]
+    for _ in range(n_ylo - 1):
+        right.append(lax.ppermute(right[-1], "ylo", line_pairs(n_ylo, 1)))
+        left.append(lax.ppermute(left[-1], "ylo", line_pairs(n_ylo, -1)))
+    stacked = jnp.stack(right[:0:-1] + left)
+    line = lax.dynamic_slice_in_dim(stacked, n_ylo - 1 - y, n_ylo, axis=0)
+    other = lax.ppermute(line, "core", swap_pairs(n_core))
+    pair = jnp.where(c == 0, jnp.stack([line, other], 1), jnp.stack([other, line], 1))
+    return pair.reshape((n_ylo * n_core * piece.shape[0],) + piece.shape[1:])
 
 
 def scatter_rows(term):
     n_core = lax.axis_size("core")
-    me = lax.axis_index("core")
-    other = lax.rem(me + 1, n_core)
-    sent = lax.dynamic_index_in_dim(term, other, 0, keepdims=False)
-    kept = lax.dynamic_index_in_dim(term, me, 0, keepdims=False)
-    got = lax.ppermute(sent, "core", [(c, (c + 1) % n_core) for c in range(n_core)])
-    half = (kept.astype(jnp.float32) + got.astype(jnp.float32)).astype(jnp.bfloat16)
-    half = with_layout_constraint(half, Layout(tuple(range(half.ndim))))
-    part = lax.psum_scatter(half, "ylo", scatter_dimension=0, tiled=True)
-    return part.reshape(part.shape[1:])
+    n_ylo = lax.axis_size("ylo")
+    y = lax.axis_index("ylo")
+    c = lax.axis_index("core")
+    sent = lax.dynamic_index_in_dim(term, lax.rem(c + 1, n_core), 0, keepdims=False)
+    kept = lax.dynamic_index_in_dim(term, c, 0, keepdims=False)
+    got = lax.ppermute(sent, "core", swap_pairs(n_core))
+    chip = kept.astype(jnp.float32) + got.astype(jnp.float32)
+    total = lax.dynamic_index_in_dim(chip, y, 0, keepdims=False)
+    for step in (1, -1):
+        carry = None
+        for s in range(1, n_ylo):
+            dest = jnp.clip(y + step * (n_ylo - s), 0, n_ylo - 1)
+            block = lax.dynamic_index_in_dim(chip, dest, 0, keepdims=False)
+            if carry is not None:
+                block = block + carry.astype(jnp.float32)
+            carry = lax.ppermute(block.astype(jnp.bfloat16), "ylo", line_pairs(n_ylo, step))
+        total = total + carry.astype(jnp.float32)
+    return total.astype(jnp.bfloat16)
 
 
 def shards(input_field, target_field, first_factor, second_factor):

time: 345 us -> 309 us (0.90); the launches traced: 344 us -> 305 us
  waiting for transfers between devices: 238 us -> 115 us
  starting transfers between devices: 38.3 us -> 120 us
  other arithmetic: 3.7 us -> 18.7 us
  between operations: 14.3 us -> 1.35 us
    all_gather x4 -> x0, waiting for transfers between devices: 147 us -> none  [the longest x2 97.9 us: gather_rows(): along = lax.all_gather(piece, 'ylo', axis=0, tiled=True)]
    ppermute x2 -> x28, starting transfers between devices: 8.48 us -> 90.2 us  [the longest x12 37.5 us: scatter_rows(): lax.ppermute(block.astype(jnp.bfloat16), 'ylo', line_pairs(n_ylo, step))]
    ppermute x2 -> x28, waiting for transfers between devices: 4.53 us -> 74.5 us  [the longest x6 57.8 us: gather_rows(): right.append(lax.ppermute(right[-1], 'ylo', line_pairs(n_ylo, 1)))]
    reduce_scatter x2 -> x0, waiting for transfers between devices: 45.4 us -> none  [scatter_rows(): part = lax.psum_scatter(half, 'ylo', scatter_dimension=0, tiled=True)]
    convert_element_type x2 -> x8, other arithmetic: 3.11 us -> 12.7 us  [the longest x6 9.67 us: scatter_rows(): block.astype(jnp.bfloat16)]
    unnamed x11 -> x41, local copies, waits for them, and re-layouts: 2.1 us -> 8.91 us
    convert_element_type x1 -> x2, local copies, waits for them, and re-layouts: 4.61 us -> 0.15 us  [scatter_rows(): block.astype(jnp.bfloat16)]
    add x0 -> x2, other arithmetic: none -> 3.67 us  [scatter_rows(): chip = kept.astype(jnp.float32) + got.astype(jnp.float32)]
  transfers between devices with their start and end apart: 10 -> 30, of which waited for: 8 -> 13; matrix products, arithmetic and copies ran while one was open for 10% -> 15% of each run, Pallas kernels for 0% -> 0%
where the time goes in v2:
time: 309 us; the launch traced here: 305 us
  starting transfers between devices  120 us (39%)
  waiting for transfers between devices  115 us (37%)
  local copies, waits for them, and re-layouts  34.1 us (11%)
  other arithmetic  18.7 us (6%)
  matrix products  14.8 us (5%)
    ppermute x6, waiting for transfers between devices, gather_rows(): right.append(lax.ppermute(right[-1], 'ylo', line_pairs(n_ylo, 1)))  57.8 us
    all_to_all x1, waiting for transfers between devices, shards(): lax.all_to_all(sending, 'blk', split_axis=0, concat_axis=1, tiled=True)  40.8 us
    ppermute x12, starting transfers between devices, scatter_rows(): lax.ppermute(block.astype(jnp.bfloat16), 'ylo', line_pairs(n_ylo, step))  37.5 us
    ppermute x6, starting transfers between devices, gather_rows(): right.append(lax.ppermute(right[-1], 'ylo', line_pairs(n_ylo, 1)))  24.5 us
    all_to_all x1, starting transfers between devices, shards(): lax.all_to_all(activated, 'blk', split_axis=1, concat_axis=0, tiled=True)  17.6 us
    all_to_all x1, starting transfers between devices, shards(): lax.all_to_all(sending, 'blk', split_axis=0, concat_axis=1, tiled=True)  12.6 us
    ppermute x2, starting transfers between devices, gather_rows(): other = lax.ppermute(line, 'core', swap_pairs(n_core))  11.7 us
    convert_element_type x2, local copies, waits for them, and re-layouts, shards(): activated_grad.astype(jnp.float32) * gelu_slope(pre_act)  10.1 us
  transfers between devices with their start and end apart: 30, of which 13 were waited for; matrix products, arithmetic and copies ran while one was open for 15% of the time, Pallas kernels for 0%

profile of v2, /device:TPU:1, one launch (start us, length us, event | category | flops | bytes accessed | tf_op | source)
XLA Modules:
  0.0 304.6 jit_solution(15500277670619523874)
XLA Ops:
  1.8 4.0 %collective-permute-start.7 = (bf16[32,16,256]{2,0,1:T(8,128)(2,1)S(1)}, bf16[32,16,256]{2,0,1:T(8,128)(2,1)S(1)}, u32[]{:S(2)}, u32[]{:S(2)}) collective-permute-start(bf16[32,16,256]{2,0,1:T(8,128)(2,1)S(1)} %copy.50), channel_id=1, source_target_pairs={{0,2},{2,4},{4,6},{1,3},{3,5},{5,7},{8,10},{10,12},{12,14},{9,11},... | collective-permute-start | bytes 786440 | tf_op jit(solution)/shard_map/ppermute | solution.py:45
  5.9 1.3 collective-permute-start.10
  7.2 2.0 collective-permute-done.7
  9.2 4.9 %collective-permute-start.8 = (bf16[32,16,256]{2,0,1:T(8,128)(2,1)S(1)}, bf16[32,16,256]{2,0,1:T(8,128)(2,1)S(1)}, u32[]{:S(2)}, u32[]{:S(2)}) collective-permute-start(bf16[32,16,256]{2,0,1:T(8,128)(2,1)S(1)} %collective-permute-done.7), channel_id=1, source_target_pairs={{0,2},{2,4},{4,6},{1,3},{3,5},{5,7},{8,10},{10,12},{12,14},{9,11},... | collective-permute-start | bytes 786440 | tf_op jit(solution)/shard_map/ppermute | solution.py:45
  14.1 1.3 collective-permute-start.11
  15.4 2.0 collective-permute-done.8
  17.3 5.5 %collective-permute-start.9 = (bf16[32,16,256]{2,0,1:T(8,128)(2,1)S(1)}, bf16[32,16,256]{2,0,1:T(8,128)(2,1)}, u32[]{:S(2)}, u32[]{:S(2)}) collective-permute-start(bf16[32,16,256]{2,0,1:T(8,128)(2,1)S(1)} %collective-permute-done.8), channel_id=1, source_target_pairs={{0,2},{2,4},{4,6},{1,3},{3,5},{5,7},{8,10},{10,12},{12,14},{9,11},... | collective-permute-start | bytes 786440 | tf_op jit(solution)/shard_map/ppermute | solution.py:45
  22.9 1.3 collective-permute-start.12
  24.2 1.3 collective-permute-done.9
  26.7 3.4 %collective-permute-done.12 = bf16[32,16,256]{2,0,1:T(8,128)(2,1)S(1)} collective-permute-done((bf16[32,16,256]{2,0,1:T(8,128)(2,1)S(1)}, bf16[32,16,256]{2,0,1:T(8,128)(2,1)S(1)}, u32[]{:S(2)}, u32[]{:S(2)}) %collective-permute-start.12) | collective-permute-done | bytes 262176 | tf_op jit(solution)/shard_map/ppermute | solution.py:46
  30.1 1.3 copy-done.7
  32.4 7.3 %collective-permute-start.13 = (bf16[4,32,16,256]{3,1,0,2:T(8,128)(2,1)}, bf16[4,32,16,256]{3,1,0,2:T(8,128)(2,1)S(1)}, u32[]{:S(2)}, u32[]{:S(2)}) collective-permute-start(bf16[4,32,16,256]{3,1,0,2:T(8,128)(2,1)} %constant_dynamic-slice_fusion.2), channel_id=1, source_target_pairs={{0,1},{1,0},{2,3},{3,2},{4,5},{5,4},{6,7},{7,6},{8,9},{9,8},{10,11... | collective-permute-start | bytes 3145736 | tf_op jit(solution)/shard_map/ppermute | solution.py:49
  39.8 1.3 fusion.54
  42.5 3.6 %multiply_convert_fusion = (bf16[16,256,256]{2,1,0:T(8,128)(2,1)S(1)}, f32[16,256,256]{2,1,0:T(8,128)}) fusion(bf16[256,16,256]{2,0,1:T(8,128)(2,1)S(1)} %bitcast.175, bf16[16,256,256]{2,1,0:T(8,128)(2,1)S(1)} %bitcast.167), kind=kOutput, calls=%fused_computation.13 | convolution fusion | flops 546308096 | bytes 10485760 | tf_op jit(solution)/shard_map/bkr,kbi->bir/dot_general | solution.py:87
  46.1 2.5 copy.59
  48.6 17.6 %all-to-all-start = ((bf16[16,256,256]{2,0,1:T(8,128)(2,1)}), bf16[16,256,256]{2,0,1:T(8,128)(2,1)}, u32[]{:S(2)}, u32[]{:S(2)}) async-start(bf16[16,256,256]{2,0,1:T(8,128)(2,1)} %copy.59), calls=%async_computation | async-start | bytes 4194304 | tf_op jit(solution)/shard_map/all_to_all | solution.py:89
  66.2 1.6 collective-permute-start
  67.9 1.3 collective-permute-start.3
  69.2 47.1 %collective-permute-done = bf16[32,16,256]{2,0,1:T(8,128)(2,1)S(1)} collective-permute-done((bf16[32,16,256]{2,0,1:T(8,128)(2,1)S(1)}, bf16[32,16,256]{2,0,1:T(8,128)(2,1)S(1)}, u32[]{:S(2)}, u32[]{:S(2)}) %collective-permute-start) | collective-permute-done | bytes 262176 | tf_op jit(solution)/shard_map/ppermute | solution.py:45
  116.3 4.2 %collective-permute-start.1 = (bf16[32,16,256]{2,0,1:T(8,128)(2,1)S(1)}, bf16[32,16,256]{2,0,1:T(8,128)(2,1)S(1)}, u32[]{:S(2)}, u32[]{:S(2)}) collective-permute-start(bf16[32,16,256]{2,0,1:T(8,128)(2,1)S(1)} %collective-permute-done), channel_id=1, source_target_pairs={{0,2},{2,4},{4,6},{1,3},{3,5},{5,7},{8,10},{10,12},{12,14},{9,11},... | collective-permute-start | bytes 786440 | tf_op jit(solution)/shard_map/ppermute | solution.py:45
  120.5 1.3 collective-permute-start.4
  121.8 3.2 %collective-permute-done.1 = bf16[32,16,256]{2,0,1:T(8,128)(2,1)S(1)} collective-permute-done((bf16[32,16,256]{2,0,1:T(8,128)(2,1)S(1)}, bf16[32,16,256]{2,0,1:T(8,128)(2,1)S(1)}, u32[]{:S(2)}, u32[]{:S(2)}) %collective-permute-start.1) | collective-permute-done | bytes 262176 | tf_op jit(solution)/shard_map/ppermute | solution.py:45
  125.0 4.2 %collective-permute-start.2 = (bf16[32,16,256]{2,0,1:T(8,128)(2,1)S(1)}, bf16[32,16,256]{2,0,1:T(8,128)(2,1)S(1)}, u32[]{:S(2)}, u32[]{:S(2)}) collective-permute-start(bf16[32,16,256]{2,0,1:T(8,128)(2,1)S(1)} %collective-permute-done.1), channel_id=1, source_target_pairs={{0,2},{2,4},{4,6},{1,3},{3,5},{5,7},{8,10},{10,12},{12,14},{9,11},... | collective-permute-start | bytes 786440 | tf_op jit(solution)/shard_map/ppermute | solution.py:45
  129.2 1.3 collective-permute-start.5
  130.5 2.3 collective-permute-done.2
  133.0 5.1 %collective-permute-done.5 = bf16[32,16,256]{2,0,1:T(8,128)(2,1)S(1)} collective-permute-done((bf16[32,16,256]{2,0,1:T(8,128)(2,1)S(1)}, bf16[32,16,256]{2,0,1:T(8,128)(2,1)S(1)}, u32[]{:S(2)}, u32[]{:S(2)}) %collective-permute-start.5) | collective-permute-done | bytes 262176 | tf_op jit(solution)/shard_map/ppermute | solution.py:46
  138.2 4.3 %collective-permute-start.6 = (bf16[4,32,16,256]{3,1,0,2:T(8,128)(2,1)S(1)}, bf16[4,32,16,256]{3,1,0,2:T(8,128)(2,1)S(1)}, u32[]{:S(2)}, u32[]{:S(2)}) collective-permute-start(bf16[4,32,16,256]{3,1,0,2:T(8,128)(2,1)S(1)} %constant_dynamic-slice_fusion.3), channel_id=1, source_target_pairs={{0,1},{1,0},{2,3},{3,2},{4,5},{5,4},{6,7},{7,6},{8,9},{9,8},{10,11... | collective-permute-start | bytes 3145736 | tf_op jit(solution)/shard_map/ppermute | solution.py:49
  142.7 2.2 collective-permute-done.6
  144.9 1.5 maximum_select_fusion
  146.4 1.9 copy.60
  151.9 3.0 copy.65
  154.9 12.6 %all-to-all-start.1 = ((bf16[1024,4,256]{2,1,0:T(4,128)(2,1)}), bf16[1024,4,256]{2,1,0:T(4,128)(2,1)}, u32[]{:S(2)}, u32[]{:S(2)}) async-start(bf16[1024,4,256]{2,1,0:T(4,128)(2,1)} %copy.65), calls=%async_computation.1 | async-start | bytes 4194304 | tf_op jit(solution)/shard_map/all_to_all | solution.py:112
  167.6 3.0 fusion.24
  170.7 1.6 copy.95
  172.3 2.5 collective-permute-start.21
  174.9 40.8 %all-to-all-done.1 = bf16[1024,4,256]{2,1,0:T(4,128)(2,1)} async-done(((bf16[1024,4,256]{2,1,0:T(4,128)(2,1)}), bf16[1024,4,256]{2,1,0:T(4,128)(2,1)}, u32[]{:S(2)}, u32[]{:S(2)}) %all-to-all-start.1) | async-done | bytes 2097184 | tf_op jit(solution)/shard_map/all_to_all | solution.py:112
  215.7 1.9 copy.66
  218.1 4.8 %copy.67 = f32[16,64,4,256]{3,2,1,0:T(4,128)} copy(f32[16,64,4,256]{3,0,1,2:T(8,128)S(1)} %convert_bitcast_fusion) | data formatting | bytes 8388608 | tf_op jit(solution)/shard_map/convert_element_type | solution.py:113
  222.9 5.3 %reshape.45 = f32[16,256,256]{2,1,0:T(8,128)} reshape(f32[16,64,4,256]{3,2,1,0:T(4,128)} %copy.67) | data formatting | bytes 8388608 | tf_op jit(solution)/shard_map/convert_element_type | solution.py:113
  228.2 6.4 %fusion.21 = bf16[16,256,4,2,32]{1,4,3,2,0:T(8,128)(2,1)S(1)} fusion(bf16[16,4,2,32,256]{4,3,2,1,0:T(8,128)(2,1)S(1)} %bitcast.166, f32[16,256,256]{2,1,0:T(8,128)} %reshape.45, f32[16,256,256]{2,1,0:T(8,128)} %get-tuple-element.19), kind=kOutput, calls=%fused_computation.26 | convolution fusion | flops 557842432 | bytes 12582912 | tf_op jit(solution)/shard_map/byxkr,bir->xykbi/dot_general | solution.py:116
  234.7 1.3 copy-done.8
  237.1 6.2 %collective-permute-start.14 = (bf16[4,32,16,256]{3,1,0,2:T(8,128)(2,1)}, bf16[4,32,16,256]{3,1,0,2:T(8,128)(2,1)}, u32[]{:S(2)}, u32[]{:S(2)}) collective-permute-start(bf16[4,32,16,256]{3,1,0,2:T(8,128)(2,1)} %dynamic-slice_bitcast_fusion), channel_id=1, source_target_pairs={{0,1},{1,0},{2,3},{3,2},{4,5},{5,4},{6,7},{7,6},{8,9},{9,8},{10,11... | collective-permute-start | bytes 3145736 | tf_op jit(solution)/shard_map/ppermute | solution.py:61
  243.4 2.1 convert_add_fusion
  245.5 10.4 %collective-permute-start.22 = (bf16[32,16,256]{2,1,0:T(8,128)(2,1)S(1)}, bf16[32,16,256]{2,1,0:T(8,128)(2,1)}, u32[]{:S(2)}, u32[]{:S(2)}) collective-permute-start(bf16[32,16,256]{2,1,0:T(8,128)(2,1)S(1)} %get-tuple-element.10), channel_id=1, source_target_pairs={{0,2},{2,4},{4,6},{1,3},{3,5},{5,7},{8,10},{10,12},{12,14},{9,11},... | collective-permute-start | bytes 786440 | tf_op jit(solution)/shard_map/ppermute | solution.py:71
  255.9 1.6 bitcast_add_fusion
  257.6 1.2 copy-done.3
  258.9 2.0 collective-permute-start.15
  260.9 1.3 collective-permute-start.25
  262.2 1.2 fusion.29
  263.4 4.7 %collective-permute-start.23 = (bf16[32,16,256]{2,1,0:T(8,128)(2,1)S(1)}, bf16[32,16,256]{2,1,0:T(8,128)(2,1)}, u32[]{:S(2)}, u32[]{:S(2)}) collective-permute-start(bf16[32,16,256]{2,1,0:T(8,128)(2,1)S(1)} %fusion.29), channel_id=1, source_target_pairs={{0,2},{2,4},{4,6},{1,3},{3,5},{5,7},{8,10},{10,12},{12,14},{9,11},... | collective-permute-start | bytes 786440 | tf_op jit(solution)/shard_map/ppermute | solution.py:71
  268.1 1.3 collective-permute-start.18
  269.4 1.2 fusion.35
  270.6 4.0 %collective-permute-start.16 = (bf16[32,16,256]{2,0,1:T(8,128)(2,1)S(1)}, bf16[32,16,256]{2,0,1:T(8,128)(2,1)S(1)}, u32[]{:S(2)}, u32[]{:S(2)}) collective-permute-start(bf16[32,16,256]{2,0,1:T(8,128)(2,1)S(1)} %fusion.35), channel_id=1, source_target_pairs={{0,2},{2,4},{4,6},{1,3},{3,5},{5,7},{8,10},{10,12},{12,14},{9,11},... | collective-permute-start | bytes 786440 | tf_op jit(solution)/shard_map/ppermute | solution.py:71
  274.7 2.4 fusion.30
  277.0 1.3 collective-permute-start.26
  279.0 1.9 fusion.36
  280.9 1.3 collective-permute-start.19
  282.2 4.7 %collective-permute-start.24 = (bf16[32,16,256]{2,1,0:T(8,128)(2,1)}, bf16[32,16,256]{2,1,0:T(8,128)(2,1)S(1)}, u32[]{:S(2)}, u32[]{:S(2)}) collective-permute-start(bf16[32,16,256]{2,1,0:T(8,128)(2,1)} %get-tuple-element.8), channel_id=1, source_target_pairs={{0,2},{2,4},{4,6},{1,3},{3,5},{5,7},{8,10},{10,12},{12,14},{9,11},... | collective-permute-start | bytes 786440 | tf_op jit(solution)/shard_map/ppermute | solution.py:71
  288.1 1.3 collective-permute-start.27
  289.4 4.0 %collective-permute-start.17 = (bf16[32,16,256]{2,0,1:T(8,128)(2,1)}, bf16[32,16,256]{2,0,1:T(8,128)(2,1)S(1)}, u32[]{:S(2)}, u32[]{:S(2)}) collective-permute-start(bf16[32,16,256]{2,0,1:T(8,128)(2,1)} %get-tuple-element.14), channel_id=1, source_target_pairs={{0,2},{2,4},{4,6},{1,3},{3,5},{5,7},{8,10},{10,12},{12,14},{9,11},... | collective-permute-start | bytes 786440 | tf_op jit(solution)/shard_map/ppermute | solution.py:71
  293.4 1.8 fusion.34
  295.3 1.3 collective-permute-start.20
  296.6 1.9 fusion.32
  298.5 4.1 %collective-permute-done.20 = bf16[32,16,256]{2,0,1:T(8,128)(2,1)S(1)} collective-permute-done((bf16[32,16,256]{2,0,1:T(8,128)(2,1)}, bf16[32,16,256]{2,0,1:T(8,128)(2,1)S(1)}, u32[]{:S(2)}, u32[]{:S(2)}) %collective-permute-start.20) | collective-permute-done | bytes 262176 | tf_op jit(solution)/shard_map/ppermute | solution.py:71
  (73 shorter events, 14.7 us)
Async XLA Ops:
  0.6 41.8 %copy-start = (bf16[4096,256]{1,0:T(8,128)(2,1)S(1)}, bf16[4096,256]{1,0:T(8,128)(2,1)}, u32[]{:S(2)}) copy-start(bf16[4096,256]{1,0:T(8,128)(2,1)} %param.4) | copy-start | bytes 6291460
  0.6 25.9 %copy-start.11 = (bf16[32,16,256]{2,1,0:T(8,128)(2,1)S(1)}, bf16[32,16,256]{2,1,0:T(8,128)(2,1)}, u32[]{:S(2)}) copy-start(bf16[32,16,256]{2,1,0:T(8,128)(2,1)} %param.6) | copy-start | bytes 786436
  1.8 7.3 %collective-permute-start.7 = (bf16[32,16,256]{2,0,1:T(8,128)(2,1)S(1)}, bf16[32,16,256]{2,0,1:T(8,128)(2,1)S(1)}, u32[]{:S(2)}, u32[]{:S(2)}) collective-permute-start(bf16[32,16,256]{2,0,1:T(8,128)(2,1)S(1)} %copy.50), channel_id=1, source_target_pairs={{0,2},{2,4},{4,6},{1,3},{3,5},{5,7},{8,10},{10,12},{12,14},{9,11},... | collective-permute-start | bytes 786440 | tf_op jit(solution)/shard_map/ppermute | solution.py:45
  5.9 8.2 %collective-permute-start.10 = (bf16[32,16,256]{2,0,1:T(8,128)(2,1)S(1)}, bf16[32,16,256]{2,0,1:T(8,128)(2,1)S(1)}, u32[]{:S(2)}, u32[]{:S(2)}) collective-permute-start(bf16[32,16,256]{2,0,1:T(8,128)(2,1)S(1)} %copy.50), channel_id=1, source_target_pairs={{2,0},{4,2},{6,4},{3,1},{5,3},{7,5},{10,8},{12,10},{14,12},{11,9},... | collective-permute-start | bytes 786440 | tf_op jit(solution)/shard_map/ppermute | solution.py:46
  9.2 8.2 %collective-permute-start.8 = (bf16[32,16,256]{2,0,1:T(8,128)(2,1)S(1)}, bf16[32,16,256]{2,0,1:T(8,128)(2,1)S(1)}, u32[]{:S(2)}, u32[]{:S(2)}) collective-permute-start(bf16[32,16,256]{2,0,1:T(8,128)(2,1)S(1)} %collective-permute-done.7), channel_id=1, source_target_pairs={{0,2},{2,4},{4,6},{1,3},{3,5},{5,7},{8,10},{10,12},{12,14},{9,11},... | collective-permute-start | bytes 786440 | tf_op jit(solution)/shard_map/ppermute | solution.py:45
  14.1 8.8 %collective-permute-start.11 = (bf16[32,16,256]{2,0,1:T(8,128)(2,1)S(1)}, bf16[32,16,256]{2,0,1:T(8,128)(2,1)S(1)}, u32[]{:S(2)}, u32[]{:S(2)}) collective-permute-start(bf16[32,16,256]{2,0,1:T(8,128)(2,1)S(1)} %collective-permute-done.10), channel_id=1, source_target_pairs={{2,0},{4,2},{6,4},{3,1},{5,3},{7,5},{10,8},{12,10},{14,12},{11,9},... | collective-permute-start | bytes 786440 | tf_op jit(solution)/shard_map/ppermute | solution.py:46
  17.3 8.1 %collective-permute-start.9 = (bf16[32,16,256]{2,0,1:T(8,128)(2,1)S(1)}, bf16[32,16,256]{2,0,1:T(8,128)(2,1)}, u32[]{:S(2)}, u32[]{:S(2)}) collective-permute-start(bf16[32,16,256]{2,0,1:T(8,128)(2,1)S(1)} %collective-permute-done.8), channel_id=1, source_target_pairs={{0,2},{2,4},{4,6},{1,3},{3,5},{5,7},{8,10},{10,12},{12,14},{9,11},... | collective-permute-start | bytes 786440 | tf_op jit(solution)/shard_map/ppermute | solution.py:45
  22.9 7.2 %collective-permute-start.12 = (bf16[32,16,256]{2,0,1:T(8,128)(2,1)S(1)}, bf16[32,16,256]{2,0,1:T(8,128)(2,1)S(1)}, u32[]{:S(2)}, u32[]{:S(2)}) collective-permute-start(bf16[32,16,256]{2,0,1:T(8,128)(2,1)S(1)} %collective-permute-done.11), channel_id=1, source_target_pairs={{2,0},{4,2},{6,4},{3,1},{5,3},{7,5},{10,8},{12,10},{14,12},{11,9},... | collective-permute-start | bytes 786440 | tf_op jit(solution)/shard_map/ppermute | solution.py:46
  30.1 1.3 copy-start.7
  32.4 9.8 %collective-permute-start.13 = (bf16[4,32,16,256]{3,1,0,2:T(8,128)(2,1)}, bf16[4,32,16,256]{3,1,0,2:T(8,128)(2,1)S(1)}, u32[]{:S(2)}, u32[]{:S(2)}) collective-permute-start(bf16[4,32,16,256]{3,1,0,2:T(8,128)(2,1)} %constant_dynamic-slice_fusion.2), channel_id=1, source_target_pairs={{0,1},{1,0},{2,3},{3,2},{4,5},{5,4},{6,7},{7,6},{8,9},{9,8},{10,11... | collective-permute-start | bytes 3145736 | tf_op jit(solution)/shard_map/ppermute | solution.py:49
  48.6 17.6 %copy-start.12 = (bf16[32,16,256]{2,1,0:T(8,128)(2,1)S(1)}, bf16[32,16,256]{2,1,0:T(8,128)(2,1)}, u32[]{:S(2)}) copy-start(bf16[32,16,256]{2,1,0:T(8,128)(2,1)} %param.7) | copy-start | bytes 786436
  48.6 97.8 %all-to-all-start = ((bf16[16,256,256]{2,0,1:T(8,128)(2,1)}), bf16[16,256,256]{2,0,1:T(8,128)(2,1)}, u32[]{:S(2)}, u32[]{:S(2)}) async-start(bf16[16,256,256]{2,0,1:T(8,128)(2,1)} %copy.59), calls=%async_computation | async-start | bytes 4194304 | tf_op jit(solution)/shard_map/all_to_all | solution.py:89
  66.2 50.1 %collective-permute-start = (bf16[32,16,256]{2,0,1:T(8,128)(2,1)S(1)}, bf16[32,16,256]{2,0,1:T(8,128)(2,1)S(1)}, u32[]{:S(2)}, u32[]{:S(2)}) collective-permute-start(bf16[32,16,256]{2,0,1:T(8,128)(2,1)S(1)} %copy.43), channel_id=1, source_target_pairs={{0,2},{2,4},{4,6},{1,3},{3,5},{5,7},{8,10},{10,12},{12,14},{9,11},... | collective-permute-start | bytes 786440 | tf_op jit(solution)/shard_map/ppermute | solution.py:45
  67.9 52.7 %collective-permute-start.3 = (bf16[32,16,256]{2,0,1:T(8,128)(2,1)S(1)}, bf16[32,16,256]{2,0,1:T(8,128)(2,1)S(1)}, u32[]{:S(2)}, u32[]{:S(2)}) collective-permute-start(bf16[32,16,256]{2,0,1:T(8,128)(2,1)S(1)} %copy.43), channel_id=1, source_target_pairs={{2,0},{4,2},{6,4},{3,1},{5,3},{7,5},{10,8},{12,10},{14,12},{11,9},... | collective-permute-start | bytes 786440 | tf_op jit(solution)/shard_map/ppermute | solution.py:46
  116.3 8.7 %collective-permute-start.1 = (bf16[32,16,256]{2,0,1:T(8,128)(2,1)S(1)}, bf16[32,16,256]{2,0,1:T(8,128)(2,1)S(1)}, u32[]{:S(2)}, u32[]{:S(2)}) collective-permute-start(bf16[32,16,256]{2,0,1:T(8,128)(2,1)S(1)} %collective-permute-done), channel_id=1, source_target_pairs={{0,2},{2,4},{4,6},{1,3},{3,5},{5,7},{8,10},{10,12},{12,14},{9,11},... | collective-permute-start | bytes 786440 | tf_op jit(solution)/shard_map/ppermute | solution.py:45
  120.5 8.6 %collective-permute-start.4 = (bf16[32,16,256]{2,0,1:T(8,128)(2,1)S(1)}, bf16[32,16,256]{2,0,1:T(8,128)(2,1)S(1)}, u32[]{:S(2)}, u32[]{:S(2)}) collective-permute-start(bf16[32,16,256]{2,0,1:T(8,128)(2,1)S(1)} %collective-permute-done.3), channel_id=1, source_target_pairs={{2,0},{4,2},{6,4},{3,1},{5,3},{7,5},{10,8},{12,10},{14,12},{11,9},... | collective-permute-start | bytes 786440 | tf_op jit(solution)/shard_map/ppermute | solution.py:46
  125.0 7.8 %collective-permute-start.2 = (bf16[32,16,256]{2,0,1:T(8,128)(2,1)S(1)}, bf16[32,16,256]{2,0,1:T(8,128)(2,1)S(1)}, u32[]{:S(2)}, u32[]{:S(2)}) collective-permute-start(bf16[32,16,256]{2,0,1:T(8,128)(2,1)S(1)} %collective-permute-done.1), channel_id=1, source_target_pairs={{0,2},{2,4},{4,6},{1,3},{3,5},{5,7},{8,10},{10,12},{12,14},{9,11},... | collective-permute-start | bytes 786440 | tf_op jit(solution)/shard_map/ppermute | solution.py:45
  129.2 8.9 %collective-permute-start.5 = (bf16[32,16,256]{2,0,1:T(8,128)(2,1)S(1)}, bf16[32,16,256]{2,0,1:T(8,128)(2,1)S(1)}, u32[]{:S(2)}, u32[]{:S(2)}) collective-permute-start(bf16[32,16,256]{2,0,1:T(8,128)(2,1)S(1)} %collective-permute-done.4), channel_id=1, source_target_pairs={{2,0},{4,2},{6,4},{3,1},{5,3},{7,5},{10,8},{12,10},{14,12},{11,9},... | collective-permute-start | bytes 786440 | tf_op jit(solution)/shard_map/ppermute | solution.py:46
  138.2 6.6 %collective-permute-start.6 = (bf16[4,32,16,256]{3,1,0,2:T(8,128)(2,1)S(1)}, bf16[4,32,16,256]{3,1,0,2:T(8,128)(2,1)S(1)}, u32[]{:S(2)}, u32[]{:S(2)}) collective-permute-start(bf16[4,32,16,256]{3,1,0,2:T(8,128)(2,1)S(1)} %constant_dynamic-slice_fusion.3), channel_id=1, source_target_pairs={{0,1},{1,0},{2,3},{3,2},{4,5},{5,4},{6,7},{7,6},{8,9},{9,8},{10,11... | collective-permute-start | bytes 3145736 | tf_op jit(solution)/shard_map/ppermute | solution.py:49
  146.4 2.2 copy-start.6
  146.4 2.9 copy-start.10
  148.3 2.0 copy-start.1
  150.3 1.4 copy-start.5
  154.9 60.8 %all-to-all-start.1 = ((bf16[1024,4,256]{2,1,0:T(4,128)(2,1)}), bf16[1024,4,256]{2,1,0:T(4,128)(2,1)}, u32[]{:S(2)}, u32[]{:S(2)}) async-start(bf16[1024,4,256]{2,1,0:T(4,128)(2,1)} %copy.65), calls=%async_computation.1 | async-start | bytes 4194304 | tf_op jit(solution)/shard_map/all_to_all | solution.py:112
  172.3 71.0 %collective-permute-start.21 = (bf16[4,32,16,256]{3,2,1,0:T(8,128)(2,1)}, bf16[4,32,16,256]{3,2,1,0:T(8,128)(2,1)}, u32[]{:S(2)}, u32[]{:S(2)}) collective-permute-start(bf16[4,32,16,256]{3,2,1,0:T(8,128)(2,1)} %bitcast.165), channel_id=1, source_target_pairs={{0,1},{1,0},{2,3},{3,2},{4,5},{5,4},{6,7},{7,6},{8,9},{9,8},{10,11... | collective-permute-start | bytes 3145736 | tf_op jit(solution)/shard_map/ppermute | solution.py:61
  234.7 1.3 copy-start.8
  237.1 18.8 %collective-permute-start.14 = (bf16[4,32,16,256]{3,1,0,2:T(8,128)(2,1)}, bf16[4,32,16,256]{3,1,0,2:T(8,128)(2,1)}, u32[]{:S(2)}, u32[]{:S(2)}) collective-permute-start(bf16[4,32,16,256]{3,1,0,2:T(8,128)(2,1)} %dynamic-slice_bitcast_fusion), channel_id=1, source_target_pairs={{0,1},{1,0},{2,3},{3,2},{4,5},{5,4},{6,7},{7,6},{8,9},{9,8},{10,11... | collective-permute-start | bytes 3145736 | tf_op jit(solution)/shard_map/ppermute | solution.py:61
  243.4 12.6 %copy-start.9 = (bf16[16,256,4,2,32]{1,4,3,2,0:T(8,128)(2,1)S(1)}, bf16[16,256,4,2,32]{1,4,3,2,0:T(8,128)(2,1)}, u32[]{:S(2)}) copy-start(bf16[16,256,4,2,32]{1,4,3,2,0:T(8,128)(2,1)} %copy-done.8) | copy-start | bytes 6291460
  245.4 12.1 %copy-start.2 = (f32[4,32,16,256]{3,2,1,0:T(8,128)}, f32[4,32,16,256]{3,2,1,0:T(8,128)S(1)}, u32[]{:S(2)}) copy-start(f32[4,32,16,256]{3,2,1,0:T(8,128)S(1)} %convert_add_fusion) | copy-start | bytes 6291460
  245.5 16.6 %collective-permute-start.22 = (bf16[32,16,256]{2,1,0:T(8,128)(2,1)S(1)}, bf16[32,16,256]{2,1,0:T(8,128)(2,1)}, u32[]{:S(2)}, u32[]{:S(2)}) collective-permute-start(bf16[32,16,256]{2,1,0:T(8,128)(2,1)S(1)} %get-tuple-element.10), channel_id=1, source_target_pairs={{0,2},{2,4},{4,6},{1,3},{3,5},{5,7},{8,10},{10,12},{12,14},{9,11},... | collective-permute-start | bytes 786440 | tf_op jit(solution)/shard_map/ppermute | solution.py:71
  257.5 1.3 copy-start.3
  258.9 10.5 %collective-permute-start.15 = (bf16[32,16,256]{2,0,1:T(8,128)(2,1)S(1)}, bf16[32,16,256]{2,0,1:T(8,128)(2,1)}, u32[]{:S(2)}, u32[]{:S(2)}) collective-permute-start(bf16[32,16,256]{2,0,1:T(8,128)(2,1)S(1)} %get-tuple-element.16), channel_id=1, source_target_pairs={{0,2},{2,4},{4,6},{1,3},{3,5},{5,7},{8,10},{10,12},{12,14},{9,11},... | collective-permute-start | bytes 786440 | tf_op jit(solution)/shard_map/ppermute | solution.py:71
  260.9 13.8 %collective-permute-start.25 = (bf16[32,16,256]{2,1,0:T(8,128)(2,1)S(1)}, bf16[32,16,256]{2,1,0:T(8,128)(2,1)}, u32[]{:S(2)}, u32[]{:S(2)}) collective-permute-start(bf16[32,16,256]{2,1,0:T(8,128)(2,1)S(1)} %get-tuple-element.11), channel_id=1, source_target_pairs={{2,0},{4,2},{6,4},{3,1},{5,3},{7,5},{10,8},{12,10},{14,12},{11,9},... | collective-permute-start | bytes 786440 | tf_op jit(solution)/shard_map/ppermute | solution.py:71
  263.4 11.3 %collective-permute-start.23 = (bf16[32,16,256]{2,1,0:T(8,128)(2,1)S(1)}, bf16[32,16,256]{2,1,0:T(8,128)(2,1)}, u32[]{:S(2)}, u32[]{:S(2)}) collective-permute-start(bf16[32,16,256]{2,1,0:T(8,128)(2,1)S(1)} %fusion.29), channel_id=1, source_target_pairs={{0,2},{2,4},{4,6},{1,3},{3,5},{5,7},{8,10},{10,12},{12,14},{9,11},... | collective-permute-start | bytes 786440 | tf_op jit(solution)/shard_map/ppermute | solution.py:71
  268.1 10.2 %collective-permute-start.18 = (bf16[32,16,256]{2,0,1:T(8,128)(2,1)S(1)}, bf16[32,16,256]{2,0,1:T(8,128)(2,1)}, u32[]{:S(2)}, u32[]{:S(2)}) collective-permute-start(bf16[32,16,256]{2,0,1:T(8,128)(2,1)S(1)} %get-tuple-element.17), channel_id=1, source_target_pairs={{2,0},{4,2},{6,4},{3,1},{5,3},{7,5},{10,8},{12,10},{14,12},{11,9},... | collective-permute-start | bytes 786440 | tf_op jit(solution)/shard_map/ppermute | solution.py:71
  270.6 8.4 %collective-permute-start.16 = (bf16[32,16,256]{2,0,1:T(8,128)(2,1)S(1)}, bf16[32,16,256]{2,0,1:T(8,128)(2,1)S(1)}, u32[]{:S(2)}, u32[]{:S(2)}) collective-permute-start(bf16[32,16,256]{2,0,1:T(8,128)(2,1)S(1)} %fusion.35), channel_id=1, source_target_pairs={{0,2},{2,4},{4,6},{1,3},{3,5},{5,7},{8,10},{10,12},{12,14},{9,11},... | collective-permute-start | bytes 786440 | tf_op jit(solution)/shard_map/ppermute | solution.py:71
  274.6 4.4 %copy-start.4 = (f32[4,32,16,256]{3,1,0,2:T(8,128)S(1)}, f32[4,32,16,256]{3,1,0,2:T(8,128)}, u32[]{:S(2)}) copy-start(f32[4,32,16,256]{3,1,0,2:T(8,128)} %copy-done.3) | copy-start | bytes 6291460
  277.0 10.0 %collective-permute-start.26 = (bf16[32,16,256]{2,1,0:T(8,128)(2,1)S(1)}, bf16[32,16,256]{2,1,0:T(8,128)(2,1)S(1)}, u32[]{:S(2)}, u32[]{:S(2)}) collective-permute-start(bf16[32,16,256]{2,1,0:T(8,128)(2,1)S(1)} %get-tuple-element.9), channel_id=1, source_target_pairs={{2,0},{4,2},{6,4},{3,1},{5,3},{7,5},{10,8},{12,10},{14,12},{11,9},... | collective-permute-start | bytes 786440 | tf_op jit(solution)/shard_map/ppermute | solution.py:71
  280.9 12.5 %collective-permute-start.19 = (bf16[32,16,256]{2,0,1:T(8,128)(2,1)}, bf16[32,16,256]{2,0,1:T(8,128)(2,1)S(1)}, u32[]{:S(2)}, u32[]{:S(2)}) collective-permute-start(bf16[32,16,256]{2,0,1:T(8,128)(2,1)} %get-tuple-element.15), channel_id=1, source_target_pairs={{2,0},{4,2},{6,4},{3,1},{5,3},{7,5},{10,8},{12,10},{14,12},{11,9},... | collective-permute-start | bytes 786440 | tf_op jit(solution)/shard_map/ppermute | solution.py:71
  282.2 14.3 %collective-permute-start.24 = (bf16[32,16,256]{2,1,0:T(8,128)(2,1)}, bf16[32,16,256]{2,1,0:T(8,128)(2,1)S(1)}, u32[]{:S(2)}, u32[]{:S(2)}) collective-permute-start(bf16[32,16,256]{2,1,0:T(8,128)(2,1)} %get-tuple-element.8), channel_id=1, source_target_pairs={{0,2},{2,4},{4,6},{1,3},{3,5},{5,7},{8,10},{10,12},{12,14},{9,11},... | collective-permute-start | bytes 786440 | tf_op jit(solution)/shard_map/ppermute | solution.py:71
  288.1 8.5 %collective-permute-start.27 = (bf16[32,16,256]{2,1,0:T(8,128)(2,1)S(1)}, bf16[32,16,256]{2,1,0:T(8,128)(2,1)S(1)}, u32[]{:S(2)}, u32[]{:S(2)}) collective-permute-start(bf16[32,16,256]{2,1,0:T(8,128)(2,1)S(1)} %fusion.28), channel_id=1, source_target_pairs={{2,0},{4,2},{6,4},{3,1},{5,3},{7,5},{10,8},{12,10},{14,12},{11,9},... | collective-permute-start | bytes 786440 | tf_op jit(solution)/shard_map/ppermute | solution.py:71
  289.4 9.0 %collective-permute-start.17 = (bf16[32,16,256]{2,0,1:T(8,128)(2,1)}, bf16[32,16,256]{2,0,1:T(8,128)(2,1)S(1)}, u32[]{:S(2)}, u32[]{:S(2)}) collective-permute-start(bf16[32,16,256]{2,0,1:T(8,128)(2,1)} %get-tuple-element.14), channel_id=1, source_target_pairs={{0,2},{2,4},{4,6},{1,3},{3,5},{5,7},{8,10},{10,12},{12,14},{9,11},... | collective-permute-start | bytes 786440 | tf_op jit(solution)/shard_map/ppermute | solution.py:71
  295.3 7.3 %collective-permute-start.20 = (bf16[32,16,256]{2,0,1:T(8,128)(2,1)}, bf16[32,16,256]{2,0,1:T(8,128)(2,1)S(1)}, u32[]{:S(2)}, u32[]{:S(2)}) collective-permute-start(bf16[32,16,256]{2,0,1:T(8,128)(2,1)} %fusion.34), channel_id=1, source_target_pairs={{2,0},{4,2},{6,4},{3,1},{5,3},{7,5},{10,8},{12,10},{14,12},{11,9},... | collective-permute-start | bytes 786440 | tf_op jit(solution)/shard_map/ppermute | solution.py:71

commit v3 on v2

--- a/solution.py
+++ b/solution.py
@@ -83,7 +83,7 @@
     scale_factor = 1.0 / math.sqrt(row_count * replica_count)
     inputs = input_field.reshape(block_count, block_size, row_count)
     first_full = gather_rows(first_factor)
-    second_full = gather_rows(second_factor)
+    second_full = lax.all_gather(second_factor, ("ylo", "core"), axis=0, tiled=True)
     pre_act = jnp.einsum("bkr,kbi->bir", inputs, first_full, preferred_element_type=jnp.float32)
     activated = gelu_value(pre_act).astype(jnp.bfloat16)
     received = lax.all_to_all(activated, "blk", split_axis=1, concat_axis=0, tiled=True)
@@ -101,12 +101,14 @@
     n_core = lax.axis_size("core")
     n_ylo = lax.axis_size("ylo")
     kk = block_size // (n_core * n_ylo)
-    permuted_cm = permuted.reshape(group_count, n_ylo, n_core, kk, inner_count, row_count)
     term = jnp.einsum(
-        "gyxcir,igjr->xycigj", permuted_cm, residual, preferred_element_type=jnp.float32
+        "gcir,igjr->cigj", permuted, residual, preferred_element_type=jnp.float32
     )
-    second_out = scatter_rows(
-        term.reshape(n_core, n_ylo, kk, block_count, block_size).astype(jnp.bfloat16)
+    second_out = lax.psum_scatter(
+        term.reshape(count, block_count, block_size).astype(jnp.bfloat16),
+        ("ylo", "core"),
+        scatter_dimension=0,
+        tiled=True,
     )
     sending = permuted_grad.reshape(group_count * block_size, inner_count, row_count)
     activated_grad = lax.all_to_all(sending, "blk", split_axis=0, concat_axis=1, tiled=True)

time: 309 us -> 314 us (1.016)
  starting transfers between devices: 120 us -> 95 us
  waiting for transfers between devices: 115 us -> 131 us
  between operations: 1.35 us -> 14.5 us
  other arithmetic: 18.7 us -> 7.97 us
  local copies, waits for them, and re-layouts: 34.1 us -> 43.2 us
  matrix products: 14.8 us -> 18.4 us
    all_gather x0 -> x1, waiting for transfers between devices: none -> 61.3 us  [shards(): lax.all_gather(second_factor, ('ylo', 'core'), axis=0, tiled=True)]
    ppermute x6 -> x3, waiting for transfers between devices: 57.8 us -> 6.24 us  [gather_rows(): right.append(lax.ppermute(right[-1], 'ylo', line_pairs(n_ylo, 1)))]
    ppermute x12 -> x6, waiting for transfers between devices: 4.87 us -> 17.6 us  [scatter_rows(): lax.ppermute(block.astype(jnp.bfloat16), 'ylo', line_pairs(n_ylo, step))]
    ppermute x6 -> x3, starting transfers between devices: 24.5 us -> 13.8 us  [gather_rows(): right.append(lax.ppermute(right[-1], 'ylo', line_pairs(n_ylo, 1)))]
    convert_element_type x0 -> x2, local copies, waits for them, and re-layouts: none -> 9.16 us  [the longest x1 4.62 us: shards(): targets.astype(jnp.float32)]
    convert_element_type x6 -> x3, other arithmetic: 9.67 us -> 4.32 us  [scatter_rows(): block.astype(jnp.bfloat16)]
    ppermute x6 -> x3, waiting for transfers between devices: 8.53 us -> 3.49 us  [gather_rows(): left.append(lax.ppermute(left[-1], 'ylo', line_pairs(n_ylo, -1)))]
    ppermute x2 -> x1, starting transfers between devices: 11.7 us -> 6.67 us  [gather_rows(): other = lax.ppermute(line, 'core', swap_pairs(n_core))]
  transfers between devices with their start and end apart: 30 -> 18, of which waited for: 13 -> 12; matrix products, arithmetic and copies ran while one was open for 15% -> 15% of each run, Pallas kernels for 0% -> 0%
where the time goes in v3:
time: 314 us; the launch traced here: 310 us
  waiting for transfers between devices  131 us (42%)
  starting transfers between devices  95 us (30%)
  local copies, waits for them, and re-layouts  43.2 us (14%)
  matrix products  18.4 us (6%)
  between operations  14.5 us (5%)
  other arithmetic  7.97 us (3%)
    all_gather x1, waiting for transfers between devices, shards(): lax.all_gather(second_factor, ('ylo', 'core'), axis=0, tiled=True)  61.3 us
    all_to_all x1, waiting for transfers between devices, shards(): lax.all_to_all(sending, 'blk', split_axis=0, concat_axis=1, tiled=True)  38.2 us
    ppermute x6, starting transfers between devices, scatter_rows(): lax.ppermute(block.astype(jnp.bfloat16), 'ylo', line_pairs(n_ylo, step))  33.3 us
    ppermute x6, waiting for transfers between devices, scatter_rows(): lax.ppermute(block.astype(jnp.bfloat16), 'ylo', line_pairs(n_ylo, step))  17.6 us
    all_to_all x1, starting transfers between devices, shards(): lax.all_to_all(activated, 'blk', split_axis=1, concat_axis=0, tiled=True)  17.4 us
    all_to_all x1, starting transfers between devices, shards(): lax.all_to_all(sending, 'blk', split_axis=0, concat_axis=1, tiled=True)  14 us
    ppermute x3, starting transfers between devices, gather_rows(): right.append(lax.ppermute(right[-1], 'ylo', line_pairs(n_ylo, 1)))  13.8 us
    convert_element_type x2, local copies, waits for them, and re-layouts, shards(): activated_grad.astype(jnp.float32) * gelu_slope(pre_act)  10.1 us
  transfers between devices with their start and end apart: 18, of which 12 were waited for; matrix products, arithmetic and copies ran while one was open for 15% of the time, Pallas kernels for 0%

profile of v3, /device:TPU:1, one launch (start us, length us, event | category | flops | bytes accessed | tf_op | source)
XLA Modules:
  0.0 310.2 jit_solution(16158436295923360821)
XLA Ops:
  7.2 4.2 %collective-permute-start = (bf16[32,16,256]{2,1,0:T(8,128)(2,1)}, bf16[32,16,256]{2,1,0:T(8,128)(2,1)S(1)}, u32[]{:S(2)}, u32[]{:S(2)}) collective-permute-start(bf16[32,16,256]{2,1,0:T(8,128)(2,1)} %param.6), channel_id=1, source_target_pairs={{0,2},{2,4},{4,6},{1,3},{3,5},{5,7},{8,10},{10,12},{12,14},{9,11},... | collective-permute-start | bytes 786440 | tf_op jit(solution)/shard_map/ppermute | solution.py:45
  11.4 1.3 collective-permute-start.3
  12.7 2.3 collective-permute-done
  15.0 4.9 %collective-permute-start.1 = (bf16[32,16,256]{2,1,0:T(8,128)(2,1)S(1)}, bf16[32,16,256]{2,1,0:T(8,128)(2,1)S(1)}, u32[]{:S(2)}, u32[]{:S(2)}) collective-permute-start(bf16[32,16,256]{2,1,0:T(8,128)(2,1)S(1)} %collective-permute-done), channel_id=1, source_target_pairs={{0,2},{2,4},{4,6},{1,3},{3,5},{5,7},{8,10},{10,12},{12,14},{9,11},... | collective-permute-start | bytes 786440 | tf_op jit(solution)/shard_map/ppermute | solution.py:45
  19.8 1.3 collective-permute-start.4
  21.1 2.0 collective-permute-done.1
  23.1 4.7 %collective-permute-start.2 = (bf16[32,16,256]{2,1,0:T(8,128)(2,1)S(1)}, bf16[32,16,256]{2,1,0:T(8,128)(2,1)S(1)}, u32[]{:S(2)}, u32[]{:S(2)}) collective-permute-start(bf16[32,16,256]{2,1,0:T(8,128)(2,1)S(1)} %collective-permute-done.1), channel_id=1, source_target_pairs={{0,2},{2,4},{4,6},{1,3},{3,5},{5,7},{8,10},{10,12},{12,14},{9,11},... | collective-permute-start | bytes 786440 | tf_op jit(solution)/shard_map/ppermute | solution.py:45
  27.9 1.3 collective-permute-start.5
  29.2 2.0 collective-permute-done.2
  31.2 1.0 bitcast_dynamic-update-slice_fusion.3
  32.3 3.5 %collective-permute-done.5 = bf16[32,16,256]{2,1,0:T(8,128)(2,1)S(1)} collective-permute-done((bf16[32,16,256]{2,1,0:T(8,128)(2,1)S(1)}, bf16[32,16,256]{2,1,0:T(8,128)(2,1)S(1)}, u32[]{:S(2)}, u32[]{:S(2)}) %collective-permute-start.5) | collective-permute-done | bytes 262176 | tf_op jit(solution)/shard_map/ppermute | solution.py:46
  35.8 1.2 copy-done.6
  37.0 1.0 constant_dynamic-slice_fusion
  38.0 6.7 %collective-permute-start.6 = (bf16[4,32,16,256]{3,2,1,0:T(8,128)(2,1)}, bf16[4,32,16,256]{3,2,1,0:T(8,128)(2,1)S(1)}, u32[]{:S(2)}, u32[]{:S(2)}) collective-permute-start(bf16[4,32,16,256]{3,2,1,0:T(8,128)(2,1)} %constant_dynamic-slice_fusion), channel_id=1, source_target_pairs={{0,1},{1,0},{2,3},{3,2},{4,5},{5,4},{6,7},{7,6},{8,9},{9,8},{10,11... | collective-permute-start | bytes 3145736 | tf_op jit(solution)/shard_map/ppermute | solution.py:49
  44.7 1.3 fusion.43
  46.0 1.2 collective-permute-done.6
  47.2 0.3 maximum_select_fusion
  47.5 4.1 %multiply_convert_fusion = (bf16[16,256,256]{2,1,0:T(8,128)(2,1)S(1)}, f32[16,256,256]{2,1,0:T(8,128)}) fusion(bf16[16,256,256]{2,1,0:T(8,128)(2,1)S(1)} %bitcast.97, bf16[256,16,256]{2,1,0:T(8,128)(2,1)S(1)} %bitcast.106), kind=kOutput, calls=%fused_computation.13 | convolution fusion | flops 546308096 | bytes 10485760 | tf_op jit(solution)/shard_map/bkr,kbi->bir/dot_general | solution.py:87
  51.6 2.5 copy.46
  54.1 17.4 %all-to-all-start = ((bf16[16,256,256]{2,0,1:T(8,128)(2,1)}), bf16[16,256,256]{2,0,1:T(8,128)(2,1)}, u32[]{:S(2)}, u32[]{:S(2)}) async-start(bf16[16,256,256]{2,0,1:T(8,128)(2,1)} %copy.46), calls=%async_computation | async-start | bytes 4194304 | tf_op jit(solution)/shard_map/all_to_all | solution.py:89
  71.5 0.0 all-gather.2.cloned.1.call-start
  71.6 0.7 all-gather.2.cloned.1.call-update
  72.3 4.6 %copy.50 = f32[4,4,256,256]{2,3,1,0:T(8,128)} copy(bf16[4,4,256,256]{3,2,1,0:T(8,128)(2,1)} %bitcast.105) | data formatting | bytes 6291456 | tf_op jit(solution)/shard_map/convert_element_type | solution.py:97
  76.9 61.3 %all-gather.2.cloned.1.call-done = bf16[256,16,256]{2,1,0:T(8,128)(2,1)} async-done(((bf16[32,16,256]{2,1,0:T(8,128)(2,1)}), bf16[256,16,256]{2,1,0:T(8,128)(2,1)}) %all-gather.2.cloned.1.call-update) | async-done | bytes 2097168 | tf_op jit(solution)/shard_map/all_gather | solution.py:86
  138.1 3.7 %copy.48 = bf16[256,16,256]{2,0,1:T(8,128)(2,1)} copy(bf16[256,16,256]{2,1,0:T(8,128)(2,1)} %all-gather.2.cloned.1.call-done) | data formatting | bytes 4194304 | tf_op jit(solution)/shard_map/all_gather | solution.py:86
  141.8 1.9 copy.47
  143.7 0.9 copy-done.2
  144.6 2.8 fusion.8
  147.4 0.7 convert_bitcast_fusion.1
  148.2 0.6 copy-done.4
  148.8 0.1 copy.53
  148.9 3.0 copy.54
  151.9 14.0 %all-to-all-start.1 = ((bf16[1024,4,256]{2,1,0:T(4,128)(2,1)}), bf16[1024,4,256]{2,1,0:T(4,128)(2,1)}, u32[]{:S(2)}, u32[]{:S(2)}) async-start(bf16[1024,4,256]{2,1,0:T(4,128)(2,1)} %copy.54), calls=%async_computation.1 | async-start | bytes 4194304 | tf_op jit(solution)/shard_map/all_to_all | solution.py:114
  166.0 0.2 reduce-scatter.2.cloned.1.call-start
  166.2 4.3 %convolution_convert_fusion = bf16[4,4,256,256]{3,2,1,0:T(8,128)(2,1)} fusion(bf16[4,4,256,256]{2,3,1,0:T(8,128)(2,1)} %copy-done.4, bf16[4,256,4,256]{3,1,0,2:T(8,128)(2,1)} %bitcast.99), kind=kOutput, calls=%fused_computation.25 | convolution fusion | flops 537919488 | bytes 6291456 | tf_op jit(solution)/shard_map/gcir,igjr->cigj/dot_general | solution.py:104
  170.5 4.5 %copy.60 = bf16[256,16,256]{2,1,0:T(8,128)(2,1)} copy(bf16[256,16,256]{0,2,1:T(8,128)(2,1)} %bitcast.102) | data formatting | bytes 4194304 | tf_op jit(solution)/shard_map/convert_element_type | solution.py:108
  175.1 38.2 %all-to-all-done.1 = bf16[1024,4,256]{2,1,0:T(4,128)(2,1)} async-done(((bf16[1024,4,256]{2,1,0:T(4,128)(2,1)}), bf16[1024,4,256]{2,1,0:T(4,128)(2,1)}, u32[]{:S(2)}, u32[]{:S(2)}) %all-to-all-start.1) | async-done | bytes 2097184 | tf_op jit(solution)/shard_map/all_to_all | solution.py:114
  213.4 1.9 copy.55
  215.2 0.6 convert_bitcast_fusion
  215.8 4.7 %copy.56 = f32[16,64,4,256]{3,2,1,0:T(4,128)} copy(f32[16,64,4,256]{3,0,1,2:T(8,128)S(1)} %convert_bitcast_fusion) | data formatting | bytes 8388608 | tf_op jit(solution)/shard_map/convert_element_type | solution.py:115
  220.5 5.4 %reshape.40 = f32[16,256,256]{2,1,0:T(8,128)} reshape(f32[16,64,4,256]{3,2,1,0:T(4,128)} %copy.56) | data formatting | bytes 8388608 | tf_op jit(solution)/shard_map/convert_element_type | solution.py:115
  225.9 6.5 %fusion.21 = bf16[16,256,4,2,32]{1,4,3,2,0:T(8,128)(2,1)S(1)} fusion(bf16[16,4,2,32,256]{4,3,2,1,0:T(8,128)(2,1)S(1)} %bitcast.96, f32[16,256,256]{2,1,0:T(8,128)} %reshape.40, f32[16,256,256]{2,1,0:T(8,128)} %get-tuple-element.15), kind=kOutput, calls=%fused_computation.24 | convolution fusion | flops 557842432 | bytes 12582912 | tf_op jit(solution)/shard_map/byxkr,bir->xykbi/dot_general | solution.py:118
  232.4 1.4 copy-done.7
  233.8 1.1 dynamic-slice_bitcast_fusion
  234.9 5.7 %collective-permute-start.7 = (bf16[4,32,16,256]{3,1,0,2:T(8,128)(2,1)}, bf16[4,32,16,256]{3,1,0,2:T(8,128)(2,1)S(1)}, u32[]{:S(2)}, u32[]{:S(2)}) collective-permute-start(bf16[4,32,16,256]{3,1,0,2:T(8,128)(2,1)} %dynamic-slice_bitcast_fusion), channel_id=1, source_target_pairs={{0,1},{1,0},{2,3},{3,2},{4,5},{5,4},{6,7},{7,6},{8,9},{9,8},{10,11... | collective-permute-start | bytes 3145736 | tf_op jit(solution)/shard_map/ppermute | solution.py:61
  240.5 2.5 collective-permute-done.7
  243.0 1.6 bitcast_add_fusion
  244.7 1.4 copy-done.3
  246.0 0.1 fusion.31
  246.1 19.7 %collective-permute-start.8 = (bf16[32,16,256]{2,0,1:T(8,128)(2,1)S(1)}, bf16[32,16,256]{2,0,1:T(8,128)(2,1)S(1)}, u32[]{:S(2)}, u32[]{:S(2)}) collective-permute-start(bf16[32,16,256]{2,0,1:T(8,128)(2,1)S(1)} %get-tuple-element.12), channel_id=1, source_target_pairs={{0,2},{2,4},{4,6},{1,3},{3,5},{5,7},{8,10},{10,12},{12,14},{9,11},... | collective-permute-start | bytes 786440 | tf_op jit(solution)/shard_map/ppermute | solution.py:71
  265.8 1.3 collective-permute-start.11
  267.1 4.0 %collective-permute-done.8 = bf16[32,16,256]{2,0,1:T(8,128)(2,1)S(1)} collective-permute-done((bf16[32,16,256]{2,0,1:T(8,128)(2,1)S(1)}, bf16[32,16,256]{2,0,1:T(8,128)(2,1)S(1)}, u32[]{:S(2)}, u32[]{:S(2)}) %collective-permute-start.8) | collective-permute-done | bytes 262176 | tf_op jit(solution)/shard_map/ppermute | solution.py:71
  271.1 1.1 fusion.26
  272.2 4.9 %collective-permute-start.9 = (bf16[32,16,256]{2,0,1:T(8,128)(2,1)S(1)}, bf16[32,16,256]{2,0,1:T(8,128)(2,1)S(1)}, u32[]{:S(2)}, u32[]{:S(2)}) collective-permute-start(bf16[32,16,256]{2,0,1:T(8,128)(2,1)S(1)} %fusion.26), channel_id=1, source_target_pairs={{0,2},{2,4},{4,6},{1,3},{3,5},{5,7},{8,10},{10,12},{12,14},{9,11},... | collective-permute-start | bytes 786440 | tf_op jit(solution)/shard_map/ppermute | solution.py:71
  277.2 4.3 %collective-permute-done.9 = bf16[32,16,256]{2,0,1:T(8,128)(2,1)S(1)} collective-permute-done((bf16[32,16,256]{2,0,1:T(8,128)(2,1)S(1)}, bf16[32,16,256]{2,0,1:T(8,128)(2,1)S(1)}, u32[]{:S(2)}, u32[]{:S(2)}) %collective-permute-start.9) | collective-permute-done | bytes 262176 | tf_op jit(solution)/shard_map/ppermute | solution.py:71
  281.5 2.1 fusion.27
  283.6 1.3 collective-permute-start.12
  284.9 4.7 %collective-permute-start.10 = (bf16[32,16,256]{2,0,1:T(8,128)(2,1)S(1)}, bf16[32,16,256]{2,0,1:T(8,128)(2,1)S(1)}, u32[]{:S(2)}, u32[]{:S(2)}) collective-permute-start(bf16[32,16,256]{2,0,1:T(8,128)(2,1)S(1)} %get-tuple-element.10), channel_id=1, source_target_pairs={{0,2},{2,4},{4,6},{1,3},{3,5},{5,7},{8,10},{10,12},{12,14},{9,11},... | collective-permute-start | bytes 786440 | tf_op jit(solution)/shard_map/ppermute | solution.py:71
  289.7 2.7 collective-permute-done.12
  292.4 1.1 fusion.25
  293.5 1.3 collective-permute-start.13
  294.8 6.6 %collective-permute-done.13 = bf16[32,16,256]{2,0,1:T(8,128)(2,1)S(1)} collective-permute-done((bf16[32,16,256]{2,0,1:T(8,128)(2,1)S(1)}, bf16[32,16,256]{2,0,1:T(8,128)(2,1)S(1)}, u32[]{:S(2)}, u32[]{:S(2)}) %collective-permute-start.13) | collective-permute-done | bytes 262176 | tf_op jit(solution)/shard_map/ppermute | solution.py:71
  301.4 1.2 fusion.29
  302.5 0.9 copy.61
  (24 shorter events, 0.2 us)
Async XLA Ops:
  7.2 40.3 %copy-start = (bf16[4096,256]{1,0:T(8,128)(2,1)S(1)}, bf16[4096,256]{1,0:T(8,128)(2,1)}, u32[]{:S(2)}) copy-start(bf16[4096,256]{1,0:T(8,128)(2,1)} %param.4) | copy-start | bytes 6291460
  7.2 7.8 %collective-permute-start = (bf16[32,16,256]{2,1,0:T(8,128)(2,1)}, bf16[32,16,256]{2,1,0:T(8,128)(2,1)S(1)}, u32[]{:S(2)}, u32[]{:S(2)}) collective-permute-start(bf16[32,16,256]{2,1,0:T(8,128)(2,1)} %param.6), channel_id=1, source_target_pairs={{0,2},{2,4},{4,6},{1,3},{3,5},{5,7},{8,10},{10,12},{12,14},{9,11},... | collective-permute-start | bytes 786440 | tf_op jit(solution)/shard_map/ppermute | solution.py:45
  11.4 8.5 %collective-permute-start.3 = (bf16[32,16,256]{2,1,0:T(8,128)(2,1)}, bf16[32,16,256]{2,1,0:T(8,128)(2,1)S(1)}, u32[]{:S(2)}, u32[]{:S(2)}) collective-permute-start(bf16[32,16,256]{2,1,0:T(8,128)(2,1)} %param.6), channel_id=1, source_target_pairs={{2,0},{4,2},{6,4},{3,1},{5,3},{7,5},{10,8},{12,10},{14,12},{11,9},... | collective-permute-start | bytes 786440 | tf_op jit(solution)/shard_map/ppermute | solution.py:46
  15.0 8.2 %collective-permute-start.1 = (bf16[32,16,256]{2,1,0:T(8,128)(2,1)S(1)}, bf16[32,16,256]{2,1,0:T(8,128)(2,1)S(1)}, u32[]{:S(2)}, u32[]{:S(2)}) collective-permute-start(bf16[32,16,256]{2,1,0:T(8,128)(2,1)S(1)} %collective-permute-done), channel_id=1, source_target_pairs={{0,2},{2,4},{4,6},{1,3},{3,5},{5,7},{8,10},{10,12},{12,14},{9,11},... | collective-permute-start | bytes 786440 | tf_op jit(solution)/shard_map/ppermute | solution.py:45
  19.8 8.0 %collective-permute-start.4 = (bf16[32,16,256]{2,1,0:T(8,128)(2,1)S(1)}, bf16[32,16,256]{2,1,0:T(8,128)(2,1)S(1)}, u32[]{:S(2)}, u32[]{:S(2)}) collective-permute-start(bf16[32,16,256]{2,1,0:T(8,128)(2,1)S(1)} %collective-permute-done.3), channel_id=1, source_target_pairs={{2,0},{4,2},{6,4},{3,1},{5,3},{7,5},{10,8},{12,10},{14,12},{11,9},... | collective-permute-start | bytes 786440 | tf_op jit(solution)/shard_map/ppermute | solution.py:46
  23.1 8.0 %collective-permute-start.2 = (bf16[32,16,256]{2,1,0:T(8,128)(2,1)S(1)}, bf16[32,16,256]{2,1,0:T(8,128)(2,1)S(1)}, u32[]{:S(2)}, u32[]{:S(2)}) collective-permute-start(bf16[32,16,256]{2,1,0:T(8,128)(2,1)S(1)} %collective-permute-done.1), channel_id=1, source_target_pairs={{0,2},{2,4},{4,6},{1,3},{3,5},{5,7},{8,10},{10,12},{12,14},{9,11},... | collective-permute-start | bytes 786440 | tf_op jit(solution)/shard_map/ppermute | solution.py:45
  27.9 7.9 %collective-permute-start.5 = (bf16[32,16,256]{2,1,0:T(8,128)(2,1)S(1)}, bf16[32,16,256]{2,1,0:T(8,128)(2,1)S(1)}, u32[]{:S(2)}, u32[]{:S(2)}) collective-permute-start(bf16[32,16,256]{2,1,0:T(8,128)(2,1)S(1)} %collective-permute-done.4), channel_id=1, source_target_pairs={{2,0},{4,2},{6,4},{3,1},{5,3},{7,5},{10,8},{12,10},{14,12},{11,9},... | collective-permute-start | bytes 786440 | tf_op jit(solution)/shard_map/ppermute | solution.py:46
  35.8 1.3 copy-start.6
  38.0 9.2 %collective-permute-start.6 = (bf16[4,32,16,256]{3,2,1,0:T(8,128)(2,1)}, bf16[4,32,16,256]{3,2,1,0:T(8,128)(2,1)S(1)}, u32[]{:S(2)}, u32[]{:S(2)}) collective-permute-start(bf16[4,32,16,256]{3,2,1,0:T(8,128)(2,1)} %constant_dynamic-slice_fusion), channel_id=1, source_target_pairs={{0,1},{1,0},{2,3},{3,2},{4,5},{5,4},{6,7},{7,6},{8,9},{9,8},{10,11... | collective-permute-start | bytes 3145736 | tf_op jit(solution)/shard_map/ppermute | solution.py:49
  54.1 87.7 %all-to-all-start = ((bf16[16,256,256]{2,0,1:T(8,128)(2,1)}), bf16[16,256,256]{2,0,1:T(8,128)(2,1)}, u32[]{:S(2)}, u32[]{:S(2)}) async-start(bf16[16,256,256]{2,0,1:T(8,128)(2,1)} %copy.46), calls=%async_computation | async-start | bytes 4194304 | tf_op jit(solution)/shard_map/all_to_all | solution.py:89
  71.5 66.6 %all-gather.2.cloned.1.call-start = ((), (), s32[]{:S(2)}) async-start(), calls=%async_computation.3 | async-start | bytes 2359296 | tf_op jit(solution)/shard_map/all_gather | solution.py:86
  141.8 2.8 copy-start.2
  143.7 3.7 %copy-start.1 = (bf16[64,16,4,256]{3,1,0,2:T(8,128)(2,1)}, bf16[64,16,4,256]{3,1,0,2:T(8,128)(2,1)S(1)}, u32[]{:S(2)}) copy-start(bf16[64,16,4,256]{3,1,0,2:T(8,128)(2,1)S(1)} %copy.47) | copy-start | bytes 6291460
  144.6 2.8 copy-start.5
  147.4 1.4 copy-start.4
  151.9 61.4 %all-to-all-start.1 = ((bf16[1024,4,256]{2,1,0:T(4,128)(2,1)}), bf16[1024,4,256]{2,1,0:T(4,128)(2,1)}, u32[]{:S(2)}, u32[]{:S(2)}) async-start(bf16[1024,4,256]{2,1,0:T(4,128)(2,1)} %copy.54), calls=%async_computation.1 | async-start | bytes 4194304 | tf_op jit(solution)/shard_map/all_to_all | solution.py:114
  166.0 137.4 %reduce-scatter.2.cloned.1.call-start = ((), (), s32[]{:S(2)}) async-start(), calls=%async_computation.4 | async-start | bytes 2359296 | tf_op jit(solution)/shard_map/reduce_scatter | solution.py:107
  232.4 1.4 copy-start.7
  234.9 8.1 %collective-permute-start.7 = (bf16[4,32,16,256]{3,1,0,2:T(8,128)(2,1)}, bf16[4,32,16,256]{3,1,0,2:T(8,128)(2,1)S(1)}, u32[]{:S(2)}, u32[]{:S(2)}) collective-permute-start(bf16[4,32,16,256]{3,1,0,2:T(8,128)(2,1)} %dynamic-slice_bitcast_fusion), channel_id=1, source_target_pairs={{0,1},{1,0},{2,3},{3,2},{4,5},{5,4},{6,7},{7,6},{8,9},{9,8},{10,11... | collective-permute-start | bytes 3145736 | tf_op jit(solution)/shard_map/ppermute | solution.py:61
  244.6 1.4 copy-start.3
  246.1 25.0 %collective-permute-start.8 = (bf16[32,16,256]{2,0,1:T(8,128)(2,1)S(1)}, bf16[32,16,256]{2,0,1:T(8,128)(2,1)S(1)}, u32[]{:S(2)}, u32[]{:S(2)}) collective-permute-start(bf16[32,16,256]{2,0,1:T(8,128)(2,1)S(1)} %get-tuple-element.12), channel_id=1, source_target_pairs={{0,2},{2,4},{4,6},{1,3},{3,5},{5,7},{8,10},{10,12},{12,14},{9,11},... | collective-permute-start | bytes 786440 | tf_op jit(solution)/shard_map/ppermute | solution.py:71
  265.8 11.4 %collective-permute-start.11 = (bf16[32,16,256]{2,0,1:T(8,128)(2,1)S(1)}, bf16[32,16,256]{2,0,1:T(8,128)(2,1)S(1)}, u32[]{:S(2)}, u32[]{:S(2)}) collective-permute-start(bf16[32,16,256]{2,0,1:T(8,128)(2,1)S(1)} %get-tuple-element.13), channel_id=1, source_target_pairs={{2,0},{4,2},{6,4},{3,1},{5,3},{7,5},{10,8},{12,10},{14,12},{11,9},... | collective-permute-start | bytes 786440 | tf_op jit(solution)/shard_map/ppermute | solution.py:71
  272.2 9.3 %collective-permute-start.9 = (bf16[32,16,256]{2,0,1:T(8,128)(2,1)S(1)}, bf16[32,16,256]{2,0,1:T(8,128)(2,1)S(1)}, u32[]{:S(2)}, u32[]{:S(2)}) collective-permute-start(bf16[32,16,256]{2,0,1:T(8,128)(2,1)S(1)} %fusion.26), channel_id=1, source_target_pairs={{0,2},{2,4},{4,6},{1,3},{3,5},{5,7},{8,10},{10,12},{12,14},{9,11},... | collective-permute-start | bytes 786440 | tf_op jit(solution)/shard_map/ppermute | solution.py:71
  283.6 8.8 %collective-permute-start.12 = (bf16[32,16,256]{2,0,1:T(8,128)(2,1)}, bf16[32,16,256]{2,0,1:T(8,128)(2,1)S(1)}, u32[]{:S(2)}, u32[]{:S(2)}) collective-permute-start(bf16[32,16,256]{2,0,1:T(8,128)(2,1)} %get-tuple-element.11), channel_id=1, source_target_pairs={{2,0},{4,2},{6,4},{3,1},{5,3},{7,5},{10,8},{12,10},{14,12},{11,9},... | collective-permute-start | bytes 786440 | tf_op jit(solution)/shard_map/ppermute | solution.py:71
  284.9 9.9 %collective-permute-start.10 = (bf16[32,16,256]{2,0,1:T(8,128)(2,1)S(1)}, bf16[32,16,256]{2,0,1:T(8,128)(2,1)S(1)}, u32[]{:S(2)}, u32[]{:S(2)}) collective-permute-start(bf16[32,16,256]{2,0,1:T(8,128)(2,1)S(1)} %get-tuple-element.10), channel_id=1, source_target_pairs={{0,2},{2,4},{4,6},{1,3},{3,5},{5,7},{8,10},{10,12},{12,14},{9,11},... | collective-permute-start | bytes 786440 | tf_op jit(solution)/shard_map/ppermute | solution.py:71
  293.5 7.9 %collective-permute-start.13 = (bf16[32,16,256]{2,0,1:T(8,128)(2,1)S(1)}, bf16[32,16,256]{2,0,1:T(8,128)(2,1)S(1)}, u32[]{:S(2)}, u32[]{:S(2)}) collective-permute-start(bf16[32,16,256]{2,0,1:T(8,128)(2,1)S(1)} %fusion.25), channel_id=1, source_target_pairs={{2,0},{4,2},{6,4},{3,1},{5,3},{7,5},{10,8},{12,10},{14,12},{11,9},... | collective-permute-start | bytes 786440 | tf_op jit(solution)/shard_map/ppermute | solution.py:71
Sparse Core Ops, SparseCore 0:
  74.4 63.6 all-gather.1
  175.2 60.5 reduce-scatter.1

commit v4 on v3

--- a/solution.py
+++ b/solution.py
@@ -82,8 +82,9 @@
     inner_count = block_count // group_count
     scale_factor = 1.0 / math.sqrt(row_count * replica_count)
     inputs = input_field.reshape(block_count, block_size, row_count)
-    first_full = gather_rows(first_factor)
-    second_full = lax.all_gather(second_factor, ("ylo", "core"), axis=0, tiled=True)
+    both_full = gather_rows(jnp.stack([first_factor, second_factor], axis=1))
+    first_full = both_full[:, 0]
+    second_full = both_full[:, 1]
     pre_act = jnp.einsum("bkr,kbi->bir", inputs, first_full, preferred_element_type=jnp.float32)
     activated = gelu_value(pre_act).astype(jnp.bfloat16)
     received = lax.all_to_all(activated, "blk", split_axis=1, concat_axis=0, tiled=True)

time: 314 us -> 316 us (level)
  local copies, waits for them, and re-layouts: 43.2 us -> 50.9 us
  starting transfers between devices: 95 us -> 89.5 us
  other arithmetic: 7.97 us -> 11.9 us
    all_gather x1 -> x0, waiting for transfers between devices: 61.3 us -> none  [shards(): lax.all_gather(second_factor, ('ylo', 'core'), axis=0, tiled=True)]
    all_to_all x1, waiting for transfers between devices: 0.01 us -> 43.3 us  [shards(): lax.all_to_all(activated, 'blk', split_axis=1, concat_axis=0, tiled=True)]
    ppermute x3, waiting for transfers between devices: 6.24 us -> 19.5 us  [gather_rows(): right.append(lax.ppermute(right[-1], 'ylo', line_pairs(n_ylo, 1)))]
    unnamed x23 -> x29, local copies, waits for them, and re-layouts: 7.39 us -> 15.8 us
    ppermute x6, starting transfers between devices: 33.3 us -> 25.8 us  [scatter_rows(): lax.ppermute(block.astype(jnp.bfloat16), 'ylo', line_pairs(n_ylo, step))]
    slice x0 -> x2, local copies, waits for them, and re-layouts: none -> 6.61 us  [the longest x1 4.33 us: shards(): second_full = both_full[:, 1]]
    all_to_all x1, waiting for transfers between devices: 38.2 us -> 43.6 us  [shards(): lax.all_to_all(sending, 'blk', split_axis=0, concat_axis=1, tiled=True)]
    convert_element_type x1 -> x0, local copies, waits for them, and re-layouts: 4.62 us -> none  [shards(): targets.astype(jnp.float32)]
  transfers between devices with their start and end apart: 18 -> 17, of which waited for: 12 -> 12; matrix products, arithmetic and copies ran while one was open for 15% -> 15% of each run, Pallas kernels for 0% -> 0%
where the time goes in v4:
time: 316 us; the launch traced here: 312 us
  waiting for transfers between devices  128 us (41%)
  starting transfers between devices  89.5 us (28%)
  local copies, waits for them, and re-layouts  50.9 us (16%)
  matrix products  17.3 us (5%)
  between operations  14.4 us (5%)
  other arithmetic  11.9 us (4%)
    all_to_all x1, waiting for transfers between devices, shards(): lax.all_to_all(sending, 'blk', split_axis=0, concat_axis=1, tiled=True)  43.6 us
    all_to_all x1, waiting for transfers between devices, shards(): lax.all_to_all(activated, 'blk', split_axis=1, concat_axis=0, tiled=True)  43.3 us
    ppermute x6, starting transfers between devices, scatter_rows(): lax.ppermute(block.astype(jnp.bfloat16), 'ylo', line_pairs(n_ylo, step))  25.8 us
    ppermute x3, waiting for transfers between devices, gather_rows(): right.append(lax.ppermute(right[-1], 'ylo', line_pairs(n_ylo, 1)))  19.5 us
    all_to_all x1, starting transfers between devices, shards(): lax.all_to_all(activated, 'blk', split_axis=1, concat_axis=0, tiled=True)  19.1 us
    ppermute x3, starting transfers between devices, gather_rows(): right.append(lax.ppermute(right[-1], 'ylo', line_pairs(n_ylo, 1)))  17.1 us
    ppermute x6, waiting for transfers between devices, scatter_rows(): lax.ppermute(block.astype(jnp.bfloat16), 'ylo', line_pairs(n_ylo, step))  16.9 us
    unnamed x29, local copies, waits for them, and re-layouts  15.8 us
  transfers between devices with their start and end apart: 17, of which 12 were waited for; matrix products, arithmetic and copies ran while one was open for 15% of the time, Pallas kernels for 0%

profile of v4, /device:TPU:1, one launch (start us, length us, event | category | flops | bytes accessed | tf_op | source)
XLA Modules:
  0.0 312.4 jit_solution(16937782266425382874)
XLA Ops:
  7.2 1.2 pad_maximum_fusion
  8.4 4.1 %collective-permute-start = (bf16[32,2,16,256]{3,2,1,0:T(8,128)(2,1)S(1)}, bf16[32,2,16,256]{3,2,1,0:T(8,128)(2,1)S(1)}, u32[]{:S(2)}, u32[]{:S(2)}) collective-permute-start(bf16[32,2,16,256]{3,2,1,0:T(8,128)(2,1)S(1)} %pad_maximum_fusion), channel_id=1, source_target_pairs={{0,2},{2,4},{4,6},{1,3},{3,5},{5,7},{8,10},{10,12},{12,14},{9,11},... | collective-permute-start | bytes 1572872 | tf_op jit(solution)/shard_map/ppermute | solution.py:45
  12.5 1.3 collective-permute-start.3
  13.8 6.0 %collective-permute-done = bf16[32,2,16,256]{3,2,1,0:T(8,128)(2,1)S(1)} collective-permute-done((bf16[32,2,16,256]{3,2,1,0:T(8,128)(2,1)S(1)}, bf16[32,2,16,256]{3,2,1,0:T(8,128)(2,1)S(1)}, u32[]{:S(2)}, u32[]{:S(2)}) %collective-permute-start) | collective-permute-done | bytes 524320 | tf_op jit(solution)/shard_map/ppermute | solution.py:45
  19.8 7.2 %collective-permute-start.1 = (bf16[32,2,16,256]{3,2,1,0:T(8,128)(2,1)S(1)}, bf16[32,2,16,256]{3,2,1,0:T(8,128)(2,1)}, u32[]{:S(2)}, u32[]{:S(2)}) collective-permute-start(bf16[32,2,16,256]{3,2,1,0:T(8,128)(2,1)S(1)} %collective-permute-done), channel_id=1, source_target_pairs={{0,2},{2,4},{4,6},{1,3},{3,5},{5,7},{8,10},{10,12},{12,14},{9,11},... | collective-permute-start | bytes 1572872 | tf_op jit(solution)/shard_map/ppermute | solution.py:45
  27.1 1.3 collective-permute-start.4
  28.3 6.6 %collective-permute-done.1 = bf16[32,2,16,256]{3,2,1,0:T(8,128)(2,1)} collective-permute-done((bf16[32,2,16,256]{3,2,1,0:T(8,128)(2,1)S(1)}, bf16[32,2,16,256]{3,2,1,0:T(8,128)(2,1)}, u32[]{:S(2)}, u32[]{:S(2)}) %collective-permute-start.1) | collective-permute-done | bytes 524320 | tf_op jit(solution)/shard_map/ppermute | solution.py:45
  35.0 5.8 %collective-permute-start.2 = (bf16[32,2,16,256]{3,2,1,0:T(8,128)(2,1)}, bf16[32,2,16,256]{3,2,1,0:T(8,128)(2,1)}, u32[]{:S(2)}, u32[]{:S(2)}) collective-permute-start(bf16[32,2,16,256]{3,2,1,0:T(8,128)(2,1)} %collective-permute-done.1), channel_id=1, source_target_pairs={{0,2},{2,4},{4,6},{1,3},{3,5},{5,7},{8,10},{10,12},{12,14},{9,11},... | collective-permute-start | bytes 1572872 | tf_op jit(solution)/shard_map/ppermute | solution.py:45
  40.8 1.3 collective-permute-start.5
  42.1 6.9 %collective-permute-done.2 = bf16[32,2,16,256]{3,2,1,0:T(8,128)(2,1)} collective-permute-done((bf16[32,2,16,256]{3,2,1,0:T(8,128)(2,1)}, bf16[32,2,16,256]{3,2,1,0:T(8,128)(2,1)}, u32[]{:S(2)}, u32[]{:S(2)}) %collective-permute-start.2) | collective-permute-done | bytes 524320 | tf_op jit(solution)/shard_map/ppermute | solution.py:45
  48.9 1.1 bitcast_dynamic-update-slice_fusion.6
  50.0 1.1 bitcast_dynamic-update-slice_fusion.5
  51.1 1.1 bitcast_dynamic-update-slice_fusion.4
  52.3 1.1 bitcast_dynamic-update-slice_fusion.1
  53.4 0.2 collective-permute-done.5
  53.7 1.8 copy-done.5
  55.4 1.5 constant_dynamic-slice_fusion
  56.9 5.6 %collective-permute-start.6 = (bf16[4,32,2,16,256]{4,3,2,1,0:T(8,128)(2,1)}, bf16[4,32,2,16,256]{4,3,2,1,0:T(8,128)(2,1)}, u32[]{:S(2)}, u32[]{:S(2)}) collective-permute-start(bf16[4,32,2,16,256]{4,3,2,1,0:T(8,128)(2,1)} %constant_dynamic-slice_fusion), channel_id=1, source_target_pairs={{0,1},{1,0},{2,3},{3,2},{4,5},{5,4},{6,7},{7,6},{8,9},{9,8},{10,11... | collective-permute-start | bytes 6291464 | tf_op jit(solution)/shard_map/ppermute | solution.py:49
  62.5 1.8 fusion.44
  64.3 2.3 collective-permute-done.6
  66.6 2.9 maximum_select_fusion
  69.6 2.3 fusion.37
  71.9 4.3 %copy.42 = bf16[256,1,16,256]{0,3,2,1:T(8,128)(2,1)} copy(bf16[256,1,16,256]{3,2,1,0:T(8,128)(2,1)} %get-tuple-element.8) | data formatting | bytes 4194304
  76.2 4.9 %multiply_convert_fusion = (bf16[16,256,256]{2,1,0:T(8,128)(2,1)S(1)}, f32[16,256,256]{2,1,0:T(8,128)}) fusion(bf16[16,256,256]{2,1,0:T(8,128)(2,1)S(1)} %bitcast.98, bf16[256,1,16,256]{0,3,2,1:T(8,128)(2,1)} %copy.42), kind=kOutput, calls=%fused_computation.14 | convolution fusion | flops 546308096 | bytes 10485760 | tf_op jit(solution)/shard_map/bkr,kbi->bir/dot_general | solution.py:88
  81.1 2.6 copy.27
  83.7 19.1 %all-to-all-start = ((bf16[16,256,256]{2,0,1:T(8,128)(2,1)}), bf16[16,256,256]{2,0,1:T(8,128)(2,1)}, u32[]{:S(2)}, u32[]{:S(2)}) async-start(bf16[16,256,256]{2,0,1:T(8,128)(2,1)} %copy.27), calls=%async_computation | async-start | bytes 4194304 | tf_op jit(solution)/shard_map/all_to_all | solution.py:90
  102.7 4.3 %copy.25 = bf16[256,1,16,256]{0,3,2,1:T(8,128)(2,1)} copy(bf16[256,1,16,256]{3,2,1,0:T(8,128)(2,1)} %get-tuple-element.9) | data formatting | bytes 4194304 | tf_op jit(solution)/shard_map/slice | solution.py:87
  107.0 43.3 %all-to-all-done = bf16[16,256,256]{2,0,1:T(8,128)(2,1)} async-done(((bf16[16,256,256]{2,0,1:T(8,128)(2,1)}), bf16[16,256,256]{2,0,1:T(8,128)(2,1)}, u32[]{:S(2)}, u32[]{:S(2)}) %all-to-all-start) | async-done | bytes 2097184 | tf_op jit(solution)/shard_map/all_to_all | solution.py:90
  150.4 1.9 copy.28
  152.3 1.4 copy-done.1
  153.7 0.7 fusion.8
  154.4 0.8 convert_bitcast_fusion.1
  155.3 0.4 copy-done.3
  155.8 3.0 copy.32
  158.7 13.4 %all-to-all-start.1 = ((bf16[1024,4,256]{2,1,0:T(4,128)(2,1)}), bf16[1024,4,256]{2,1,0:T(4,128)(2,1)}, u32[]{:S(2)}, u32[]{:S(2)}) async-start(bf16[1024,4,256]{2,1,0:T(4,128)(2,1)} %copy.32), calls=%async_computation.1 | async-start | bytes 4194304 | tf_op jit(solution)/shard_map/all_to_all | solution.py:115
  172.4 4.3 %convolution_convert_fusion = bf16[4,4,256,256]{3,2,1,0:T(8,128)(2,1)} fusion(bf16[4,4,256,256]{3,2,1,0:T(8,128)(2,1)} %copy-done.3, bf16[4,256,4,256]{3,1,0,2:T(8,128)(2,1)} %bitcast.100), kind=kOutput, calls=%fused_computation.25 | convolution fusion | flops 537919488 | bytes 6291456 | tf_op jit(solution)/shard_map/gcir,igjr->cigj/dot_general | solution.py:105
  176.7 4.6 %copy.37 = bf16[256,16,256]{2,1,0:T(8,128)(2,1)} copy(bf16[256,16,256]{0,2,1:T(8,128)(2,1)} %bitcast.102) | data formatting | bytes 4194304 | tf_op jit(solution)/shard_map/convert_element_type | solution.py:109
  181.2 43.6 %all-to-all-done.1 = bf16[1024,4,256]{2,1,0:T(4,128)(2,1)} async-done(((bf16[1024,4,256]{2,1,0:T(4,128)(2,1)}), bf16[1024,4,256]{2,1,0:T(4,128)(2,1)}, u32[]{:S(2)}, u32[]{:S(2)}) %all-to-all-start.1) | async-done | bytes 2097184 | tf_op jit(solution)/shard_map/all_to_all | solution.py:115
  224.8 1.9 copy.33
  226.7 0.6 convert_bitcast_fusion
  227.3 4.7 %copy.34 = f32[16,64,4,256]{3,2,1,0:T(4,128)} copy(f32[16,64,4,256]{3,0,1,2:T(8,128)S(1)} %convert_bitcast_fusion) | data formatting | bytes 8388608 | tf_op jit(solution)/shard_map/convert_element_type | solution.py:116
  232.0 5.3 %reshape.36 = f32[16,256,256]{2,1,0:T(8,128)} reshape(f32[16,64,4,256]{3,2,1,0:T(4,128)} %copy.34) | data formatting | bytes 8388608 | tf_op jit(solution)/shard_map/convert_element_type | solution.py:116
  237.4 6.5 %fusion.21 = bf16[16,256,4,2,32]{1,4,3,2,0:T(8,128)(2,1)S(1)} fusion(bf16[16,4,2,32,256]{4,3,2,1,0:T(8,128)(2,1)S(1)} %bitcast.97, f32[16,256,256]{2,1,0:T(8,128)} %reshape.36, f32[16,256,256]{2,1,0:T(8,128)} %get-tuple-element.15), kind=kOutput, calls=%fused_computation.24 | convolution fusion | flops 557842432 | bytes 12582912 | tf_op jit(solution)/shard_map/byxkr,bir->xykbi/dot_general | solution.py:119
  243.9 1.3 copy-done.6
  245.3 1.1 dynamic-slice_bitcast_fusion
  246.3 4.5 %collective-permute-start.7 = (bf16[4,32,16,256]{3,1,0,2:T(8,128)(2,1)}, bf16[4,32,16,256]{3,1,0,2:T(8,128)(2,1)S(1)}, u32[]{:S(2)}, u32[]{:S(2)}) collective-permute-start(bf16[4,32,16,256]{3,1,0,2:T(8,128)(2,1)} %dynamic-slice_bitcast_fusion), channel_id=1, source_target_pairs={{0,1},{1,0},{2,3},{3,2},{4,5},{5,4},{6,7},{7,6},{8,9},{9,8},{10,11... | collective-permute-start | bytes 3145736 | tf_op jit(solution)/shard_map/ppermute | solution.py:61
  250.8 2.5 collective-permute-done.7
  253.3 1.6 bitcast_add_fusion
  254.9 1.3 copy-done.2
  256.4 13.1 %collective-permute-start.8 = (bf16[32,16,256]{2,0,1:T(8,128)(2,1)S(1)}, bf16[32,16,256]{2,0,1:T(8,128)(2,1)S(1)}, u32[]{:S(2)}, u32[]{:S(2)}) collective-permute-start(bf16[32,16,256]{2,0,1:T(8,128)(2,1)S(1)} %get-tuple-element.12), channel_id=1, source_target_pairs={{0,2},{2,4},{4,6},{1,3},{3,5},{5,7},{8,10},{10,12},{12,14},{9,11},... | collective-permute-start | bytes 786440 | tf_op jit(solution)/shard_map/ppermute | solution.py:71
  269.5 1.3 collective-permute-start.11
  270.8 4.0 %collective-permute-done.8 = bf16[32,16,256]{2,0,1:T(8,128)(2,1)S(1)} collective-permute-done((bf16[32,16,256]{2,0,1:T(8,128)(2,1)S(1)}, bf16[32,16,256]{2,0,1:T(8,128)(2,1)S(1)}, u32[]{:S(2)}, u32[]{:S(2)}) %collective-permute-start.8) | collective-permute-done | bytes 262176 | tf_op jit(solution)/shard_map/ppermute | solution.py:71
  274.8 1.1 fusion.26
  275.9 4.1 %collective-permute-start.9 = (bf16[32,16,256]{2,0,1:T(8,128)(2,1)S(1)}, bf16[32,16,256]{2,0,1:T(8,128)(2,1)S(1)}, u32[]{:S(2)}, u32[]{:S(2)}) collective-permute-start(bf16[32,16,256]{2,0,1:T(8,128)(2,1)S(1)} %fusion.26), channel_id=1, source_target_pairs={{0,2},{2,4},{4,6},{1,3},{3,5},{5,7},{8,10},{10,12},{12,14},{9,11},... | collective-permute-start | bytes 786440 | tf_op jit(solution)/shard_map/ppermute | solution.py:71
  280.0 4.3 %collective-permute-done.9 = bf16[32,16,256]{2,0,1:T(8,128)(2,1)S(1)} collective-permute-done((bf16[32,16,256]{2,0,1:T(8,128)(2,1)S(1)}, bf16[32,16,256]{2,0,1:T(8,128)(2,1)S(1)}, u32[]{:S(2)}, u32[]{:S(2)}) %collective-permute-start.9) | collective-permute-done | bytes 262176 | tf_op jit(solution)/shard_map/ppermute | solution.py:71
  284.4 2.1 fusion.27
  286.5 1.3 collective-permute-start.12
  287.8 4.7 %collective-permute-start.10 = (bf16[32,16,256]{2,0,1:T(8,128)(2,1)S(1)}, bf16[32,16,256]{2,0,1:T(8,128)(2,1)S(1)}, u32[]{:S(2)}, u32[]{:S(2)}) collective-permute-start(bf16[32,16,256]{2,0,1:T(8,128)(2,1)S(1)} %get-tuple-element.10), channel_id=1, source_target_pairs={{0,2},{2,4},{4,6},{1,3},{3,5},{5,7},{8,10},{10,12},{12,14},{9,11},... | collective-permute-start | bytes 786440 | tf_op jit(solution)/shard_map/ppermute | solution.py:71
  292.5 2.7 collective-permute-done.12
  295.3 1.1 fusion.25
  296.4 1.3 collective-permute-start.13
  297.7 5.8 %collective-permute-done.13 = bf16[32,16,256]{2,0,1:T(8,128)(2,1)S(1)} collective-permute-done((bf16[32,16,256]{2,0,1:T(8,128)(2,1)S(1)}, bf16[32,16,256]{2,0,1:T(8,128)(2,1)S(1)}, u32[]{:S(2)}, u32[]{:S(2)}) %collective-permute-start.13) | collective-permute-done | bytes 262176 | tf_op jit(solution)/shard_map/ppermute | solution.py:71
  303.5 1.2 fusion.29
  304.7 0.9 copy.38
  (29 shorter events, 0.6 us)
Async XLA Ops:
  7.2 69.0 %copy-start = (bf16[4096,256]{1,0:T(8,128)(2,1)S(1)}, bf16[4096,256]{1,0:T(8,128)(2,1)}, u32[]{:S(2)}) copy-start(bf16[4096,256]{1,0:T(8,128)(2,1)} %param.4) | copy-start | bytes 6291460
  7.2 45.0 %copy-start.9 = (bf16[32,16,256]{2,1,0:T(8,128)(2,1)S(1)}, bf16[32,16,256]{2,1,0:T(8,128)(2,1)}, u32[]{:S(2)}) copy-start(bf16[32,16,256]{2,1,0:T(8,128)(2,1)} %param.6) | copy-start | bytes 786436
  7.2 45.0 %copy-start.8 = (bf16[32,16,256]{2,1,0:T(8,128)(2,1)S(1)}, bf16[32,16,256]{2,1,0:T(8,128)(2,1)}, u32[]{:S(2)}) copy-start(bf16[32,16,256]{2,1,0:T(8,128)(2,1)} %param.7) | copy-start | bytes 786436
  8.4 11.4 %collective-permute-start = (bf16[32,2,16,256]{3,2,1,0:T(8,128)(2,1)S(1)}, bf16[32,2,16,256]{3,2,1,0:T(8,128)(2,1)S(1)}, u32[]{:S(2)}, u32[]{:S(2)}) collective-permute-start(bf16[32,2,16,256]{3,2,1,0:T(8,128)(2,1)S(1)} %pad_maximum_fusion), channel_id=1, source_target_pairs={{0,2},{2,4},{4,6},{1,3},{3,5},{5,7},{8,10},{10,12},{12,14},{9,11},... | collective-permute-start | bytes 1572872 | tf_op jit(solution)/shard_map/ppermute | solution.py:45
  12.5 14.5 %collective-permute-start.3 = (bf16[32,2,16,256]{3,2,1,0:T(8,128)(2,1)S(1)}, bf16[32,2,16,256]{3,2,1,0:T(8,128)(2,1)S(1)}, u32[]{:S(2)}, u32[]{:S(2)}) collective-permute-start(bf16[32,2,16,256]{3,2,1,0:T(8,128)(2,1)S(1)} %pad_maximum_fusion), channel_id=1, source_target_pairs={{2,0},{4,2},{6,4},{3,1},{5,3},{7,5},{10,8},{12,10},{14,12},{11,9},... | collective-permute-start | bytes 1572872 | tf_op jit(solution)/shard_map/ppermute | solution.py:46
  19.8 7.2 %copy-start.10 = (bf16[32,2,16,256]{3,2,1,0:T(8,128)(2,1)}, bf16[32,2,16,256]{3,2,1,0:T(8,128)(2,1)S(1)}, u32[]{:S(2)}) copy-start(bf16[32,2,16,256]{3,2,1,0:T(8,128)(2,1)S(1)} %collective-permute-done) | copy-start | bytes 1572868
  19.8 15.2 %collective-permute-start.1 = (bf16[32,2,16,256]{3,2,1,0:T(8,128)(2,1)S(1)}, bf16[32,2,16,256]{3,2,1,0:T(8,128)(2,1)}, u32[]{:S(2)}, u32[]{:S(2)}) collective-permute-start(bf16[32,2,16,256]{3,2,1,0:T(8,128)(2,1)S(1)} %collective-permute-done), channel_id=1, source_target_pairs={{0,2},{2,4},{4,6},{1,3},{3,5},{5,7},{8,10},{10,12},{12,14},{9,11},... | collective-permute-start | bytes 1572872 | tf_op jit(solution)/shard_map/ppermute | solution.py:45
  27.1 13.7 %collective-permute-start.4 = (bf16[32,2,16,256]{3,2,1,0:T(8,128)(2,1)S(1)}, bf16[32,2,16,256]{3,2,1,0:T(8,128)(2,1)}, u32[]{:S(2)}, u32[]{:S(2)}) collective-permute-start(bf16[32,2,16,256]{3,2,1,0:T(8,128)(2,1)S(1)} %collective-permute-done.3), channel_id=1, source_target_pairs={{2,0},{4,2},{6,4},{3,1},{5,3},{7,5},{10,8},{12,10},{14,12},{11,9},... | collective-permute-start | bytes 1572872 | tf_op jit(solution)/shard_map/ppermute | solution.py:46
  35.0 13.9 %collective-permute-start.2 = (bf16[32,2,16,256]{3,2,1,0:T(8,128)(2,1)}, bf16[32,2,16,256]{3,2,1,0:T(8,128)(2,1)}, u32[]{:S(2)}, u32[]{:S(2)}) collective-permute-start(bf16[32,2,16,256]{3,2,1,0:T(8,128)(2,1)} %collective-permute-done.1), channel_id=1, source_target_pairs={{0,2},{2,4},{4,6},{1,3},{3,5},{5,7},{8,10},{10,12},{12,14},{9,11},... | collective-permute-start | bytes 1572872 | tf_op jit(solution)/shard_map/ppermute | solution.py:45
  40.8 12.8 %collective-permute-start.5 = (bf16[32,2,16,256]{3,2,1,0:T(8,128)(2,1)}, bf16[32,2,16,256]{3,2,1,0:T(8,128)(2,1)S(1)}, u32[]{:S(2)}, u32[]{:S(2)}) collective-permute-start(bf16[32,2,16,256]{3,2,1,0:T(8,128)(2,1)} %collective-permute-done.4), channel_id=1, source_target_pairs={{2,0},{4,2},{6,4},{3,1},{5,3},{7,5},{10,8},{12,10},{14,12},{11,9},... | collective-permute-start | bytes 1572872 | tf_op jit(solution)/shard_map/ppermute | solution.py:46
  53.7 1.8 copy-start.5
  56.9 9.7 %collective-permute-start.6 = (bf16[4,32,2,16,256]{4,3,2,1,0:T(8,128)(2,1)}, bf16[4,32,2,16,256]{4,3,2,1,0:T(8,128)(2,1)}, u32[]{:S(2)}, u32[]{:S(2)}) collective-permute-start(bf16[4,32,2,16,256]{4,3,2,1,0:T(8,128)(2,1)} %constant_dynamic-slice_fusion), channel_id=1, source_target_pairs={{0,1},{1,0},{2,3},{3,2},{4,5},{5,4},{6,7},{7,6},{8,9},{9,8},{10,11... | collective-permute-start | bytes 6291464 | tf_op jit(solution)/shard_map/ppermute | solution.py:49
  83.7 66.7 %all-to-all-start = ((bf16[16,256,256]{2,0,1:T(8,128)(2,1)}), bf16[16,256,256]{2,0,1:T(8,128)(2,1)}, u32[]{:S(2)}, u32[]{:S(2)}) async-start(bf16[16,256,256]{2,0,1:T(8,128)(2,1)} %copy.27), calls=%async_computation | async-start | bytes 4194304 | tf_op jit(solution)/shard_map/all_to_all | solution.py:90
  150.4 3.3 %copy-start.4 = (bf16[256,1,16,256]{0,3,2,1:T(8,128)(2,1)S(1)}, bf16[256,1,16,256]{0,3,2,1:T(8,128)(2,1)}, u32[]{:S(2)}) copy-start(bf16[256,1,16,256]{0,3,2,1:T(8,128)(2,1)} %copy.25) | copy-start | bytes 6291460
  150.4 3.3 %copy-start.7 = (bf16[4096,256]{1,0:T(8,128)(2,1)S(1)}, bf16[4096,256]{1,0:T(8,128)(2,1)}, u32[]{:S(2)}) copy-start(bf16[4096,256]{1,0:T(8,128)(2,1)} %param.5) | copy-start | bytes 6291460
  152.3 1.4 copy-start.1
  154.4 1.4 copy-start.3
  158.7 66.1 %all-to-all-start.1 = ((bf16[1024,4,256]{2,1,0:T(4,128)(2,1)}), bf16[1024,4,256]{2,1,0:T(4,128)(2,1)}, u32[]{:S(2)}, u32[]{:S(2)}) async-start(bf16[1024,4,256]{2,1,0:T(4,128)(2,1)} %copy.32), calls=%async_computation.1 | async-start | bytes 4194304 | tf_op jit(solution)/shard_map/all_to_all | solution.py:115
  172.1 133.4 %reduce-scatter.2.cloned.1.call-start = ((), (), s32[]{:S(2)}) async-start(), calls=%async_computation.3 | async-start | bytes 2359296 | tf_op jit(solution)/shard_map/reduce_scatter | solution.py:108
  243.9 1.4 copy-start.6
  246.3 7.0 %collective-permute-start.7 = (bf16[4,32,16,256]{3,1,0,2:T(8,128)(2,1)}, bf16[4,32,16,256]{3,1,0,2:T(8,128)(2,1)S(1)}, u32[]{:S(2)}, u32[]{:S(2)}) collective-permute-start(bf16[4,32,16,256]{3,1,0,2:T(8,128)(2,1)} %dynamic-slice_bitcast_fusion), channel_id=1, source_target_pairs={{0,1},{1,0},{2,3},{3,2},{4,5},{5,4},{6,7},{7,6},{8,9},{9,8},{10,11... | collective-permute-start | bytes 3145736 | tf_op jit(solution)/shard_map/ppermute | solution.py:61
  254.9 1.4 copy-start.2
  256.4 18.4 %collective-permute-start.8 = (bf16[32,16,256]{2,0,1:T(8,128)(2,1)S(1)}, bf16[32,16,256]{2,0,1:T(8,128)(2,1)S(1)}, u32[]{:S(2)}, u32[]{:S(2)}) collective-permute-start(bf16[32,16,256]{2,0,1:T(8,128)(2,1)S(1)} %get-tuple-element.12), channel_id=1, source_target_pairs={{0,2},{2,4},{4,6},{1,3},{3,5},{5,7},{8,10},{10,12},{12,14},{9,11},... | collective-permute-start | bytes 786440 | tf_op jit(solution)/shard_map/ppermute | solution.py:71
  269.5 10.5 %collective-permute-start.11 = (bf16[32,16,256]{2,0,1:T(8,128)(2,1)S(1)}, bf16[32,16,256]{2,0,1:T(8,128)(2,1)S(1)}, u32[]{:S(2)}, u32[]{:S(2)}) collective-permute-start(bf16[32,16,256]{2,0,1:T(8,128)(2,1)S(1)} %get-tuple-element.13), channel_id=1, source_target_pairs={{2,0},{4,2},{6,4},{3,1},{5,3},{7,5},{10,8},{12,10},{14,12},{11,9},... | collective-permute-start | bytes 786440 | tf_op jit(solution)/shard_map/ppermute | solution.py:71
  275.9 8.5 %collective-permute-start.9 = (bf16[32,16,256]{2,0,1:T(8,128)(2,1)S(1)}, bf16[32,16,256]{2,0,1:T(8,128)(2,1)S(1)}, u32[]{:S(2)}, u32[]{:S(2)}) collective-permute-start(bf16[32,16,256]{2,0,1:T(8,128)(2,1)S(1)} %fusion.26), channel_id=1, source_target_pairs={{0,2},{2,4},{4,6},{1,3},{3,5},{5,7},{8,10},{10,12},{12,14},{9,11},... | collective-permute-start | bytes 786440 | tf_op jit(solution)/shard_map/ppermute | solution.py:71
  286.5 8.8 %collective-permute-start.12 = (bf16[32,16,256]{2,0,1:T(8,128)(2,1)}, bf16[32,16,256]{2,0,1:T(8,128)(2,1)S(1)}, u32[]{:S(2)}, u32[]{:S(2)}) collective-permute-start(bf16[32,16,256]{2,0,1:T(8,128)(2,1)} %get-tuple-element.11), channel_id=1, source_target_pairs={{2,0},{4,2},{6,4},{3,1},{5,3},{7,5},{10,8},{12,10},{14,12},{11,9},... | collective-permute-start | bytes 786440 | tf_op jit(solution)/shard_map/ppermute | solution.py:71
  287.8 9.9 %collective-permute-start.10 = (bf16[32,16,256]{2,0,1:T(8,128)(2,1)S(1)}, bf16[32,16,256]{2,0,1:T(8,128)(2,1)S(1)}, u32[]{:S(2)}, u32[]{:S(2)}) collective-permute-start(bf16[32,16,256]{2,0,1:T(8,128)(2,1)S(1)} %get-tuple-element.10), channel_id=1, source_target_pairs={{0,2},{2,4},{4,6},{1,3},{3,5},{5,7},{8,10},{10,12},{12,14},{9,11},... | collective-permute-start | bytes 786440 | tf_op jit(solution)/shard_map/ppermute | solution.py:71
  296.4 7.1 %collective-permute-start.13 = (bf16[32,16,256]{2,0,1:T(8,128)(2,1)S(1)}, bf16[32,16,256]{2,0,1:T(8,128)(2,1)S(1)}, u32[]{:S(2)}, u32[]{:S(2)}) collective-permute-start(bf16[32,16,256]{2,0,1:T(8,128)(2,1)S(1)} %fusion.25), channel_id=1, source_target_pairs={{2,0},{4,2},{6,4},{3,1},{5,3},{7,5},{10,8},{12,10},{14,12},{11,9},... | collective-permute-start | bytes 786440 | tf_op jit(solution)/shard_map/ppermute | solution.py:71
Sparse Core Ops, SparseCore 0:
  181.4 64.3 reduce-scatter.1

commit v5 on v3

--- a/solution.py
+++ b/solution.py
@@ -77,47 +77,46 @@
     block_count = first_factor.shape[1]
     block_size = first_factor.shape[2]
     row_count = input_field.shape[1]
+    dp = ("ylo", "core")
     replica_count = lax.axis_size("ylo") * lax.axis_size("core")
+    blk_count = lax.axis_size("blk")
     group_count = NB // BS
     inner_count = block_count // group_count
     scale_factor = 1.0 / math.sqrt(row_count * replica_count)
     inputs = input_field.reshape(block_count, block_size, row_count)
     first_full = gather_rows(first_factor)
-    second_full = lax.all_gather(second_factor, ("ylo", "core"), axis=0, tiled=True)
+    second_full = lax.all_gather(second_factor, dp, axis=0, tiled=True)
     pre_act = jnp.einsum("bkr,kbi->bir", inputs, first_full, preferred_element_type=jnp.float32)
-    activated = gelu_value(pre_act).astype(jnp.bfloat16)
-    received = lax.all_to_all(activated, "blk", split_axis=1, concat_axis=0, tiled=True)
-    permuted = received.reshape(group_count, block_size, inner_count, row_count)
-    targets = target_field.reshape(inner_count, group_count, block_size, row_count)
-    count = second_full.shape[0]
-    split_part = second_full.reshape(count, inner_count, group_count, block_size)
+    pre_split = pre_act.reshape(block_count, blk_count, inner_count, row_count)
+    activated = gelu_value(pre_split).astype(jnp.bfloat16)
+    slope = jnp.transpose(gelu_slope(pre_split), (2, 1, 0, 3))
+    sending = jnp.transpose(activated, (2, 1, 0, 3))
+    received = lax.all_to_all(sending, "blk", split_axis=1, concat_axis=1, tiled=True)
+    permuted = received.reshape(block_count, block_size, row_count)
+    targets = target_field.reshape(block_count, block_size, row_count)
+    second_t = jnp.transpose(second_full, (1, 0, 2))
     predicted = jnp.einsum(
-        "gcir,cigj->igjr", permuted, split_part, preferred_element_type=jnp.float32
+        "qcj,qcr->qjr", second_t, permuted, preferred_element_type=jnp.float32
     )
     residual = ((predicted - targets.astype(jnp.float32)) * scale_factor).astype(jnp.bfloat16)
     permuted_grad = jnp.einsum(
-        "cigj,igjr->gcir", split_part, residual, preferred_element_type=jnp.float32
+        "qcj,qjr->qcr", second_t, residual, preferred_element_type=jnp.float32
     ).astype(jnp.bfloat16)
-    n_core = lax.axis_size("core")
-    n_ylo = lax.axis_size("ylo")
-    kk = block_size // (n_core * n_ylo)
-    term = jnp.einsum(
-        "gcir,igjr->cigj", permuted, residual, preferred_element_type=jnp.float32
+    term = jnp.einsum("qcr,qjr->cqj", permuted, residual, preferred_element_type=jnp.float32)
+    second_out = lax.psum_scatter(
+        term.astype(jnp.bfloat16), dp, scatter_dimension=0, tiled=True
     )
-    second_out = lax.psum_scatter(
-        term.reshape(count, block_count, block_size).astype(jnp.bfloat16),
-        ("ylo", "core"),
+    back = permuted_grad.reshape(inner_count, blk_count, block_count, row_count)
+    activated_grad = lax.all_to_all(back, "blk", split_axis=1, concat_axis=1, tiled=True)
+    pre_grad = (activated_grad.astype(jnp.float32) * slope).astype(jnp.bfloat16)
+    pre_grad = jnp.transpose(pre_grad, (2, 1, 0, 3)).reshape(block_count, block_size, row_count)
+    first_sum = lax.psum_scatter(
+        jnp.einsum("bkr,bir->kbi", inputs, pre_grad, preferred_element_type=jnp.float32).astype(
+            jnp.bfloat16
+        ),
+        dp,
         scatter_dimension=0,
         tiled=True,
-    )
-    sending = permuted_grad.reshape(group_count * block_size, inner_count, row_count)
-    activated_grad = lax.all_to_all(sending, "blk", split_axis=0, concat_axis=1, tiled=True)
-    pre_grad = (activated_grad.astype(jnp.float32) * gelu_slope(pre_act)).astype(jnp.bfloat16)
-    inputs_cm = inputs.reshape(block_count, n_ylo, n_core, kk, row_count)
-    first_sum = scatter_rows(
-        jnp.einsum(
-            "byxkr,bir->xykbi", inputs_cm, pre_grad, preferred_element_type=jnp.float32
-        ).astype(jnp.bfloat16)
     )
     return (first_sum, second_out)
 

time: 314 us -> 287 us (0.914)
  starting transfers between devices: 95 us -> 56.9 us
  waiting for transfers between devices: 131 us -> 164 us
  local copies, waits for them, and re-layouts: 43.2 us -> 28.6 us
  matrix products: 18.4 us -> 13.3 us
    reduce_scatter x1 -> x2, waiting for transfers between devices: 0.01 us -> 57.7 us  [the longest x1 45.9 us: shards(): lax.psum_scatter(jnp.einsum('bkr,bir->kbi', inputs, pre_grad, preferred_e...]
    all_gather x1, waiting for transfers between devices: 61.3 us -> 9.38 us  [shards(): second_full = lax.all_gather(second_factor, dp, axis=0, tiled=True)]
    all_to_all x2, waiting for transfers between devices: 38.2 us -> 86.3 us  [the longest x1 48 us: shards(): lax.all_to_all(sending, 'blk', split_axis=1, concat_axis=1, tiled=True)]
    ppermute x7 -> x0, starting transfers between devices: 38.9 us -> none  [the longest x6 33.3 us: scatter_rows(): lax.ppermute(block.astype(jnp.bfloat16), 'ylo', line_pairs(n_ylo, step))]
    ppermute x7 -> x0, waiting for transfers between devices: 20.1 us -> none  [the longest x6 17.6 us: scatter_rows(): lax.ppermute(block.astype(jnp.bfloat16), 'ylo', line_pairs(n_ylo, step))]
    convert_element_type x6 -> x2, local copies, waits for them, and re-layouts: 17.3 us -> 9.15 us  [the longest x1 4.6 us: shards(): term.astype(jnp.bfloat16)]
    all_gather x1 -> x0, local copies, waits for them, and re-layouts: 3.66 us -> none  [shards(): lax.all_gather(second_factor, ('ylo', 'core'), axis=0, tiled=True)]
    unnamed x23 -> x19, local copies, waits for them, and re-layouts: 7.39 us -> 5.64 us
  transfers between devices with their start and end apart: 18 -> 12, of which waited for: 12 -> 10; matrix products, arithmetic and copies ran while one was open for 15% -> 11% of each run, Pallas kernels for 0% -> 0%
where the time goes in v5:
time: 287 us; the launch traced here: 285 us
  waiting for transfers between devices  164 us (57%)
  starting transfers between devices  56.9 us (20%)
  local copies, waits for them, and re-layouts  28.6 us (10%)
  between operations  14 us (5%)
  matrix products  13.3 us (5%)
  other arithmetic  7.65 us (3%)
    all_to_all x1, waiting for transfers between devices, shards(): lax.all_to_all(sending, 'blk', split_axis=1, concat_axis=1, tiled=True)  48 us
    reduce_scatter x1, waiting for transfers between devices, shards(): lax.psum_scatter(jnp.einsum('bkr,bir->kbi', inputs, pre_grad, preferred_e...  45.9 us
    all_to_all x1, waiting for transfers between devices, shards(): lax.all_to_all(back, 'blk', split_axis=1, concat_axis=1, tiled=True)  38.2 us
    all_to_all x1, starting transfers between devices, shards(): lax.all_to_all(sending, 'blk', split_axis=1, concat_axis=1, tiled=True)  17.6 us
    all_to_all x1, starting transfers between devices, shards(): lax.all_to_all(back, 'blk', split_axis=1, concat_axis=1, tiled=True)  14.8 us
    ppermute x3, starting transfers between devices, gather_rows(): right.append(lax.ppermute(right[-1], 'ylo', line_pairs(n_ylo, 1)))  13.8 us
    reduce_scatter x1, waiting for transfers between devices, shards(): lax.psum_scatter(term.astype(jnp.bfloat16), dp, scatter_dimension=0, tile...  11.8 us
    all_gather x1, waiting for transfers between devices, shards(): second_full = lax.all_gather(second_factor, dp, axis=0, tiled=True)  9.38 us
  transfers between devices with their start and end apart: 12, of which 10 were waited for; matrix products, arithmetic and copies ran while one was open for 11% of the time, Pallas kernels for 0%

profile of v5, /device:TPU:1, one launch (start us, length us, event | category | flops | bytes accessed | tf_op | source)
XLA Modules:
  0.0 284.8 jit_solution(2704254259740991413)
XLA Ops:
  7.2 0.0 copy-start
  7.2 4.2 %collective-permute-start = (bf16[32,16,256]{2,1,0:T(8,128)(2,1)}, bf16[32,16,256]{2,1,0:T(8,128)(2,1)S(1)}, u32[]{:S(2)}, u32[]{:S(2)}) collective-permute-start(bf16[32,16,256]{2,1,0:T(8,128)(2,1)} %param.6), channel_id=1, source_target_pairs={{0,2},{2,4},{4,6},{1,3},{3,5},{5,7},{8,10},{10,12},{12,14},{9,11},... | collective-permute-start | bytes 786440 | tf_op jit(solution)/shard_map/ppermute | solution.py:45
  11.4 1.3 collective-permute-start.3
  12.7 2.3 collective-permute-done
  15.0 4.9 %collective-permute-start.1 = (bf16[32,16,256]{2,1,0:T(8,128)(2,1)S(1)}, bf16[32,16,256]{2,1,0:T(8,128)(2,1)S(1)}, u32[]{:S(2)}, u32[]{:S(2)}) collective-permute-start(bf16[32,16,256]{2,1,0:T(8,128)(2,1)S(1)} %collective-permute-done), channel_id=1, source_target_pairs={{0,2},{2,4},{4,6},{1,3},{3,5},{5,7},{8,10},{10,12},{12,14},{9,11},... | collective-permute-start | bytes 786440 | tf_op jit(solution)/shard_map/ppermute | solution.py:45
  19.8 0.0 collective-permute-done.3
  19.8 1.3 collective-permute-start.4
  21.1 2.0 collective-permute-done.1
  23.1 4.7 %collective-permute-start.2 = (bf16[32,16,256]{2,1,0:T(8,128)(2,1)S(1)}, bf16[32,16,256]{2,1,0:T(8,128)(2,1)S(1)}, u32[]{:S(2)}, u32[]{:S(2)}) collective-permute-start(bf16[32,16,256]{2,1,0:T(8,128)(2,1)S(1)} %collective-permute-done.1), channel_id=1, source_target_pairs={{0,2},{2,4},{4,6},{1,3},{3,5},{5,7},{8,10},{10,12},{12,14},{9,11},... | collective-permute-start | bytes 786440 | tf_op jit(solution)/shard_map/ppermute | solution.py:45
  27.9 0.0 collective-permute-done.4
  27.9 1.3 collective-permute-start.5
  29.2 2.0 collective-permute-done.2
  31.2 1.0 bitcast_dynamic-update-slice_fusion.3
  32.3 3.5 %collective-permute-done.5 = bf16[32,16,256]{2,1,0:T(8,128)(2,1)S(1)} collective-permute-done((bf16[32,16,256]{2,1,0:T(8,128)(2,1)S(1)}, bf16[32,16,256]{2,1,0:T(8,128)(2,1)S(1)}, u32[]{:S(2)}, u32[]{:S(2)}) %collective-permute-start.5) | collective-permute-done | bytes 262176 | tf_op jit(solution)/shard_map/ppermute | solution.py:46
  35.8 0.0 copy-start.4
  35.8 1.2 copy-done.4
  37.0 1.1 constant_dynamic-slice_fusion
  38.1 6.7 %collective-permute-start.6 = (bf16[4,32,16,256]{3,2,1,0:T(8,128)(2,1)}, bf16[4,32,16,256]{3,2,1,0:T(8,128)(2,1)S(1)}, u32[]{:S(2)}, u32[]{:S(2)}) collective-permute-start(bf16[4,32,16,256]{3,2,1,0:T(8,128)(2,1)} %constant_dynamic-slice_fusion), channel_id=1, source_target_pairs={{0,1},{1,0},{2,3},{3,2},{4,5},{5,4},{6,7},{7,6},{8,9},{9,8},{10,11... | collective-permute-start | bytes 3145736 | tf_op jit(solution)/shard_map/ppermute | solution.py:49
  44.7 1.3 fusion.29
  46.1 1.2 collective-permute-done.6
  47.2 0.3 maximum_select_fusion
  47.5 0.0 copy-done
  47.5 1.5 fusion.15
  49.0 2.4 copy.66
  51.5 0.0 copy-start.1
  51.5 1.9 copy-done.1
  53.4 2.7 fusion.17
  56.1 0.0 copy-start.5
  56.1 17.6 %all-to-all-start = ((bf16[4,64,16,256]{3,2,0,1:T(8,128)(2,1)}), bf16[4,64,16,256]{3,2,0,1:T(8,128)(2,1)}, u32[]{:S(2)}, u32[]{:S(2)}) async-start(bf16[4,64,16,256]{3,2,0,1:T(8,128)(2,1)} %fusion.17), calls=%async_computation | async-start | bytes 4194304 | tf_op jit(solution)/shard_map/all_to_all | solution.py:94
  73.7 0.0 all-gather.2.cloned.1.call-start
  73.7 0.0 copy-done.5
  73.7 0.8 copy.52
  74.5 0.0 all-gather.2.cloned.1.call-update
  74.5 4.2 %copy.54 = f32[16,256,256]{1,2,0:T(8,128)} copy(bf16[16,256,256]{2,1,0:T(8,128)(2,1)} %bitcast.69) | data formatting | bytes 6291456 | tf_op jit(solution)/shard_map/convert_element_type | solution.py:101
  78.7 48.0 %all-to-all-done = bf16[4,64,16,256]{3,2,0,1:T(8,128)(2,1)} async-done(((bf16[4,64,16,256]{3,2,0,1:T(8,128)(2,1)}), bf16[4,64,16,256]{3,2,0,1:T(8,128)(2,1)}, u32[]{:S(2)}, u32[]{:S(2)}) %all-to-all-start) | async-done | bytes 2097184 | tf_op jit(solution)/shard_map/all_to_all | solution.py:94
  126.7 3.2 %copy.51 = bf16[4,64,16,256]{3,2,1,0:T(8,128)(2,1)} copy(bf16[4,64,16,256]{3,2,0,1:T(8,128)(2,1)} %all-to-all-done) | data formatting | bytes 4194304 | tf_op jit(solution)/shard_map/all_to_all | solution.py:94
  129.9 9.4 %all-gather.2.cloned.1.call-done = bf16[256,16,256]{2,0,1:T(8,128)(2,1)} async-done(((bf16[32,16,256]{2,0,1:T(8,128)(2,1)}), bf16[256,16,256]{2,0,1:T(8,128)(2,1)}) %all-gather.2.cloned.1.call-update) | async-done | bytes 2097168 | tf_op jit(solution)/shard_map/all_gather | solution.py:88
  139.3 0.0 copy-start.3
  139.3 4.5 %fusion.9 = bf16[16,256,256]{1,2,0:T(8,128)(2,1)S(1)} fusion(f32[16,256,256]{1,2,0:T(8,128)} %copy.54, bf16[16,256,256]{2,1,0:T(8,128)(2,1)} %bitcast.64, bf16[256,16,256]{2,0,1:T(8,128)(2,1)} %all-gather.2.cloned.1.call-done), kind=kOutput, calls=%fused_computation.12 | convolution fusion | flops 540016640 | bytes 10485760 | tf_op jit(solution)/shard_map/qcj,qcr->qjr/dot_general | solution.py:98
  143.8 0.0 copy-done.3
  143.8 0.0 copy-start.2
  143.8 0.7 fusion.20
  144.6 0.6 copy-done.2
  145.2 1.6 copy.56
  146.8 14.8 %all-to-all-start.1 = ((bf16[4,64,16,256]{3,2,0,1:T(8,128)(2,1)}), bf16[4,64,16,256]{3,2,0,1:T(8,128)(2,1)}, u32[]{:S(2)}, u32[]{:S(2)}) async-start(bf16[4,64,16,256]{3,2,0,1:T(8,128)(2,1)} %copy.56), calls=%async_computation.1 | async-start | bytes 4194304 | tf_op jit(solution)/shard_map/all_to_all | solution.py:110
  161.6 0.2 reduce-scatter.5.cloned.1.call-start
  161.8 4.3 %convert_bitcast_fusion = bf16[256,16,256]{0,2,1:T(8,128)(2,1)} fusion(bf16[16,256,256]{1,2,0:T(8,128)(2,1)} %copy-done.2, bf16[16,256,256]{2,1,0:T(8,128)(2,1)} %bitcast.65), kind=kOutput, calls=%fused_computation.22 | convolution fusion | flops 537919488 | bytes 6291456 | tf_op jit(solution)/shard_map/qcr,qjr->cqj/dot_general | solution.py:105
  166.1 4.6 %copy.62 = bf16[256,16,256]{2,1,0:T(8,128)(2,1)} copy(bf16[256,16,256]{0,2,1:T(8,128)(2,1)} %convert_bitcast_fusion) | data formatting | bytes 4194304 | tf_op jit(solution)/shard_map/convert_element_type | solution.py:107
  170.7 0.0 reduce-scatter.5.cloned.1.call-update
  170.8 0.0 reduce-scatter.3.cloned.1.call-start
  170.8 38.2 %all-to-all-done.1 = bf16[4,64,16,256]{3,2,0,1:T(8,128)(2,1)} async-done(((bf16[4,64,16,256]{3,2,0,1:T(8,128)(2,1)}), bf16[4,64,16,256]{3,2,0,1:T(8,128)(2,1)}, u32[]{:S(2)}, u32[]{:S(2)}) %all-to-all-start.1) | async-done | bytes 2097184 | tf_op jit(solution)/shard_map/all_to_all | solution.py:110
  209.0 4.7 %fusion.7 = bf16[4,64,16,256]{3,2,0,1:T(8,128)(2,1)S(1)} fusion(f32[16,64,4,256]{3,0,2,1:T(8,128)} %bitcast.63, bf16[4,64,16,256]{3,2,0,1:T(8,128)(2,1)} %all-to-all-done.1), kind=kLoop, calls=%fused_computation.9 | loop fusion | flops 20971520 | bytes 8388608 | tf_op jit(solution)/shard_map/convert_element_type | solution.py:111
  213.7 2.2 convert_bitcast_fusion.1
  216.0 4.6 %copy.60 = bf16[256,16,256]{2,1,0:T(8,128)(2,1)} copy(bf16[256,16,256]{0,2,1:T(8,128)(2,1)} %convert_bitcast_fusion.1) | data formatting | bytes 4194304 | tf_op jit(solution)/shard_map/convert_element_type | solution.py:114
  220.5 0.0 reduce-scatter.3.cloned.1.call-update
  220.5 11.8 %reduce-scatter.5.cloned.1.call-done = bf16[32,16,256]{2,1,0:T(8,128)(2,1)} async-done(((bf16[256,16,256]{2,1,0:T(8,128)(2,1)}), bf16[32,16,256]{2,1,0:T(8,128)(2,1)}) %reduce-scatter.5.cloned.1.call-update) | async-done | bytes 262160 | tf_op jit(solution)/shard_map/reduce_scatter | solution.py:106
  232.3 45.9 %reduce-scatter.3.cloned.1.call-done = bf16[32,16,256]{2,1,0:T(8,128)(2,1)} async-done(((bf16[256,16,256]{2,1,0:T(8,128)(2,1)}), bf16[32,16,256]{2,1,0:T(8,128)(2,1)}) %reduce-scatter.3.cloned.1.call-update) | async-done | bytes 262160 | tf_op jit(solution)/shard_map/reduce_scatter | solution.py:113
  (6 shorter events, 0.1 us)
Async XLA Ops:
  7.2 40.4 %copy-start = (bf16[4096,256]{1,0:T(8,128)(2,1)S(1)}, bf16[4096,256]{1,0:T(8,128)(2,1)}, u32[]{:S(2)}) copy-start(bf16[4096,256]{1,0:T(8,128)(2,1)} %param.4) | copy-start | bytes 6291460
  7.2 7.8 %collective-permute-start = (bf16[32,16,256]{2,1,0:T(8,128)(2,1)}, bf16[32,16,256]{2,1,0:T(8,128)(2,1)S(1)}, u32[]{:S(2)}, u32[]{:S(2)}) collective-permute-start(bf16[32,16,256]{2,1,0:T(8,128)(2,1)} %param.6), channel_id=1, source_target_pairs={{0,2},{2,4},{4,6},{1,3},{3,5},{5,7},{8,10},{10,12},{12,14},{9,11},... | collective-permute-start | bytes 786440 | tf_op jit(solution)/shard_map/ppermute | solution.py:45
  11.4 8.5 %collective-permute-start.3 = (bf16[32,16,256]{2,1,0:T(8,128)(2,1)}, bf16[32,16,256]{2,1,0:T(8,128)(2,1)S(1)}, u32[]{:S(2)}, u32[]{:S(2)}) collective-permute-start(bf16[32,16,256]{2,1,0:T(8,128)(2,1)} %param.6), channel_id=1, source_target_pairs={{2,0},{4,2},{6,4},{3,1},{5,3},{7,5},{10,8},{12,10},{14,12},{11,9},... | collective-permute-start | bytes 786440 | tf_op jit(solution)/shard_map/ppermute | solution.py:46
  15.0 8.2 %collective-permute-start.1 = (bf16[32,16,256]{2,1,0:T(8,128)(2,1)S(1)}, bf16[32,16,256]{2,1,0:T(8,128)(2,1)S(1)}, u32[]{:S(2)}, u32[]{:S(2)}) collective-permute-start(bf16[32,16,256]{2,1,0:T(8,128)(2,1)S(1)} %collective-permute-done), channel_id=1, source_target_pairs={{0,2},{2,4},{4,6},{1,3},{3,5},{5,7},{8,10},{10,12},{12,14},{9,11},... | collective-permute-start | bytes 786440 | tf_op jit(solution)/shard_map/ppermute | solution.py:45
  19.8 8.0 %collective-permute-start.4 = (bf16[32,16,256]{2,1,0:T(8,128)(2,1)S(1)}, bf16[32,16,256]{2,1,0:T(8,128)(2,1)S(1)}, u32[]{:S(2)}, u32[]{:S(2)}) collective-permute-start(bf16[32,16,256]{2,1,0:T(8,128)(2,1)S(1)} %collective-permute-done.3), channel_id=1, source_target_pairs={{2,0},{4,2},{6,4},{3,1},{5,3},{7,5},{10,8},{12,10},{14,12},{11,9},... | collective-permute-start | bytes 786440 | tf_op jit(solution)/shard_map/ppermute | solution.py:46
  23.1 8.0 %collective-permute-start.2 = (bf16[32,16,256]{2,1,0:T(8,128)(2,1)S(1)}, bf16[32,16,256]{2,1,0:T(8,128)(2,1)S(1)}, u32[]{:S(2)}, u32[]{:S(2)}) collective-permute-start(bf16[32,16,256]{2,1,0:T(8,128)(2,1)S(1)} %collective-permute-done.1), channel_id=1, source_target_pairs={{0,2},{2,4},{4,6},{1,3},{3,5},{5,7},{8,10},{10,12},{12,14},{9,11},... | collective-permute-start | bytes 786440 | tf_op jit(solution)/shard_map/ppermute | solution.py:45
  27.9 7.9 %collective-permute-start.5 = (bf16[32,16,256]{2,1,0:T(8,128)(2,1)S(1)}, bf16[32,16,256]{2,1,0:T(8,128)(2,1)S(1)}, u32[]{:S(2)}, u32[]{:S(2)}) collective-permute-start(bf16[32,16,256]{2,1,0:T(8,128)(2,1)S(1)} %collective-permute-done.4), channel_id=1, source_target_pairs={{2,0},{4,2},{6,4},{3,1},{5,3},{7,5},{10,8},{12,10},{14,12},{11,9},... | collective-permute-start | bytes 786440 | tf_op jit(solution)/shard_map/ppermute | solution.py:46
  35.8 1.2 copy-start.4
  38.1 9.2 %collective-permute-start.6 = (bf16[4,32,16,256]{3,2,1,0:T(8,128)(2,1)}, bf16[4,32,16,256]{3,2,1,0:T(8,128)(2,1)S(1)}, u32[]{:S(2)}, u32[]{:S(2)}) collective-permute-start(bf16[4,32,16,256]{3,2,1,0:T(8,128)(2,1)} %constant_dynamic-slice_fusion), channel_id=1, source_target_pairs={{0,1},{1,0},{2,3},{3,2},{4,5},{5,4},{6,7},{7,6},{8,9},{9,8},{10,11... | collective-permute-start | bytes 3145736 | tf_op jit(solution)/shard_map/ppermute | solution.py:49
  51.5 1.9 copy-start.1
  56.1 17.6 %copy-start.5 = (bf16[32,16,256]{2,1,0:T(8,128)(2,1)S(1)}, bf16[32,16,256]{2,1,0:T(8,128)(2,1)}, u32[]{:S(2)}) copy-start(bf16[32,16,256]{2,1,0:T(8,128)(2,1)} %param.7) | copy-start | bytes 786436
  56.1 70.6 %all-to-all-start = ((bf16[4,64,16,256]{3,2,0,1:T(8,128)(2,1)}), bf16[4,64,16,256]{3,2,0,1:T(8,128)(2,1)}, u32[]{:S(2)}, u32[]{:S(2)}) async-start(bf16[4,64,16,256]{3,2,0,1:T(8,128)(2,1)} %fusion.17), calls=%async_computation | async-start | bytes 4194304 | tf_op jit(solution)/shard_map/all_to_all | solution.py:94
  73.7 65.6 %all-gather.2.cloned.1.call-start = ((), (), s32[]{:S(2)}) async-start(), calls=%async_computation.4 | async-start | bytes 2359296 | tf_op jit(solution)/shard_map/all_gather | solution.py:88
  139.3 4.5 %copy-start.3 = (bf16[256,16,256]{2,0,1:T(8,128)(2,1)S(1)}, bf16[256,16,256]{2,0,1:T(8,128)(2,1)}, u32[]{:S(2)}) copy-start(bf16[256,16,256]{2,0,1:T(8,128)(2,1)} %all-gather.2.cloned.1.call-done) | copy-start | bytes 6291460
  143.8 1.4 copy-start.2
  146.8 62.2 %all-to-all-start.1 = ((bf16[4,64,16,256]{3,2,0,1:T(8,128)(2,1)}), bf16[4,64,16,256]{3,2,0,1:T(8,128)(2,1)}, u32[]{:S(2)}, u32[]{:S(2)}) async-start(bf16[4,64,16,256]{3,2,0,1:T(8,128)(2,1)} %copy.56), calls=%async_computation.1 | async-start | bytes 4194304 | tf_op jit(solution)/shard_map/all_to_all | solution.py:110
  161.6 70.7 %reduce-scatter.5.cloned.1.call-start = ((), (), s32[]{:S(2)}) async-start(), calls=%async_computation.6 | async-start | bytes 2359296 | tf_op jit(solution)/shard_map/reduce_scatter | solution.py:106
  170.8 107.5 %reduce-scatter.3.cloned.1.call-start = ((), (), s32[]{:S(2)}) async-start(), calls=%async_computation.5 | async-start | bytes 2359296 | tf_op jit(solution)/shard_map/reduce_scatter | solution.py:113
Sparse Core Ops, SparseCore 0:
  77.2 62.0 all-gather.1
  170.9 61.3 reduce-scatter.4
  235.7 42.4 reduce-scatter.2

commit v6 on v5

--- a/solution.py
+++ b/solution.py
@@ -34,18 +34,16 @@
     return [(c, (c + 1) % n) for c in range(n)]
 
 
+def swap_pairs(n):
+    return [(c, (c + 1) % n) for c in range(n)]
+
+
 def gather_rows(piece):
     n_core = lax.axis_size("core")
     n_ylo = lax.axis_size("ylo")
-    y = lax.axis_index("ylo")
     c = lax.axis_index("core")
-    right = [piece]
-    left = [piece]
-    for _ in range(n_ylo - 1):
-        right.append(lax.ppermute(right[-1], "ylo", line_pairs(n_ylo, 1)))
-        left.append(lax.ppermute(left[-1], "ylo", line_pairs(n_ylo, -1)))
-    stacked = jnp.stack(right[:0:-1] + left)
-    line = lax.dynamic_slice_in_dim(stacked, n_ylo - 1 - y, n_ylo, axis=0)
+    copies = jnp.broadcast_to(piece[None], (n_ylo,) + piece.shape)
+    line = lax.all_to_all(copies, "ylo", split_axis=0, concat_axis=0, tiled=True)
     other = lax.ppermute(line, "core", swap_pairs(n_core))
     pair = jnp.where(c == 0, jnp.stack([line, other], 1), jnp.stack([other, line], 1))
     return pair.reshape((n_ylo * n_core * piece.shape[0],) + piece.shape[1:])
@@ -54,23 +52,17 @@
 def scatter_rows(term):
     n_core = lax.axis_size("core")
     n_ylo = lax.axis_size("ylo")
-    y = lax.axis_index("ylo")
     c = lax.axis_index("core")
-    sent = lax.dynamic_index_in_dim(term, lax.rem(c + 1, n_core), 0, keepdims=False)
-    kept = lax.dynamic_index_in_dim(term, c, 0, keepdims=False)
+    blocks, total_rows, width = term.shape
+    rows = total_rows // (n_core * n_ylo)
+    split = term.reshape(blocks, n_ylo, n_core, rows, width)
+    sent = lax.dynamic_index_in_dim(split, lax.rem(c + 1, n_core), 2, keepdims=False)
+    kept = lax.dynamic_index_in_dim(split, c, 2, keepdims=False)
     got = lax.ppermute(sent, "core", swap_pairs(n_core))
-    chip = kept.astype(jnp.float32) + got.astype(jnp.float32)
-    total = lax.dynamic_index_in_dim(chip, y, 0, keepdims=False)
-    for step in (1, -1):
-        carry = None
-        for s in range(1, n_ylo):
-            dest = jnp.clip(y + step * (n_ylo - s), 0, n_ylo - 1)
-            block = lax.dynamic_index_in_dim(chip, dest, 0, keepdims=False)
-            if carry is not None:
-                block = block + carry.astype(jnp.float32)
-            carry = lax.ppermute(block.astype(jnp.bfloat16), "ylo", line_pairs(n_ylo, step))
-        total = total + carry.astype(jnp.float32)
-    return total.astype(jnp.bfloat16)
+    half = (kept.astype(jnp.float32) + got.astype(jnp.float32)).astype(jnp.bfloat16)
+    arrived = lax.all_to_all(half, "ylo", split_axis=1, concat_axis=1, tiled=True)
+    total = jnp.sum(arrived.astype(jnp.float32), axis=1).astype(jnp.bfloat16)
+    return jnp.transpose(total, (1, 0, 2))
 
 
 def shards(input_field, target_field, first_factor, second_factor):
@@ -110,13 +102,10 @@
     activated_grad = lax.all_to_all(back, "blk", split_axis=1, concat_axis=1, tiled=True)
     pre_grad = (activated_grad.astype(jnp.float32) * slope).astype(jnp.bfloat16)
     pre_grad = jnp.transpose(pre_grad, (2, 1, 0, 3)).reshape(block_count, block_size, row_count)
-    first_sum = lax.psum_scatter(
-        jnp.einsum("bkr,bir->kbi", inputs, pre_grad, preferred_element_type=jnp.float32).astype(
+    first_sum = scatter_rows(
+        jnp.einsum("bkr,bir->bki", inputs, pre_grad, preferred_element_type=jnp.float32).astype(
             jnp.bfloat16
-        ),
-        dp,
-        scatter_dimension=0,
-        tiled=True,
+        )
     )
     return (first_sum, second_out)
 

time: 287 us -> 278 us (0.969)
  blocking collectives: 0 us -> 74.8 us
  waiting for transfers between devices: 164 us -> 105 us
  starting transfers between devices: 56.9 us -> 39.8 us
  local copies, waits for them, and re-layouts: 28.6 us -> 21.7 us
    all_to_all x0 -> x2, blocking collectives: none -> 74.8 us  [the longest x1 45.4 us: scatter_rows(): lax.all_to_all(half, 'ylo', split_axis=1, concat_axis=1, tiled=True)]
    reduce_scatter x1 -> x0, waiting for transfers between devices: 45.9 us -> none  [shards(): lax.psum_scatter(jnp.einsum('bkr,bir->kbi', inputs, pre_grad, preferred_e...]
    ppermute x6 -> x1, starting transfers between devices: 17.7 us -> 4.86 us  [scatter_rows(): got = lax.ppermute(sent, 'core', swap_pairs(n_core))]
    reduce_scatter x1, waiting for transfers between devices: 11.8 us -> 0.01 us  [shards(): lax.psum_scatter(term.astype(jnp.bfloat16), dp, scatter_dimension=0, tile...]
    ppermute x6 -> x1, waiting for transfers between devices: 9.72 us -> 2.26 us  [scatter_rows(): got = lax.ppermute(sent, 'core', swap_pairs(n_core))]
    all_to_all x1, waiting for transfers between devices: 48 us -> 54.6 us  [shards(): lax.all_to_all(sending, 'blk', split_axis=1, concat_axis=1, tiled=True)]
    all_gather x1, waiting for transfers between devices: 9.38 us -> 4.73 us  [shards(): second_full = lax.all_gather(second_factor, dp, axis=0, tiled=True)]
    convert_element_type x1 -> x0, local copies, waits for them, and re-layouts: 4.55 us -> none  [shards(): jnp.einsum('bkr,bir->kbi', inputs, pre_grad, preferred_element_type=jnp.f...]
  transfers between devices with their start and end apart: 12 -> 6, of which waited for: 10 -> 5; matrix products, arithmetic and copies ran while one was open for 11% -> 9% of each run, Pallas kernels for 0% -> 0%
where the time goes in v6:
time: 278 us; the launch traced here: 277 us
  waiting for transfers between devices  105 us (38%)
  blocking collectives  74.8 us (27%)
  starting transfers between devices  39.8 us (14%)
  local copies, waits for them, and re-layouts  21.7 us (8%)
  between operations  14.2 us (5%)
  matrix products  12.1 us (4%)
  other arithmetic  9.84 us (4%)
    all_to_all x1, waiting for transfers between devices, shards(): lax.all_to_all(sending, 'blk', split_axis=1, concat_axis=1, tiled=True)  54.6 us
    all_to_all x1, blocking collectives, scatter_rows(): lax.all_to_all(half, 'ylo', split_axis=1, concat_axis=1, tiled=True)  45.4 us
    all_to_all x1, waiting for transfers between devices, shards(): lax.all_to_all(back, 'blk', split_axis=1, concat_axis=1, tiled=True)  40.8 us
    all_to_all x1, blocking collectives, gather_rows(): lax.all_to_all(copies, 'ylo', split_axis=0, concat_axis=0, tiled=True)  29.4 us
    all_to_all x1, starting transfers between devices, shards(): lax.all_to_all(sending, 'blk', split_axis=1, concat_axis=1, tiled=True)  17.2 us
    all_to_all x1, starting transfers between devices, shards(): lax.all_to_all(back, 'blk', split_axis=1, concat_axis=1, tiled=True)  13.1 us
  transfers between devices with their start and end apart: 6, of which 5 were waited for; matrix products, arithmetic and copies ran while one was open for 9% of the time, Pallas kernels for 0%

profile of v6, /device:TPU:1, one launch (start us, length us, event | category | flops | bytes accessed | tf_op | source)
XLA Modules:
  0.0 277.2 jit_solution(10054956328034579193)
XLA Ops:
  7.2 0.0 copy-start
  7.2 1.2 broadcast_in_dim.2
  8.4 29.4 %all_to_all.20 = bf16[4,32,16,256]{3,2,1,0:T(8,128)(2,1)S(1)} all-to-all(bf16[4,32,16,256]{3,2,1,0:T(8,128)(2,1)S(1)} %broadcast_in_dim.2), channel_id=1, replica_groups=mesh['blk'=64,'ylo'=4,'core'=2] {'ylo'}, dimensions={0} | all-to-all | bytes 2097152 | tf_op jit(solution)/shard_map/all_to_all | solution.py:46
  37.7 4.4 %collective-permute-start = (bf16[4,32,16,256]{3,2,1,0:T(8,128)(2,1)S(1)}, bf16[4,32,16,256]{3,2,1,0:T(8,128)(2,1)}, u32[]{:S(2)}, u32[]{:S(2)}) collective-permute-start(bf16[4,32,16,256]{3,2,1,0:T(8,128)(2,1)S(1)} %all_to_all.20), channel_id=1, source_target_pairs={{0,1},{1,0},{2,3},{3,2},{4,5},{5,4},{6,7},{7,6},{8,9},{9,8},{10,11... | collective-permute-start | bytes 3145736 | tf_op jit(solution)/shard_map/ppermute | solution.py:47
  42.2 2.4 collective-permute-done
  44.6 1.9 maximum_select_fusion
  46.4 0.1 copy.45
  46.6 0.0 copy-done
  46.6 1.5 fusion.16
  48.1 2.4 copy.70
  50.5 0.0 copy-start.1
  50.6 1.9 copy-done.1
  52.5 2.7 fusion.18
  55.1 0.0 copy-start.4
  55.1 17.2 %all-to-all-start.1 = ((bf16[4,64,16,256]{3,2,0,1:T(8,128)(2,1)}), bf16[4,64,16,256]{3,2,0,1:T(8,128)(2,1)}, u32[]{:S(2)}, u32[]{:S(2)}) async-start(bf16[4,64,16,256]{3,2,0,1:T(8,128)(2,1)} %fusion.18), calls=%async_computation.1 | async-start | bytes 4194304 | tf_op jit(solution)/shard_map/all_to_all | solution.py:86
  72.4 0.0 all-gather.2.cloned.1.call-start
  72.4 0.0 copy-done.4
  72.4 0.8 copy.53
  73.2 0.0 all-gather.2.cloned.1.call-update
  73.2 4.1 %copy.55 = f32[16,256,256]{1,2,0:T(8,128)} copy(bf16[16,256,256]{2,1,0:T(8,128)(2,1)} %bitcast.66) | data formatting | bytes 6291456 | tf_op jit(solution)/shard_map/convert_element_type | solution.py:93
  77.4 54.6 %all-to-all-done.1 = bf16[4,64,16,256]{3,2,0,1:T(8,128)(2,1)} async-done(((bf16[4,64,16,256]{3,2,0,1:T(8,128)(2,1)}), bf16[4,64,16,256]{3,2,0,1:T(8,128)(2,1)}, u32[]{:S(2)}, u32[]{:S(2)}) %all-to-all-start.1) | async-done | bytes 2097184 | tf_op jit(solution)/shard_map/all_to_all | solution.py:86
  131.9 3.2 %copy.52 = bf16[4,64,16,256]{3,2,1,0:T(8,128)(2,1)} copy(bf16[4,64,16,256]{3,2,0,1:T(8,128)(2,1)} %all-to-all-done.1) | data formatting | bytes 4194304 | tf_op jit(solution)/shard_map/all_to_all | solution.py:86
  135.1 4.7 %all-gather.2.cloned.1.call-done = bf16[256,16,256]{2,0,1:T(8,128)(2,1)} async-done(((bf16[32,16,256]{2,0,1:T(8,128)(2,1)}), bf16[256,16,256]{2,0,1:T(8,128)(2,1)}) %all-gather.2.cloned.1.call-update) | async-done | bytes 2097168 | tf_op jit(solution)/shard_map/all_gather | solution.py:80
  139.8 0.0 copy-start.3
  139.8 4.5 %fusion.9 = bf16[16,256,256]{1,2,0:T(8,128)(2,1)S(1)} fusion(f32[16,256,256]{1,2,0:T(8,128)} %copy.55, bf16[16,256,256]{2,1,0:T(8,128)(2,1)} %bitcast.59, bf16[256,16,256]{2,0,1:T(8,128)(2,1)} %all-gather.2.cloned.1.call-done), kind=kOutput, calls=%fused_computation.12 | convolution fusion | flops 540016640 | bytes 10485760 | tf_op jit(solution)/shard_map/qcj,qcr->qjr/dot_general | solution.py:90
  144.3 0.0 copy-done.3
  144.4 0.0 copy-start.2
  144.4 0.7 fusion.22
  145.1 0.6 copy-done.2
  145.7 1.6 copy.57
  147.3 13.1 %all-to-all-start.2 = ((bf16[4,64,16,256]{3,2,0,1:T(8,128)(2,1)}), bf16[4,64,16,256]{3,2,0,1:T(8,128)(2,1)}, u32[]{:S(2)}, u32[]{:S(2)}) async-start(bf16[4,64,16,256]{3,2,0,1:T(8,128)(2,1)} %copy.57), calls=%async_computation.2 | async-start | bytes 4194304 | tf_op jit(solution)/shard_map/all_to_all | solution.py:102
  160.4 0.2 reduce-scatter.2.cloned.1.call-start
  160.6 4.3 %convert_bitcast_fusion = bf16[256,16,256]{0,2,1:T(8,128)(2,1)} fusion(bf16[16,256,256]{1,2,0:T(8,128)(2,1)} %copy-done.2, bf16[16,256,256]{2,1,0:T(8,128)(2,1)} %bitcast.60), kind=kOutput, calls=%fused_computation.24 | convolution fusion | flops 537919488 | bytes 6291456 | tf_op jit(solution)/shard_map/qcr,qjr->cqj/dot_general | solution.py:97
  164.9 4.6 %copy.65 = bf16[256,16,256]{2,1,0:T(8,128)(2,1)} copy(bf16[256,16,256]{0,2,1:T(8,128)(2,1)} %convert_bitcast_fusion) | data formatting | bytes 4194304 | tf_op jit(solution)/shard_map/convert_element_type | solution.py:99
  169.5 0.0 reduce-scatter.2.cloned.1.call-update
  169.6 40.8 %all-to-all-done.2 = bf16[4,64,16,256]{3,2,0,1:T(8,128)(2,1)} async-done(((bf16[4,64,16,256]{3,2,0,1:T(8,128)(2,1)}), bf16[4,64,16,256]{3,2,0,1:T(8,128)(2,1)}, u32[]{:S(2)}, u32[]{:S(2)}) %all-to-all-start.2) | async-done | bytes 2097184 | tf_op jit(solution)/shard_map/all_to_all | solution.py:102
  210.3 4.7 %fusion.7 = bf16[4,64,16,256]{3,2,0,1:T(8,128)(2,1)S(1)} fusion(f32[16,64,4,256]{3,0,2,1:T(8,128)} %bitcast.58, bf16[4,64,16,256]{3,2,0,1:T(8,128)(2,1)} %all-to-all-done.2), kind=kLoop, calls=%fused_computation.9 | loop fusion | flops 20971520 | bytes 8388608 | tf_op jit(solution)/shard_map/convert_element_type | solution.py:103
  215.0 1.0 fusion.19
  216.0 0.2 constant_dynamic-slice_fusion.1
  216.2 0.1 copy.83
  216.3 4.9 %collective-permute-start.1 = (bf16[16,4,32,256]{3,2,0,1:T(8,128)(2,1)S(1)}, bf16[16,4,32,256]{3,2,0,1:T(8,128)(2,1)S(1)}, u32[]{:S(2)}, u32[]{:S(2)}) collective-permute-start(bf16[16,4,32,256]{3,2,0,1:T(8,128)(2,1)S(1)} %bitcast.68), channel_id=1, source_target_pairs={{0,1},{1,0},{2,3},{3,2},{4,5},{5,4},{6,7},{7,6},{8,9},{9,8},{10,11... | collective-permute-start | bytes 3145736 | tf_op jit(solution)/shard_map/ppermute | solution.py:61
  221.2 2.3 collective-permute-done.1
  223.4 0.4 fusion.10
  223.9 45.4 %all_to_all.21 = bf16[16,4,32,256]{3,2,0,1:T(8,128)(2,1)S(1)} all-to-all(bf16[16,4,32,256]{3,2,0,1:T(8,128)(2,1)S(1)} %fusion.10), channel_id=1, replica_groups=mesh['blk'=64,'ylo'=4,'core'=2] {'ylo'}, dimensions={1} | all-to-all | bytes 2097152 | tf_op jit(solution)/shard_map/all_to_all | solution.py:63
  269.3 0.2 reduce_sum.12
  269.5 0.9 copy.66
  270.3 0.0 reduce-scatter.2.cloned.1.call-done
Async XLA Ops:
  7.2 39.4 %copy-start = (bf16[4096,256]{1,0:T(8,128)(2,1)S(1)}, bf16[4096,256]{1,0:T(8,128)(2,1)}, u32[]{:S(2)}) copy-start(bf16[4096,256]{1,0:T(8,128)(2,1)} %param.4) | copy-start | bytes 6291460
  37.7 6.8 %collective-permute-start = (bf16[4,32,16,256]{3,2,1,0:T(8,128)(2,1)S(1)}, bf16[4,32,16,256]{3,2,1,0:T(8,128)(2,1)}, u32[]{:S(2)}, u32[]{:S(2)}) collective-permute-start(bf16[4,32,16,256]{3,2,1,0:T(8,128)(2,1)S(1)} %all_to_all.20), channel_id=1, source_target_pairs={{0,1},{1,0},{2,3},{3,2},{4,5},{5,4},{6,7},{7,6},{8,9},{9,8},{10,11... | collective-permute-start | bytes 3145736 | tf_op jit(solution)/shard_map/ppermute | solution.py:47
  50.5 2.0 copy-start.1
  55.1 17.3 %copy-start.4 = (bf16[32,16,256]{2,1,0:T(8,128)(2,1)S(1)}, bf16[32,16,256]{2,1,0:T(8,128)(2,1)}, u32[]{:S(2)}) copy-start(bf16[32,16,256]{2,1,0:T(8,128)(2,1)} %param.7) | copy-start | bytes 786436
  55.1 76.8 %all-to-all-start.1 = ((bf16[4,64,16,256]{3,2,0,1:T(8,128)(2,1)}), bf16[4,64,16,256]{3,2,0,1:T(8,128)(2,1)}, u32[]{:S(2)}, u32[]{:S(2)}) async-start(bf16[4,64,16,256]{3,2,0,1:T(8,128)(2,1)} %fusion.18), calls=%async_computation.1 | async-start | bytes 4194304 | tf_op jit(solution)/shard_map/all_to_all | solution.py:86
  72.4 67.5 %all-gather.2.cloned.1.call-start = ((), (), s32[]{:S(2)}) async-start(), calls=%async_computation.5 | async-start | bytes 2359296 | tf_op jit(solution)/shard_map/all_gather | solution.py:80
  139.8 4.5 %copy-start.3 = (bf16[256,16,256]{2,0,1:T(8,128)(2,1)S(1)}, bf16[256,16,256]{2,0,1:T(8,128)(2,1)}, u32[]{:S(2)}) copy-start(bf16[256,16,256]{2,0,1:T(8,128)(2,1)} %all-gather.2.cloned.1.call-done) | copy-start | bytes 6291460
  144.4 1.3 copy-start.2
  147.3 63.0 %all-to-all-start.2 = ((bf16[4,64,16,256]{3,2,0,1:T(8,128)(2,1)}), bf16[4,64,16,256]{3,2,0,1:T(8,128)(2,1)}, u32[]{:S(2)}, u32[]{:S(2)}) async-start(bf16[4,64,16,256]{3,2,0,1:T(8,128)(2,1)} %copy.57), calls=%async_computation.2 | async-start | bytes 4194304 | tf_op jit(solution)/shard_map/all_to_all | solution.py:102
  160.4 109.9 %reduce-scatter.2.cloned.1.call-start = ((), (), s32[]{:S(2)}) async-start(), calls=%async_computation.6 | async-start | bytes 2359296 | tf_op jit(solution)/shard_map/reduce_scatter | solution.py:98
  216.3 7.1 %collective-permute-start.1 = (bf16[16,4,32,256]{3,2,0,1:T(8,128)(2,1)S(1)}, bf16[16,4,32,256]{3,2,0,1:T(8,128)(2,1)S(1)}, u32[]{:S(2)}, u32[]{:S(2)}) collective-permute-start(bf16[16,4,32,256]{3,2,0,1:T(8,128)(2,1)S(1)} %bitcast.68), channel_id=1, source_target_pairs={{0,1},{1,0},{2,3},{3,2},{4,5},{5,4},{6,7},{7,6},{8,9},{9,8},{10,11... | collective-permute-start | bytes 3145736 | tf_op jit(solution)/shard_map/ppermute | solution.py:61
Sparse Core Ops, SparseCore 0:
  75.9 63.9 all-gather.1
  169.7 59.2 reduce-scatter.1

commit v7 on v6

--- a/solution.py
+++ b/solution.py
@@ -81,7 +81,7 @@
     pre_act = jnp.einsum("bkr,kbi->bir", inputs, first_full, preferred_element_type=jnp.float32)
     pre_split = pre_act.reshape(block_count, blk_count, inner_count, row_count)
     activated = gelu_value(pre_split).astype(jnp.bfloat16)
-    slope = jnp.transpose(gelu_slope(pre_split), (2, 1, 0, 3))
+    slope = jnp.transpose(gelu_slope(pre_split).astype(jnp.bfloat16), (2, 1, 0, 3))
     sending = jnp.transpose(activated, (2, 1, 0, 3))
     received = lax.all_to_all(sending, "blk", split_axis=1, concat_axis=1, tiled=True)
     permuted = received.reshape(block_count, block_size, row_count)

time: 278 us -> 278 us (level)
  no operation moved by 1% of the time
where the time goes in v7:
time: 278 us; the launch traced here: 277 us
  waiting for transfers between devices  105 us (38%)
  blocking collectives  74.8 us (27%)
  starting transfers between devices  39.8 us (14%)
  local copies, waits for them, and re-layouts  21.7 us (8%)
  between operations  14.2 us (5%)
  matrix products  12 us (4%)
  other arithmetic  9.9 us (4%)
    all_to_all x1, waiting for transfers between devices, shards(): lax.all_to_all(sending, 'blk', split_axis=1, concat_axis=1, tiled=True)  54.6 us
    all_to_all x1, blocking collectives, scatter_rows(): lax.all_to_all(half, 'ylo', split_axis=1, concat_axis=1, tiled=True)  45.4 us
    all_to_all x1, waiting for transfers between devices, shards(): lax.all_to_all(back, 'blk', split_axis=1, concat_axis=1, tiled=True)  40.8 us
    all_to_all x1, blocking collectives, gather_rows(): lax.all_to_all(copies, 'ylo', split_axis=0, concat_axis=0, tiled=True)  29.4 us
    all_to_all x1, starting transfers between devices, shards(): lax.all_to_all(sending, 'blk', split_axis=1, concat_axis=1, tiled=True)  17.2 us
    all_to_all x1, starting transfers between devices, shards(): lax.all_to_all(back, 'blk', split_axis=1, concat_axis=1, tiled=True)  13.1 us
  transfers between devices with their start and end apart: 6, of which 5 were waited for; matrix products, arithmetic and copies ran while one was open for 9% of the time, Pallas kernels for 0%

profile of v7, /device:TPU:1, one launch (start us, length us, event | category | flops | bytes accessed | tf_op | source)
XLA Modules:
  0.0 277.2 jit_solution(2507032751182495617)
XLA Ops:
  7.2 0.0 copy-start
  7.2 1.2 broadcast_in_dim.2
  8.4 29.4 %all_to_all.20 = bf16[4,32,16,256]{3,2,1,0:T(8,128)(2,1)S(1)} all-to-all(bf16[4,32,16,256]{3,2,1,0:T(8,128)(2,1)S(1)} %broadcast_in_dim.2), channel_id=1, replica_groups=mesh['blk'=64,'ylo'=4,'core'=2] {'ylo'}, dimensions={0} | all-to-all | bytes 2097152 | tf_op jit(solution)/shard_map/all_to_all | solution.py:46
  37.7 4.4 %collective-permute-start = (bf16[4,32,16,256]{3,2,1,0:T(8,128)(2,1)S(1)}, bf16[4,32,16,256]{3,2,1,0:T(8,128)(2,1)}, u32[]{:S(2)}, u32[]{:S(2)}) collective-permute-start(bf16[4,32,16,256]{3,2,1,0:T(8,128)(2,1)S(1)} %all_to_all.20), channel_id=1, source_target_pairs={{0,1},{1,0},{2,3},{3,2},{4,5},{5,4},{6,7},{7,6},{8,9},{9,8},{10,11... | collective-permute-start | bytes 3145736 | tf_op jit(solution)/shard_map/ppermute | solution.py:47
  42.2 2.4 collective-permute-done
  44.6 1.9 maximum_select_fusion
  46.4 0.1 copy.45
  46.6 0.0 copy-done
  46.6 1.5 fusion.15
  48.1 2.4 copy.70
  50.5 0.0 copy-start.1
  50.6 1.9 copy-done.1
  52.5 2.7 fusion.17
  55.1 0.0 copy-start.4
  55.1 17.2 %all-to-all-start.1 = ((bf16[4,64,16,256]{3,2,0,1:T(8,128)(2,1)}), bf16[4,64,16,256]{3,2,0,1:T(8,128)(2,1)}, u32[]{:S(2)}, u32[]{:S(2)}) async-start(bf16[4,64,16,256]{3,2,0,1:T(8,128)(2,1)} %fusion.17), calls=%async_computation.1 | async-start | bytes 4194304 | tf_op jit(solution)/shard_map/all_to_all | solution.py:86
  72.4 0.0 all-gather.2.cloned.1.call-start
  72.4 0.0 copy-done.4
  72.4 0.8 copy.53
  73.2 0.0 all-gather.2.cloned.1.call-update
  73.2 4.1 %copy.55 = f32[16,256,256]{1,2,0:T(8,128)} copy(bf16[16,256,256]{2,1,0:T(8,128)(2,1)} %bitcast.64) | data formatting | bytes 6291456 | tf_op jit(solution)/shard_map/convert_element_type | solution.py:93
  77.4 54.6 %all-to-all-done.1 = bf16[4,64,16,256]{3,2,0,1:T(8,128)(2,1)} async-done(((bf16[4,64,16,256]{3,2,0,1:T(8,128)(2,1)}), bf16[4,64,16,256]{3,2,0,1:T(8,128)(2,1)}, u32[]{:S(2)}, u32[]{:S(2)}) %all-to-all-start.1) | async-done | bytes 2097184 | tf_op jit(solution)/shard_map/all_to_all | solution.py:86
  131.9 3.2 %copy.52 = bf16[4,64,16,256]{3,2,1,0:T(8,128)(2,1)} copy(bf16[4,64,16,256]{3,2,0,1:T(8,128)(2,1)} %all-to-all-done.1) | data formatting | bytes 4194304 | tf_op jit(solution)/shard_map/all_to_all | solution.py:86
  135.1 4.7 %all-gather.2.cloned.1.call-done = bf16[256,16,256]{2,0,1:T(8,128)(2,1)} async-done(((bf16[32,16,256]{2,0,1:T(8,128)(2,1)}), bf16[256,16,256]{2,0,1:T(8,128)(2,1)}) %all-gather.2.cloned.1.call-update) | async-done | bytes 2097168 | tf_op jit(solution)/shard_map/all_gather | solution.py:80
  139.8 0.0 copy-start.3
  139.8 4.5 %fusion.8 = bf16[16,256,256]{1,2,0:T(8,128)(2,1)S(1)} fusion(f32[16,256,256]{1,2,0:T(8,128)} %copy.55, bf16[16,256,256]{2,1,0:T(8,128)(2,1)} %bitcast.57, bf16[256,16,256]{2,0,1:T(8,128)(2,1)} %all-gather.2.cloned.1.call-done), kind=kOutput, calls=%fused_computation.12 | convolution fusion | flops 540016640 | bytes 10485760 | tf_op jit(solution)/shard_map/qcj,qcr->qjr/dot_general | solution.py:90
  144.3 0.0 copy-done.3
  144.4 0.0 copy-start.2
  144.4 0.7 fusion.21
  145.1 0.6 copy-done.2
  145.7 1.6 copy.57
  147.3 13.1 %all-to-all-start.2 = ((bf16[4,64,16,256]{3,2,0,1:T(8,128)(2,1)}), bf16[4,64,16,256]{3,2,0,1:T(8,128)(2,1)}, u32[]{:S(2)}, u32[]{:S(2)}) async-start(bf16[4,64,16,256]{3,2,0,1:T(8,128)(2,1)} %copy.57), calls=%async_computation.2 | async-start | bytes 4194304 | tf_op jit(solution)/shard_map/all_to_all | solution.py:102
  160.4 0.2 reduce-scatter.2.cloned.1.call-start
  160.6 4.3 %convert_bitcast_fusion = bf16[256,16,256]{0,2,1:T(8,128)(2,1)} fusion(bf16[16,256,256]{1,2,0:T(8,128)(2,1)} %copy-done.2, bf16[16,256,256]{2,1,0:T(8,128)(2,1)} %bitcast.58), kind=kOutput, calls=%fused_computation.24 | convolution fusion | flops 537919488 | bytes 6291456 | tf_op jit(solution)/shard_map/qcr,qjr->cqj/dot_general | solution.py:97
  164.9 4.6 %copy.65 = bf16[256,16,256]{2,1,0:T(8,128)(2,1)} copy(bf16[256,16,256]{0,2,1:T(8,128)(2,1)} %convert_bitcast_fusion) | data formatting | bytes 4194304 | tf_op jit(solution)/shard_map/convert_element_type | solution.py:99
  169.5 0.0 reduce-scatter.2.cloned.1.call-update
  169.6 40.8 %all-to-all-done.2 = bf16[4,64,16,256]{3,2,0,1:T(8,128)(2,1)} async-done(((bf16[4,64,16,256]{3,2,0,1:T(8,128)(2,1)}), bf16[4,64,16,256]{3,2,0,1:T(8,128)(2,1)}, u32[]{:S(2)}, u32[]{:S(2)}) %all-to-all-start.2) | async-done | bytes 2097184 | tf_op jit(solution)/shard_map/all_to_all | solution.py:102
  210.3 4.8 %fusion.6 = bf16[4,64,16,256]{3,2,0,1:T(8,128)(2,1)S(1)} fusion(bf16[4,64,16,256]{3,2,0,1:T(8,128)(2,1)} %all-to-all-done.2, f32[16,64,4,256]{3,0,2,1:T(8,128)} %bitcast.56), kind=kLoop, calls=%fused_computation.9 | loop fusion | flops 23068672 | bytes 8388608 | tf_op jit(solution)/shard_map/convert_element_type | solution.py:103
  215.1 1.0 fusion.18
  216.1 0.2 constant_dynamic-slice_fusion.1
  216.3 0.1 copy.83
  216.3 4.9 %collective-permute-start.1 = (bf16[16,4,32,256]{3,2,0,1:T(8,128)(2,1)S(1)}, bf16[16,4,32,256]{3,2,0,1:T(8,128)(2,1)S(1)}, u32[]{:S(2)}, u32[]{:S(2)}) collective-permute-start(bf16[16,4,32,256]{3,2,0,1:T(8,128)(2,1)S(1)} %bitcast.66), channel_id=1, source_target_pairs={{0,1},{1,0},{2,3},{3,2},{4,5},{5,4},{6,7},{7,6},{8,9},{9,8},{10,11... | collective-permute-start | bytes 3145736 | tf_op jit(solution)/shard_map/ppermute | solution.py:61
  221.2 2.3 collective-permute-done.1
  223.5 0.4 fusion.9
  223.9 45.4 %all_to_all.21 = bf16[16,4,32,256]{3,2,0,1:T(8,128)(2,1)S(1)} all-to-all(bf16[16,4,32,256]{3,2,0,1:T(8,128)(2,1)S(1)} %fusion.9), channel_id=1, replica_groups=mesh['blk'=64,'ylo'=4,'core'=2] {'ylo'}, dimensions={1} | all-to-all | bytes 2097152 | tf_op jit(solution)/shard_map/all_to_all | solution.py:63
  269.3 0.2 reduce_sum.12
  269.5 0.9 copy.66
  270.4 0.0 reduce-scatter.2.cloned.1.call-done
Async XLA Ops:
  7.2 39.4 %copy-start = (bf16[4096,256]{1,0:T(8,128)(2,1)S(1)}, bf16[4096,256]{1,0:T(8,128)(2,1)}, u32[]{:S(2)}) copy-start(bf16[4096,256]{1,0:T(8,128)(2,1)} %param.4) | copy-start | bytes 6291460
  37.7 6.8 %collective-permute-start = (bf16[4,32,16,256]{3,2,1,0:T(8,128)(2,1)S(1)}, bf16[4,32,16,256]{3,2,1,0:T(8,128)(2,1)}, u32[]{:S(2)}, u32[]{:S(2)}) collective-permute-start(bf16[4,32,16,256]{3,2,1,0:T(8,128)(2,1)S(1)} %all_to_all.20), channel_id=1, source_target_pairs={{0,1},{1,0},{2,3},{3,2},{4,5},{5,4},{6,7},{7,6},{8,9},{9,8},{10,11... | collective-permute-start | bytes 3145736 | tf_op jit(solution)/shard_map/ppermute | solution.py:47
  50.5 2.0 copy-start.1
  55.1 17.3 %copy-start.4 = (bf16[32,16,256]{2,1,0:T(8,128)(2,1)S(1)}, bf16[32,16,256]{2,1,0:T(8,128)(2,1)}, u32[]{:S(2)}) copy-start(bf16[32,16,256]{2,1,0:T(8,128)(2,1)} %param.7) | copy-start | bytes 786436
  55.1 76.8 %all-to-all-start.1 = ((bf16[4,64,16,256]{3,2,0,1:T(8,128)(2,1)}), bf16[4,64,16,256]{3,2,0,1:T(8,128)(2,1)}, u32[]{:S(2)}, u32[]{:S(2)}) async-start(bf16[4,64,16,256]{3,2,0,1:T(8,128)(2,1)} %fusion.17), calls=%async_computation.1 | async-start | bytes 4194304 | tf_op jit(solution)/shard_map/all_to_all | solution.py:86
  72.4 67.5 %all-gather.2.cloned.1.call-start = ((), (), s32[]{:S(2)}) async-start(), calls=%async_computation.5 | async-start | bytes 2359296 | tf_op jit(solution)/shard_map/all_gather | solution.py:80
  139.8 4.5 %copy-start.3 = (bf16[256,16,256]{2,0,1:T(8,128)(2,1)S(1)}, bf16[256,16,256]{2,0,1:T(8,128)(2,1)}, u32[]{:S(2)}) copy-start(bf16[256,16,256]{2,0,1:T(8,128)(2,1)} %all-gather.2.cloned.1.call-done) | copy-start | bytes 6291460
  144.4 1.3 copy-start.2
  147.3 63.0 %all-to-all-start.2 = ((bf16[4,64,16,256]{3,2,0,1:T(8,128)(2,1)}), bf16[4,64,16,256]{3,2,0,1:T(8,128)(2,1)}, u32[]{:S(2)}, u32[]{:S(2)}) async-start(bf16[4,64,16,256]{3,2,0,1:T(8,128)(2,1)} %copy.57), calls=%async_computation.2 | async-start | bytes 4194304 | tf_op jit(solution)/shard_map/all_to_all | solution.py:102
  160.4 110.0 %reduce-scatter.2.cloned.1.call-start = ((), (), s32[]{:S(2)}) async-start(), calls=%async_computation.6 | async-start | bytes 2359296 | tf_op jit(solution)/shard_map/reduce_scatter | solution.py:98
  216.3 7.1 %collective-permute-start.1 = (bf16[16,4,32,256]{3,2,0,1:T(8,128)(2,1)S(1)}, bf16[16,4,32,256]{3,2,0,1:T(8,128)(2,1)S(1)}, u32[]{:S(2)}, u32[]{:S(2)}) collective-permute-start(bf16[16,4,32,256]{3,2,0,1:T(8,128)(2,1)S(1)} %bitcast.66), channel_id=1, source_target_pairs={{0,1},{1,0},{2,3},{3,2},{4,5},{5,4},{6,7},{7,6},{8,9},{9,8},{10,11... | collective-permute-start | bytes 3145736 | tf_op jit(solution)/shard_map/ppermute | solution.py:61
Sparse Core Ops, SparseCore 0:
  75.9 63.9 all-gather.1
  169.7 59.2 reduce-scatter.1

commit v8 on v6

--- a/solution.py
+++ b/solution.py
@@ -82,6 +82,7 @@
     pre_split = pre_act.reshape(block_count, blk_count, inner_count, row_count)
     activated = gelu_value(pre_split).astype(jnp.bfloat16)
     slope = jnp.transpose(gelu_slope(pre_split), (2, 1, 0, 3))
+    activated, second_full = lax.optimization_barrier((activated, second_full))
     sending = jnp.transpose(activated, (2, 1, 0, 3))
     received = lax.all_to_all(sending, "blk", split_axis=1, concat_axis=1, tiled=True)
     permuted = received.reshape(block_count, block_size, row_count)

time: 278 us -> 276 us (level)
  blocking collectives: 74.8 us -> 107 us
  waiting for transfers between devices: 105 us -> 83.5 us
  starting transfers between devices: 39.8 us -> 29.7 us
    all_to_all x1, blocking collectives: 29.4 us -> 73.8 us  [shards(): lax.all_to_all(sending, 'blk', split_axis=1, concat_axis=1, tiled=True)]
    all_to_all x1, waiting for transfers between devices: 54.6 us -> 22.9 us  [gather_rows(): lax.all_to_all(copies, 'ylo', split_axis=0, concat_axis=0, tiled=True)]
    all_to_all x1, waiting for transfers between devices: 40.8 us -> 54.4 us  [shards(): lax.all_to_all(back, 'blk', split_axis=1, concat_axis=1, tiled=True)]
    all_to_all x1, blocking collectives: 45.4 us -> 32.8 us  [scatter_rows(): lax.all_to_all(half, 'ylo', split_axis=1, concat_axis=1, tiled=True)]
    all_to_all x1, starting transfers between devices: 17.2 us -> 5.42 us  [gather_rows(): lax.all_to_all(copies, 'ylo', split_axis=0, concat_axis=0, tiled=True)]
    ppermute x1, starting transfers between devices: 4.44 us -> 9.84 us  [gather_rows(): other = lax.ppermute(line, 'core', swap_pairs(n_core))]
    convert_element_type x1 -> x0, local copies, waits for them, and re-layouts: 4.13 us -> none  [shards(): targets.astype(jnp.float32)]
    all_gather x1, waiting for transfers between devices: 4.73 us -> 0.79 us  [shards(): second_full = lax.all_gather(second_factor, dp, axis=0, tiled=True)]
where the time goes in v8:
time: 276 us
  blocking collectives  107 us (39%)
  waiting for transfers between devices  83.5 us (30%)
  starting transfers between devices  29.7 us (11%)
  local copies, waits for them, and re-layouts  22.5 us (8%)
  between operations  14.2 us (5%)
  other arithmetic  9.85 us (4%)
  matrix products  9.36 us (3%)
    all_to_all x1, blocking collectives, shards(): lax.all_to_all(sending, 'blk', split_axis=1, concat_axis=1, tiled=True)  73.8 us
    all_to_all x1, waiting for transfers between devices, shards(): lax.all_to_all(back, 'blk', split_axis=1, concat_axis=1, tiled=True)  54.4 us
    all_to_all x1, blocking collectives, scatter_rows(): lax.all_to_all(half, 'ylo', split_axis=1, concat_axis=1, tiled=True)  32.8 us
    all_to_all x1, waiting for transfers between devices, gather_rows(): lax.all_to_all(copies, 'ylo', split_axis=0, concat_axis=0, tiled=True)  22.9 us
    ppermute x1, starting transfers between devices, gather_rows(): other = lax.ppermute(line, 'core', swap_pairs(n_core))  9.84 us
    all_to_all x1, starting transfers between devices, shards(): lax.all_to_all(back, 'blk', split_axis=1, concat_axis=1, tiled=True)  9.22 us
    unnamed x13, local copies, waits for them, and re-layouts  5.92 us
  transfers between devices with their start and end apart: 6, of which 5 were waited for; matrix products, arithmetic and copies ran while one was open for 9% of the time, Pallas kernels for 0%

profile of v8, /device:TPU:1, one launch (start us, length us, event | category | flops | bytes accessed | tf_op | source)
XLA Modules:
  0.0 275.8 jit_solution(8093816750562004966)
XLA Ops:
  7.2 0.0 copy-start
  7.2 2.2 broadcast_in_dim.2
  9.3 5.4 %all-to-all-start = ((bf16[4,32,16,256]{3,2,1,0:T(8,128)(2,1)}), bf16[4,32,16,256]{3,2,1,0:T(8,128)(2,1)S(1)}, u32[]{:S(2)}, u32[]{:S(2)}) async-start(bf16[4,32,16,256]{3,2,1,0:T(8,128)(2,1)} %broadcast_in_dim.2), calls=%async_computation | async-start | bytes 2097152 | tf_op jit(solution)/shard_map/all_to_all | solution.py:46
  14.8 0.0 all-gather.2.cloned.1.call-start
  14.8 0.7 all-gather.2.cloned.1.call-update
  15.5 22.9 %all-to-all-done = bf16[4,32,16,256]{3,2,1,0:T(8,128)(2,1)S(1)} async-done(((bf16[4,32,16,256]{3,2,1,0:T(8,128)(2,1)}), bf16[4,32,16,256]{3,2,1,0:T(8,128)(2,1)S(1)}, u32[]{:S(2)}, u32[]{:S(2)}) %all-to-all-start) | async-done | bytes 1048608 | tf_op jit(solution)/shard_map/all_to_all | solution.py:46
  38.4 9.8 %collective-permute-start = (bf16[4,32,16,256]{3,2,1,0:T(8,128)(2,1)S(1)}, bf16[4,32,16,256]{3,2,1,0:T(8,128)(2,1)}, u32[]{:S(2)}, u32[]{:S(2)}) collective-permute-start(bf16[4,32,16,256]{3,2,1,0:T(8,128)(2,1)S(1)} %all-to-all-done), channel_id=1, source_target_pairs={{0,1},{1,0},{2,3},{3,2},{4,5},{5,4},{6,7},{7,6},{8,9},{9,8},{10,11... | collective-permute-start | bytes 3145736 | tf_op jit(solution)/shard_map/ppermute | solution.py:47
  48.2 2.4 collective-permute-done
  50.6 1.9 maximum_select_fusion
  52.5 0.1 copy.37
  52.6 0.0 copy-done
  52.7 1.5 fusion.13
  54.2 2.4 copy.58
  56.6 0.0 copy-start.1
  56.6 1.9 copy-done.1
  58.6 2.6 multiply_convert_fusion
  61.2 0.8 all-gather.2.cloned.1.call-done
  62.0 2.7 copy.44
  64.7 73.8 %all_to_all.20 = bf16[4,64,16,256]{3,0,2,1:T(4,128)(2,1)S(1)} all-to-all(bf16[4,64,16,256]{3,0,2,1:T(4,128)(2,1)S(1)} %copy.44), channel_id=1, replica_groups=mesh['blk'=64,'ylo'=4,'core'=2] {'blk'}, dimensions={1} | all-to-all | bytes 4194304 | tf_op jit(solution)/shard_map/all_to_all | solution.py:87
  138.5 0.0 copy-start.4
  138.5 0.0 copy-start.5
  138.5 0.3 copy.45
  138.8 0.0 copy-start.3
  138.8 2.0 copy-done.4
  140.8 0.6 copy-done.5
  141.5 1.7 fusion.9
  143.2 0.0 copy-done.3
  143.2 0.0 copy-start.2
  143.2 0.9 convolution_convert_fusion
  144.1 0.4 copy-done.2
  144.5 4.0 %copy.48 = bf16[4,64,16,256]{3,0,2,1:T(4,128)(2,1)} copy(bf16[4,64,16,256]{3,2,1,0:T(8,128)(2,1)S(1)} %bitcast.48) | data formatting | bytes 4194304 | tf_op jit(solution)/shard_map/reshape | solution.py:102
  148.6 9.2 %all-to-all-start.2 = ((bf16[4,64,16,256]{3,0,2,1:T(4,128)(2,1)}), bf16[4,64,16,256]{3,0,2,1:T(4,128)(2,1)}, u32[]{:S(2)}, u32[]{:S(2)}) async-start(bf16[4,64,16,256]{3,0,2,1:T(4,128)(2,1)} %copy.48), calls=%async_computation.2 | async-start | bytes 4194304 | tf_op jit(solution)/shard_map/all_to_all | solution.py:103
  157.8 0.0 reduce-scatter.2.cloned.1.call-start
  157.8 4.3 %convert_bitcast_fusion = bf16[256,16,256]{0,2,1:T(8,128)(2,1)} fusion(bf16[16,256,256]{2,1,0:T(8,128)(2,1)} %copy-done.2, bf16[16,256,256]{2,1,0:T(8,128)(2,1)} %bitcast.45), kind=kOutput, calls=%fused_computation.21 | convolution fusion | flops 537919488 | bytes 6291456 | tf_op jit(solution)/shard_map/qcr,qjr->cqj/dot_general | solution.py:98
  162.1 4.6 %copy.56 = bf16[256,16,256]{2,1,0:T(8,128)(2,1)} copy(bf16[256,16,256]{0,2,1:T(8,128)(2,1)} %convert_bitcast_fusion) | data formatting | bytes 4194304 | tf_op jit(solution)/shard_map/convert_element_type | solution.py:100
  166.8 0.0 reduce-scatter.2.cloned.1.call-update
  166.8 54.4 %all-to-all-done.2 = bf16[4,64,16,256]{3,0,2,1:T(4,128)(2,1)} async-done(((bf16[4,64,16,256]{3,0,2,1:T(4,128)(2,1)}), bf16[4,64,16,256]{3,0,2,1:T(4,128)(2,1)}, u32[]{:S(2)}, u32[]{:S(2)}) %all-to-all-start.2) | async-done | bytes 2097184 | tf_op jit(solution)/shard_map/all_to_all | solution.py:103
  221.2 4.7 %fusion.7 = bf16[4,64,16,256]{3,2,0,1:T(8,128)(2,1)S(1)} fusion(f32[16,64,4,256]{3,0,2,1:T(8,128)} %bitcast.43, bf16[4,64,16,256]{3,0,2,1:T(4,128)(2,1)} %all-to-all-done.2), kind=kLoop, calls=%fused_computation.9 | loop fusion | flops 20971520 | bytes 8388608 | tf_op jit(solution)/shard_map/convert_element_type | solution.py:104
  225.9 1.0 fusion.15
  226.9 0.2 constant_dynamic-slice_fusion.1
  227.1 0.1 copy.76
  227.2 5.2 %collective-permute-start.1 = (bf16[16,4,32,256]{3,2,0,1:T(8,128)(2,1)S(1)}, bf16[16,4,32,256]{3,2,0,1:T(8,128)(2,1)S(1)}, u32[]{:S(2)}, u32[]{:S(2)}) collective-permute-start(bf16[16,4,32,256]{3,2,0,1:T(8,128)(2,1)S(1)} %bitcast.56), channel_id=1, source_target_pairs={{0,1},{1,0},{2,3},{3,2},{4,5},{5,4},{6,7},{7,6},{8,9},{9,8},{10,11... | collective-permute-start | bytes 3145736 | tf_op jit(solution)/shard_map/ppermute | solution.py:61
  232.4 2.3 collective-permute-done.1
  234.7 0.4 fusion.10
  235.1 32.8 %all_to_all.21 = bf16[16,4,32,256]{3,2,0,1:T(8,128)(2,1)S(1)} all-to-all(bf16[16,4,32,256]{3,2,0,1:T(8,128)(2,1)S(1)} %fusion.10), channel_id=1, replica_groups=mesh['blk'=64,'ylo'=4,'core'=2] {'ylo'}, dimensions={1} | all-to-all | bytes 2097152 | tf_op jit(solution)/shard_map/all_to_all | solution.py:63
  267.9 0.2 reduce_sum.12
  268.1 0.9 copy.57
  269.0 0.0 reduce-scatter.2.cloned.1.call-done
Async XLA Ops:
  7.2 45.5 %copy-start = (bf16[4096,256]{1,0:T(8,128)(2,1)S(1)}, bf16[4096,256]{1,0:T(8,128)(2,1)}, u32[]{:S(2)}) copy-start(bf16[4096,256]{1,0:T(8,128)(2,1)} %param.4) | copy-start | bytes 6291460
  9.3 29.0 %all-to-all-start = ((bf16[4,32,16,256]{3,2,1,0:T(8,128)(2,1)}), bf16[4,32,16,256]{3,2,1,0:T(8,128)(2,1)S(1)}, u32[]{:S(2)}, u32[]{:S(2)}) async-start(bf16[4,32,16,256]{3,2,1,0:T(8,128)(2,1)} %broadcast_in_dim.2), calls=%async_computation | async-start | bytes 2097152 | tf_op jit(solution)/shard_map/all_to_all | solution.py:46
  14.8 47.2 %all-gather.2.cloned.1.call-start = ((), (), s32[]{:S(2)}) async-start(), calls=%async_computation.5 | async-start | bytes 2359296 | tf_op jit(solution)/shard_map/all_gather | solution.py:80
  38.4 12.2 %collective-permute-start = (bf16[4,32,16,256]{3,2,1,0:T(8,128)(2,1)S(1)}, bf16[4,32,16,256]{3,2,1,0:T(8,128)(2,1)}, u32[]{:S(2)}, u32[]{:S(2)}) collective-permute-start(bf16[4,32,16,256]{3,2,1,0:T(8,128)(2,1)S(1)} %all-to-all-done), channel_id=1, source_target_pairs={{0,1},{1,0},{2,3},{3,2},{4,5},{5,4},{6,7},{7,6},{8,9},{9,8},{10,11... | collective-permute-start | bytes 3145736 | tf_op jit(solution)/shard_map/ppermute | solution.py:47
  56.6 1.9 copy-start.1
  138.5 2.3 copy-start.4
  138.5 3.0 %copy-start.5 = (bf16[4096,256]{1,0:T(8,128)(2,1)S(1)}, bf16[4096,256]{1,0:T(8,128)(2,1)}, u32[]{:S(2)}) copy-start(bf16[4096,256]{1,0:T(8,128)(2,1)} %param.5) | copy-start | bytes 6291460
  138.8 4.4 %copy-start.3 = (bf16[4,64,16,256]{3,2,1,0:T(8,128)(2,1)}, bf16[4,64,16,256]{3,2,1,0:T(8,128)(2,1)S(1)}, u32[]{:S(2)}) copy-start(bf16[4,64,16,256]{3,2,1,0:T(8,128)(2,1)S(1)} %copy.45) | copy-start | bytes 6291460
  143.2 1.3 copy-start.2
  148.6 72.7 %all-to-all-start.2 = ((bf16[4,64,16,256]{3,0,2,1:T(4,128)(2,1)}), bf16[4,64,16,256]{3,0,2,1:T(4,128)(2,1)}, u32[]{:S(2)}, u32[]{:S(2)}) async-start(bf16[4,64,16,256]{3,0,2,1:T(4,128)(2,1)} %copy.48), calls=%async_computation.2 | async-start | bytes 4194304 | tf_op jit(solution)/shard_map/all_to_all | solution.py:103
  157.8 111.2 %reduce-scatter.2.cloned.1.call-start = ((), (), s32[]{:S(2)}) async-start(), calls=%async_computation.6 | async-start | bytes 2359296 | tf_op jit(solution)/shard_map/reduce_scatter | solution.py:99
  227.2 7.5 %collective-permute-start.1 = (bf16[16,4,32,256]{3,2,0,1:T(8,128)(2,1)S(1)}, bf16[16,4,32,256]{3,2,0,1:T(8,128)(2,1)S(1)}, u32[]{:S(2)}, u32[]{:S(2)}) collective-permute-start(bf16[16,4,32,256]{3,2,0,1:T(8,128)(2,1)S(1)} %bitcast.56), channel_id=1, source_target_pairs={{0,1},{1,0},{2,3},{3,2},{4,5},{5,4},{6,7},{7,6},{8,9},{9,8},{10,11... | collective-permute-start | bytes 3145736 | tf_op jit(solution)/shard_map/ppermute | solution.py:61
Sparse Core Ops, SparseCore 0:
  17.7 44.2 all-gather.1
  166.9 58.5 reduce-scatter.1

commit v9 on v7

--- a/solution.py
+++ b/solution.py
@@ -45,7 +45,9 @@
     copies = jnp.broadcast_to(piece[None], (n_ylo,) + piece.shape)
     line = lax.all_to_all(copies, "ylo", split_axis=0, concat_axis=0, tiled=True)
     other = lax.ppermute(line, "core", swap_pairs(n_core))
-    pair = jnp.where(c == 0, jnp.stack([line, other], 1), jnp.stack([other, line], 1))
+    pair = jnp.zeros((n_ylo, n_core) + piece.shape, piece.dtype)
+    pair = lax.dynamic_update_index_in_dim(pair, line, c, 1)
+    pair = lax.dynamic_update_index_in_dim(pair, other, lax.rem(c + 1, n_core), 1)
     return pair.reshape((n_ylo * n_core * piece.shape[0],) + piece.shape[1:])
 
 
@@ -82,6 +84,7 @@
     pre_split = pre_act.reshape(block_count, blk_count, inner_count, row_count)
     activated = gelu_value(pre_split).astype(jnp.bfloat16)
     slope = jnp.transpose(gelu_slope(pre_split).astype(jnp.bfloat16), (2, 1, 0, 3))
+    activated, second_full, slope = lax.optimization_barrier((activated, second_full, slope))
     sending = jnp.transpose(activated, (2, 1, 0, 3))
     received = lax.all_to_all(sending, "blk", split_axis=1, concat_axis=1, tiled=True)
     permuted = received.reshape(block_count, block_size, row_count)

time: 278 us -> 272 us (0.978)
  blocking collectives: 74.8 us -> 105 us
  waiting for transfers between devices: 105 us -> 81.2 us
  starting transfers between devices: 39.8 us -> 31.3 us
    all_to_all x1, blocking collectives: 29.4 us -> 73.7 us  [shards(): lax.all_to_all(sending, 'blk', split_axis=1, concat_axis=1, tiled=True)]
    all_to_all x1, waiting for transfers between devices: 54.6 us -> 22.9 us  [gather_rows(): lax.all_to_all(copies, 'ylo', split_axis=0, concat_axis=0, tiled=True)]
    all_to_all x1, blocking collectives: 45.4 us -> 31.6 us  [scatter_rows(): lax.all_to_all(half, 'ylo', split_axis=1, concat_axis=1, tiled=True)]
    all_to_all x1, starting transfers between devices: 17.2 us -> 5.42 us  [gather_rows(): lax.all_to_all(copies, 'ylo', split_axis=0, concat_axis=0, tiled=True)]
    all_to_all x1, waiting for transfers between devices: 40.8 us -> 51.3 us  [shards(): lax.all_to_all(back, 'blk', split_axis=1, concat_axis=1, tiled=True)]
    ppermute x1, starting transfers between devices: 4.44 us -> 9.84 us  [gather_rows(): other = lax.ppermute(line, 'core', swap_pairs(n_core))]
    all_to_all x1, starting transfers between devices: 13.1 us -> 7.73 us  [shards(): lax.all_to_all(back, 'blk', split_axis=1, concat_axis=1, tiled=True)]
    convert_element_type x1 -> x0, local copies, waits for them, and re-layouts: 4.13 us -> none  [shards(): targets.astype(jnp.float32)]
where the time goes in v9:
time: 272 us; the launch traced here: 271 us
  blocking collectives  105 us (39%)
  waiting for transfers between devices  81.2 us (30%)
  starting transfers between devices  31.3 us (12%)
  local copies, waits for them, and re-layouts  22 us (8%)
  between operations  14.2 us (5%)
  matrix products  9.36 us (3%)
  other arithmetic  7.91 us (3%)
    all_to_all x1, blocking collectives, shards(): lax.all_to_all(sending, 'blk', split_axis=1, concat_axis=1, tiled=True)  73.7 us
    all_to_all x1, waiting for transfers between devices, shards(): lax.all_to_all(back, 'blk', split_axis=1, concat_axis=1, tiled=True)  51.3 us
    all_to_all x1, blocking collectives, scatter_rows(): lax.all_to_all(half, 'ylo', split_axis=1, concat_axis=1, tiled=True)  31.6 us
    all_to_all x1, waiting for transfers between devices, gather_rows(): lax.all_to_all(copies, 'ylo', split_axis=0, concat_axis=0, tiled=True)  22.9 us
    ppermute x1, starting transfers between devices, gather_rows(): other = lax.ppermute(line, 'core', swap_pairs(n_core))  9.84 us
    ppermute x1, starting transfers between devices, scatter_rows(): got = lax.ppermute(sent, 'core', swap_pairs(n_core))  8.31 us
    all_to_all x1, starting transfers between devices, shards(): lax.all_to_all(back, 'blk', split_axis=1, concat_axis=1, tiled=True)  7.73 us
  transfers between devices with their start and end apart: 6, of which 5 were waited for; matrix products, arithmetic and copies ran while one was open for 9% of the time, Pallas kernels for 0%

profile of v9, /device:TPU:1, one launch (start us, length us, event | category | flops | bytes accessed | tf_op | source)
XLA Modules:
  0.0 271.4 jit_solution(2971502335335955492)
XLA Ops:
  7.2 0.0 copy-start
  7.2 2.2 broadcast_in_dim.17
  9.3 5.4 %all-to-all-start = ((bf16[4,32,16,256]{3,2,1,0:T(8,128)(2,1)}), bf16[4,32,16,256]{3,2,1,0:T(8,128)(2,1)S(1)}, u32[]{:S(2)}, u32[]{:S(2)}) async-start(bf16[4,32,16,256]{3,2,1,0:T(8,128)(2,1)} %broadcast_in_dim.17), calls=%async_computation | async-start | bytes 2097152 | tf_op jit(solution)/shard_map/all_to_all | solution.py:46
  14.8 0.0 all-gather.2.cloned.1.call-start
  14.8 0.7 all-gather.2.cloned.1.call-update
  15.5 22.9 %all-to-all-done = bf16[4,32,16,256]{3,2,1,0:T(8,128)(2,1)S(1)} async-done(((bf16[4,32,16,256]{3,2,1,0:T(8,128)(2,1)}), bf16[4,32,16,256]{3,2,1,0:T(8,128)(2,1)S(1)}, u32[]{:S(2)}, u32[]{:S(2)}) %all-to-all-start) | async-done | bytes 1048608 | tf_op jit(solution)/shard_map/all_to_all | solution.py:46
  38.4 9.8 %collective-permute-start = (bf16[4,32,16,256]{3,2,1,0:T(8,128)(2,1)S(1)}, bf16[4,32,16,256]{3,2,1,0:T(8,128)(2,1)}, u32[]{:S(2)}, u32[]{:S(2)}) collective-permute-start(bf16[4,32,16,256]{3,2,1,0:T(8,128)(2,1)S(1)} %all-to-all-done), channel_id=1, source_target_pairs={{0,1},{1,0},{2,3},{3,2},{4,5},{5,4},{6,7},{7,6},{8,9},{9,8},{10,11... | collective-permute-start | bytes 3145736 | tf_op jit(solution)/shard_map/ppermute | solution.py:47
  48.2 0.2 broadcast_in_dim.16
  48.4 0.1 bitcast_dynamic-update-slice_fusion.1
  48.5 2.1 collective-permute-done
  50.6 1.3 bitcast_dynamic-update-slice_fusion
  51.9 0.0 copy-done
  51.9 1.5 fusion.11
  53.5 2.4 copy.62
  55.9 4.2 %fusion.13 = (bf16[4,64,16,256]{3,2,0,1:T(8,128)(2,1)}, bf16[16,64,4,256]{3,0,2,1:T(8,128)(2,1)}) fusion(f32[16,64,4,256]{3,0,2,1:T(8,128)S(1)} %bitcast.46), kind=kLoop, calls=%fused_computation.20 | loop fusion | flops 20971520 | bytes 8388608 | tf_op jit(solution)/shard_map/transpose | solution.py:86
  60.0 1.9 all-gather.2.cloned.1.call-done
  62.0 2.7 copy.50
  64.7 73.7 %all_to_all.20 = bf16[4,64,16,256]{3,0,2,1:T(4,128)(2,1)S(1)} all-to-all(bf16[4,64,16,256]{3,0,2,1:T(4,128)(2,1)S(1)} %copy.50), channel_id=1, replica_groups=mesh['blk'=64,'ylo'=4,'core'=2] {'blk'}, dimensions={1} | all-to-all | bytes 4194304 | tf_op jit(solution)/shard_map/all_to_all | solution.py:89
  138.4 0.0 copy-start.3
  138.4 0.0 copy-start.4
  138.4 0.3 copy.51
  138.7 0.0 copy-start.2
  138.7 2.0 copy-done.3
  140.7 0.6 copy-done.4
  141.4 1.7 fusion.7
  143.1 0.0 copy-done.2
  143.1 0.0 copy-start.1
  143.1 0.9 convolution_convert_fusion
  144.0 0.5 copy-done.1
  144.4 4.0 %copy.54 = bf16[4,64,16,256]{3,0,2,1:T(4,128)(2,1)} copy(bf16[4,64,16,256]{3,2,1,0:T(8,128)(2,1)S(1)} %bitcast.49) | data formatting | bytes 4194304 | tf_op jit(solution)/shard_map/reshape | solution.py:104
  148.5 7.7 %all-to-all-start.2 = ((bf16[4,64,16,256]{3,0,2,1:T(4,128)(2,1)}), bf16[4,64,16,256]{3,0,2,1:T(4,128)(2,1)}, u32[]{:S(2)}, u32[]{:S(2)}) async-start(bf16[4,64,16,256]{3,0,2,1:T(4,128)(2,1)} %copy.54), calls=%async_computation.2 | async-start | bytes 4194304 | tf_op jit(solution)/shard_map/all_to_all | solution.py:105
  156.2 0.0 reduce-scatter.2.cloned.1.call-start
  156.3 4.3 %convert_bitcast_fusion = bf16[256,16,256]{0,2,1:T(8,128)(2,1)} fusion(bf16[16,256,256]{2,1,0:T(8,128)(2,1)} %copy-done.1, bf16[16,256,256]{2,1,0:T(8,128)(2,1)} %bitcast.45), kind=kOutput, calls=%fused_computation.19 | convolution fusion | flops 537919488 | bytes 6291456 | tf_op jit(solution)/shard_map/qcr,qjr->cqj/dot_general | solution.py:100
  160.6 4.6 %copy.60 = bf16[256,16,256]{2,1,0:T(8,128)(2,1)} copy(bf16[256,16,256]{0,2,1:T(8,128)(2,1)} %convert_bitcast_fusion) | data formatting | bytes 4194304 | tf_op jit(solution)/shard_map/convert_element_type | solution.py:102
  165.2 0.0 reduce-scatter.2.cloned.1.call-update
  165.2 51.3 %all-to-all-done.2 = bf16[4,64,16,256]{3,0,2,1:T(4,128)(2,1)} async-done(((bf16[4,64,16,256]{3,0,2,1:T(4,128)(2,1)}), bf16[4,64,16,256]{3,0,2,1:T(4,128)(2,1)}, u32[]{:S(2)}, u32[]{:S(2)}) %all-to-all-start.2) | async-done | bytes 2097184 | tf_op jit(solution)/shard_map/all_to_all | solution.py:105
  216.5 3.1 %multiply_convert_fusion = bf16[4,64,16,256]{3,2,0,1:T(8,128)(2,1)S(1)} fusion(bf16[4,64,16,256]{3,2,0,1:T(8,128)(2,1)} %get-tuple-element.7, bf16[4,64,16,256]{3,0,2,1:T(4,128)(2,1)} %all-to-all-done.2), kind=kLoop, calls=%fused_computation.11 | loop fusion | flops 4194304 | bytes 6291456 | tf_op jit(solution)/shard_map/convert_element_type | solution.py:106
  219.6 1.0 fusion.14
  220.6 0.2 constant_dynamic-slice_fusion.1
  220.8 0.1 copy.80
  220.9 8.3 %collective-permute-start.1 = (bf16[16,4,32,256]{3,2,0,1:T(8,128)(2,1)S(1)}, bf16[16,4,32,256]{3,2,0,1:T(8,128)(2,1)S(1)}, u32[]{:S(2)}, u32[]{:S(2)}) collective-permute-start(bf16[16,4,32,256]{3,2,0,1:T(8,128)(2,1)S(1)} %bitcast.56), channel_id=1, source_target_pairs={{0,1},{1,0},{2,3},{3,2},{4,5},{5,4},{6,7},{7,6},{8,9},{9,8},{10,11... | collective-permute-start | bytes 3145736 | tf_op jit(solution)/shard_map/ppermute | solution.py:63
  229.2 2.3 collective-permute-done.1
  231.4 0.4 fusion.8
  231.9 31.6 %all_to_all.21 = bf16[16,4,32,256]{3,2,0,1:T(8,128)(2,1)S(1)} all-to-all(bf16[16,4,32,256]{3,2,0,1:T(8,128)(2,1)S(1)} %fusion.8), channel_id=1, replica_groups=mesh['blk'=64,'ylo'=4,'core'=2] {'ylo'}, dimensions={1} | all-to-all | bytes 2097152 | tf_op jit(solution)/shard_map/all_to_all | solution.py:65
  263.5 0.2 reduce_sum.12
  263.7 0.9 copy.61
  264.6 0.0 reduce-scatter.2.cloned.1.call-done
Async XLA Ops:
  7.2 44.8 %copy-start = (bf16[4096,256]{1,0:T(8,128)(2,1)S(1)}, bf16[4096,256]{1,0:T(8,128)(2,1)}, u32[]{:S(2)}) copy-start(bf16[4096,256]{1,0:T(8,128)(2,1)} %param.4) | copy-start | bytes 6291460
  9.3 29.0 %all-to-all-start = ((bf16[4,32,16,256]{3,2,1,0:T(8,128)(2,1)}), bf16[4,32,16,256]{3,2,1,0:T(8,128)(2,1)S(1)}, u32[]{:S(2)}, u32[]{:S(2)}) async-start(bf16[4,32,16,256]{3,2,1,0:T(8,128)(2,1)} %broadcast_in_dim.17), calls=%async_computation | async-start | bytes 2097152 | tf_op jit(solution)/shard_map/all_to_all | solution.py:46
  14.8 47.2 %all-gather.2.cloned.1.call-start = ((), (), s32[]{:S(2)}) async-start(), calls=%async_computation.5 | async-start | bytes 2359296 | tf_op jit(solution)/shard_map/all_gather | solution.py:82
  38.4 12.2 %collective-permute-start = (bf16[4,32,16,256]{3,2,1,0:T(8,128)(2,1)S(1)}, bf16[4,32,16,256]{3,2,1,0:T(8,128)(2,1)}, u32[]{:S(2)}, u32[]{:S(2)}) collective-permute-start(bf16[4,32,16,256]{3,2,1,0:T(8,128)(2,1)S(1)} %all-to-all-done), channel_id=1, source_target_pairs={{0,1},{1,0},{2,3},{3,2},{4,5},{5,4},{6,7},{7,6},{8,9},{9,8},{10,11... | collective-permute-start | bytes 3145736 | tf_op jit(solution)/shard_map/ppermute | solution.py:47
  138.4 2.3 copy-start.3
  138.4 3.0 %copy-start.4 = (bf16[4096,256]{1,0:T(8,128)(2,1)S(1)}, bf16[4096,256]{1,0:T(8,128)(2,1)}, u32[]{:S(2)}) copy-start(bf16[4096,256]{1,0:T(8,128)(2,1)} %param.5) | copy-start | bytes 6291460
  138.7 4.4 %copy-start.2 = (bf16[4,64,16,256]{3,2,1,0:T(8,128)(2,1)}, bf16[4,64,16,256]{3,2,1,0:T(8,128)(2,1)S(1)}, u32[]{:S(2)}) copy-start(bf16[4,64,16,256]{3,2,1,0:T(8,128)(2,1)S(1)} %copy.51) | copy-start | bytes 6291460
  143.1 1.4 copy-start.1
  148.5 68.0 %all-to-all-start.2 = ((bf16[4,64,16,256]{3,0,2,1:T(4,128)(2,1)}), bf16[4,64,16,256]{3,0,2,1:T(4,128)(2,1)}, u32[]{:S(2)}, u32[]{:S(2)}) async-start(bf16[4,64,16,256]{3,0,2,1:T(4,128)(2,1)} %copy.54), calls=%async_computation.2 | async-start | bytes 4194304 | tf_op jit(solution)/shard_map/all_to_all | solution.py:105
  156.2 108.4 %reduce-scatter.2.cloned.1.call-start = ((), (), s32[]{:S(2)}) async-start(), calls=%async_computation.6 | async-start | bytes 2359296 | tf_op jit(solution)/shard_map/reduce_scatter | solution.py:101
  220.9 10.6 %collective-permute-start.1 = (bf16[16,4,32,256]{3,2,0,1:T(8,128)(2,1)S(1)}, bf16[16,4,32,256]{3,2,0,1:T(8,128)(2,1)S(1)}, u32[]{:S(2)}, u32[]{:S(2)}) collective-permute-start(bf16[16,4,32,256]{3,2,0,1:T(8,128)(2,1)S(1)} %bitcast.56), channel_id=1, source_target_pairs={{0,1},{1,0},{2,3},{3,2},{4,5},{5,4},{6,7},{7,6},{8,9},{9,8},{10,11... | collective-permute-start | bytes 3145736 | tf_op jit(solution)/shard_map/ppermute | solution.py:63
Sparse Core Ops, SparseCore 0:
  17.7 44.2 all-gather.1
  165.3 60.9 reduce-scatter.1

commit v10 on v9

--- a/solution.py
+++ b/solution.py
@@ -3,6 +3,7 @@
 import jax
 import jax.numpy as jnp
 from jax import lax
+from jax.experimental.layout import Layout, with_layout_constraint
 from jax.sharding import Mesh
 from jax.sharding import PartitionSpec as P
 
@@ -86,6 +87,7 @@
     slope = jnp.transpose(gelu_slope(pre_split).astype(jnp.bfloat16), (2, 1, 0, 3))
     activated, second_full, slope = lax.optimization_barrier((activated, second_full, slope))
     sending = jnp.transpose(activated, (2, 1, 0, 3))
+    sending = with_layout_constraint(sending, Layout((1, 0, 2, 3)))
     received = lax.all_to_all(sending, "blk", split_axis=1, concat_axis=1, tiled=True)
     permuted = received.reshape(block_count, block_size, row_count)
     targets = target_field.reshape(block_count, block_size, row_count)
@@ -102,6 +104,7 @@
         term.astype(jnp.bfloat16), dp, scatter_dimension=0, tiled=True
     )
     back = permuted_grad.reshape(inner_count, blk_count, block_count, row_count)
+    back = with_layout_constraint(back, Layout((1, 0, 2, 3)))
     activated_grad = lax.all_to_all(back, "blk", split_axis=1, concat_axis=1, tiled=True)
     pre_grad = (activated_grad.astype(jnp.float32) * slope).astype(jnp.bfloat16)
     pre_grad = jnp.transpose(pre_grad, (2, 1, 0, 3)).reshape(block_count, block_size, row_count)

time: 272 us -> 267 us (0.982)
  local copies, waits for them, and re-layouts: 22 us -> 16.9 us
where the time goes in v10:
time: 267 us; the launch traced here: 266 us
  blocking collectives  106 us (40%)
  waiting for transfers between devices  81 us (30%)
  starting transfers between devices  31.5 us (12%)
  local copies, waits for them, and re-layouts  16.9 us (6%)
  between operations  14.2 us (5%)
  matrix products  9.36 us (4%)
  other arithmetic  7.96 us (3%)
    all_to_all x1, blocking collectives, shards(): lax.all_to_all(sending, 'blk', split_axis=1, concat_axis=1, tiled=True)  73.9 us
    all_to_all x1, waiting for transfers between devices, shards(): lax.all_to_all(back, 'blk', split_axis=1, concat_axis=1, tiled=True)  51 us
    all_to_all x1, blocking collectives, scatter_rows(): lax.all_to_all(half, 'ylo', split_axis=1, concat_axis=1, tiled=True)  31.6 us
    all_to_all x1, waiting for transfers between devices, gather_rows(): lax.all_to_all(copies, 'ylo', split_axis=0, concat_axis=0, tiled=True)  22.9 us
    ppermute x1, starting transfers between devices, gather_rows(): other = lax.ppermute(line, 'core', swap_pairs(n_core))  9.84 us
    ppermute x1, starting transfers between devices, scatter_rows(): got = lax.ppermute(sent, 'core', swap_pairs(n_core))  8.32 us
    all_to_all x1, starting transfers between devices, shards(): lax.all_to_all(back, 'blk', split_axis=1, concat_axis=1, tiled=True)  7.73 us
    all_to_all x1, starting transfers between devices, gather_rows(): lax.all_to_all(copies, 'ylo', split_axis=0, concat_axis=0, tiled=True)  5.42 us
  transfers between devices with their start and end apart: 6, of which 5 were waited for; matrix products, arithmetic and copies ran while one was open for 9% of the time, Pallas kernels for 0%

profile of v10, /device:TPU:1, one launch (start us, length us, event | category | flops | bytes accessed | tf_op | source)
XLA Modules:
  0.0 266.5 jit_solution(7686284974705807812)
XLA Ops:
  7.2 0.0 copy-start
  7.2 2.2 broadcast_in_dim.17
  9.3 5.4 %all-to-all-start = ((bf16[4,32,16,256]{3,2,1,0:T(8,128)(2,1)}), bf16[4,32,16,256]{3,2,1,0:T(8,128)(2,1)S(1)}, u32[]{:S(2)}, u32[]{:S(2)}) async-start(bf16[4,32,16,256]{3,2,1,0:T(8,128)(2,1)} %broadcast_in_dim.17), calls=%async_computation | async-start | bytes 2097152 | tf_op jit(solution)/shard_map/all_to_all | solution.py:47
  14.8 0.0 all-gather.2.cloned.1.call-start
  14.8 0.7 all-gather.2.cloned.1.call-update
  15.5 22.9 %all-to-all-done = bf16[4,32,16,256]{3,2,1,0:T(8,128)(2,1)S(1)} async-done(((bf16[4,32,16,256]{3,2,1,0:T(8,128)(2,1)}), bf16[4,32,16,256]{3,2,1,0:T(8,128)(2,1)S(1)}, u32[]{:S(2)}, u32[]{:S(2)}) %all-to-all-start) | async-done | bytes 1048608 | tf_op jit(solution)/shard_map/all_to_all | solution.py:47
  38.4 9.8 %collective-permute-start = (bf16[4,32,16,256]{3,2,1,0:T(8,128)(2,1)S(1)}, bf16[4,32,16,256]{3,2,1,0:T(8,128)(2,1)}, u32[]{:S(2)}, u32[]{:S(2)}) collective-permute-start(bf16[4,32,16,256]{3,2,1,0:T(8,128)(2,1)S(1)} %all-to-all-done), channel_id=1, source_target_pairs={{0,1},{1,0},{2,3},{3,2},{4,5},{5,4},{6,7},{7,6},{8,9},{9,8},{10,11... | collective-permute-start | bytes 3145736 | tf_op jit(solution)/shard_map/ppermute | solution.py:48
  48.2 0.2 broadcast_in_dim.16
  48.4 0.1 bitcast_dynamic-update-slice_fusion.1
  48.5 2.1 collective-permute-done
  50.6 1.3 bitcast_dynamic-update-slice_fusion
  51.9 0.0 copy-done
  51.9 1.5 fusion.11
  53.5 2.4 copy.26
  55.9 4.2 %fusion.13 = (bf16[4,64,16,256]{3,2,0,1:T(8,128)(2,1)}, bf16[16,64,4,256]{3,0,2,1:T(8,128)(2,1)}) fusion(f32[16,64,4,256]{3,0,2,1:T(8,128)S(1)} %bitcast.46), kind=kLoop, calls=%fused_computation.20 | loop fusion | flops 20971520 | bytes 8388608 | tf_op jit(solution)/shard_map/transpose | solution.py:87
  60.0 1.9 all-gather.2.cloned.1.call-done
  62.0 73.9 %all_to_all.20 = bf16[4,64,16,256]{3,2,0,1:T(8,128)(2,1)S(1)} all-to-all(bf16[4,64,16,256]{3,2,0,1:T(8,128)(2,1)} %bitcast.52), channel_id=1, replica_groups=mesh['blk'=64,'ylo'=4,'core'=2] {'blk'}, dimensions={1} | all-to-all | bytes 4194304 | tf_op jit(solution)/shard_map/all_to_all | solution.py:91
  135.9 0.0 copy-start.3
  135.9 0.0 copy-start.4
  135.9 0.2 copy.27
  136.1 0.0 copy-start.2
  136.1 2.2 copy-done.3
  138.3 0.6 copy-done.4
  138.9 1.7 fusion.7
  140.6 0.0 copy-done.2
  140.6 0.0 copy-start.1
  140.6 0.9 convolution_convert_fusion
  141.5 0.5 copy-done.1
  142.0 1.6 copy.30
  143.6 7.7 %all-to-all-start.2 = ((bf16[4,64,16,256]{3,2,0,1:T(8,128)(2,1)}), bf16[4,64,16,256]{3,2,0,1:T(8,128)(2,1)}, u32[]{:S(2)}, u32[]{:S(2)}) async-start(bf16[4,64,16,256]{3,2,0,1:T(8,128)(2,1)} %copy.30), calls=%async_computation.2 | async-start | bytes 4194304 | tf_op jit(solution)/shard_map/all_to_all | solution.py:108
  151.3 0.2 reduce-scatter.2.cloned.1.call-start
  151.5 4.3 %convert_bitcast_fusion = bf16[256,16,256]{0,2,1:T(8,128)(2,1)} fusion(bf16[16,256,256]{2,1,0:T(8,128)(2,1)} %copy-done.1, bf16[16,256,256]{2,1,0:T(8,128)(2,1)} %bitcast.45), kind=kOutput, calls=%fused_computation.19 | convolution fusion | flops 537919488 | bytes 6291456 | tf_op jit(solution)/shard_map/qcr,qjr->cqj/dot_general | solution.py:102
  155.8 4.6 %copy.35 = bf16[256,16,256]{2,1,0:T(8,128)(2,1)} copy(bf16[256,16,256]{0,2,1:T(8,128)(2,1)} %convert_bitcast_fusion) | data formatting | bytes 4194304 | tf_op jit(solution)/shard_map/convert_element_type | solution.py:104
  160.4 0.0 reduce-scatter.2.cloned.1.call-update
  160.4 51.0 %all-to-all-done.2 = bf16[4,64,16,256]{3,2,0,1:T(8,128)(2,1)} async-done(((bf16[4,64,16,256]{3,2,0,1:T(8,128)(2,1)}), bf16[4,64,16,256]{3,2,0,1:T(8,128)(2,1)}, u32[]{:S(2)}, u32[]{:S(2)}) %all-to-all-start.2) | async-done | bytes 2097184 | tf_op jit(solution)/shard_map/all_to_all | solution.py:108
  211.5 3.2 %multiply_convert_fusion = bf16[4,64,16,256]{3,2,0,1:T(8,128)(2,1)S(1)} fusion(bf16[4,64,16,256]{3,2,0,1:T(8,128)(2,1)} %get-tuple-element.7, bf16[4,64,16,256]{3,2,0,1:T(8,128)(2,1)} %all-to-all-done.2), kind=kLoop, calls=%fused_computation.11 | loop fusion | flops 4194304 | bytes 6291456 | tf_op jit(solution)/shard_map/convert_element_type | solution.py:109
  214.7 1.0 fusion.14
  215.7 0.2 constant_dynamic-slice_fusion.1
  215.9 0.1 copy.53
  215.9 8.3 %collective-permute-start.1 = (bf16[16,4,32,256]{3,2,0,1:T(8,128)(2,1)S(1)}, bf16[16,4,32,256]{3,2,0,1:T(8,128)(2,1)S(1)}, u32[]{:S(2)}, u32[]{:S(2)}) collective-permute-start(bf16[16,4,32,256]{3,2,0,1:T(8,128)(2,1)S(1)} %bitcast.56), channel_id=1, source_target_pairs={{0,1},{1,0},{2,3},{3,2},{4,5},{5,4},{6,7},{7,6},{8,9},{9,8},{10,11... | collective-permute-start | bytes 3145736 | tf_op jit(solution)/shard_map/ppermute | solution.py:64
  224.3 2.3 collective-permute-done.1
  226.5 0.4 fusion.8
  227.0 31.6 %all_to_all.21 = bf16[16,4,32,256]{3,2,0,1:T(8,128)(2,1)S(1)} all-to-all(bf16[16,4,32,256]{3,2,0,1:T(8,128)(2,1)S(1)} %fusion.8), channel_id=1, replica_groups=mesh['blk'=64,'ylo'=4,'core'=2] {'ylo'}, dimensions={1} | all-to-all | bytes 2097152 | tf_op jit(solution)/shard_map/all_to_all | solution.py:66
  258.6 0.2 reduce_sum.12
  258.8 0.9 copy.36
  259.6 0.0 reduce-scatter.2.cloned.1.call-done
Async XLA Ops:
  7.2 44.8 %copy-start = (bf16[4096,256]{1,0:T(8,128)(2,1)S(1)}, bf16[4096,256]{1,0:T(8,128)(2,1)}, u32[]{:S(2)}) copy-start(bf16[4096,256]{1,0:T(8,128)(2,1)} %param.4) | copy-start | bytes 6291460
  9.3 29.0 %all-to-all-start = ((bf16[4,32,16,256]{3,2,1,0:T(8,128)(2,1)}), bf16[4,32,16,256]{3,2,1,0:T(8,128)(2,1)S(1)}, u32[]{:S(2)}, u32[]{:S(2)}) async-start(bf16[4,32,16,256]{3,2,1,0:T(8,128)(2,1)} %broadcast_in_dim.17), calls=%async_computation | async-start | bytes 2097152 | tf_op jit(solution)/shard_map/all_to_all | solution.py:47
  14.8 47.2 %all-gather.2.cloned.1.call-start = ((), (), s32[]{:S(2)}) async-start(), calls=%async_computation.5 | async-start | bytes 2359296 | tf_op jit(solution)/shard_map/all_gather | solution.py:83
  38.4 12.2 %collective-permute-start = (bf16[4,32,16,256]{3,2,1,0:T(8,128)(2,1)S(1)}, bf16[4,32,16,256]{3,2,1,0:T(8,128)(2,1)}, u32[]{:S(2)}, u32[]{:S(2)}) collective-permute-start(bf16[4,32,16,256]{3,2,1,0:T(8,128)(2,1)S(1)} %all-to-all-done), channel_id=1, source_target_pairs={{0,1},{1,0},{2,3},{3,2},{4,5},{5,4},{6,7},{7,6},{8,9},{9,8},{10,11... | collective-permute-start | bytes 3145736 | tf_op jit(solution)/shard_map/ppermute | solution.py:48
  135.9 2.3 copy-start.3
  135.9 3.0 %copy-start.4 = (bf16[4096,256]{1,0:T(8,128)(2,1)S(1)}, bf16[4096,256]{1,0:T(8,128)(2,1)}, u32[]{:S(2)}) copy-start(bf16[4096,256]{1,0:T(8,128)(2,1)} %param.5) | copy-start | bytes 6291460
  136.1 4.5 %copy-start.2 = (bf16[4,64,16,256]{3,2,1,0:T(8,128)(2,1)}, bf16[4,64,16,256]{3,2,1,0:T(8,128)(2,1)S(1)}, u32[]{:S(2)}) copy-start(bf16[4,64,16,256]{3,2,1,0:T(8,128)(2,1)S(1)} %copy.27) | copy-start | bytes 6291460
  140.6 1.4 copy-start.1
  143.6 67.9 %all-to-all-start.2 = ((bf16[4,64,16,256]{3,2,0,1:T(8,128)(2,1)}), bf16[4,64,16,256]{3,2,0,1:T(8,128)(2,1)}, u32[]{:S(2)}, u32[]{:S(2)}) async-start(bf16[4,64,16,256]{3,2,0,1:T(8,128)(2,1)} %copy.30), calls=%async_computation.2 | async-start | bytes 4194304 | tf_op jit(solution)/shard_map/all_to_all | solution.py:108
  151.3 108.4 %reduce-scatter.2.cloned.1.call-start = ((), (), s32[]{:S(2)}) async-start(), calls=%async_computation.6 | async-start | bytes 2359296 | tf_op jit(solution)/shard_map/reduce_scatter | solution.py:103
  215.9 10.6 %collective-permute-start.1 = (bf16[16,4,32,256]{3,2,0,1:T(8,128)(2,1)S(1)}, bf16[16,4,32,256]{3,2,0,1:T(8,128)(2,1)S(1)}, u32[]{:S(2)}, u32[]{:S(2)}) collective-permute-start(bf16[16,4,32,256]{3,2,0,1:T(8,128)(2,1)S(1)} %bitcast.56), channel_id=1, source_target_pairs={{0,1},{1,0},{2,3},{3,2},{4,5},{5,4},{6,7},{7,6},{8,9},{9,8},{10,11... | collective-permute-start | bytes 3145736 | tf_op jit(solution)/shard_map/ppermute | solution.py:64
Sparse Core Ops, SparseCore 0:
  17.7 44.2 all-gather.1
  160.6 60.7 reduce-scatter.1

commit v11 on v10

--- a/solution.py
+++ b/solution.py
@@ -43,8 +43,11 @@
     n_core = lax.axis_size("core")
     n_ylo = lax.axis_size("ylo")
     c = lax.axis_index("core")
-    copies = jnp.broadcast_to(piece[None], (n_ylo,) + piece.shape)
-    line = lax.all_to_all(copies, "ylo", split_axis=0, concat_axis=0, tiled=True)
+    y = lax.axis_index("ylo")
+    right = [lax.ppermute(piece, "ylo", line_pairs(n_ylo, s)) for s in range(n_ylo - 1, 0, -1)]
+    left = [lax.ppermute(piece, "ylo", line_pairs(n_ylo, -s)) for s in range(1, n_ylo)]
+    stacked = jnp.stack(right + [piece] + left)
+    line = lax.dynamic_slice_in_dim(stacked, n_ylo - 1 - y, n_ylo, axis=0)
     other = lax.ppermute(line, "core", swap_pairs(n_core))
     pair = jnp.zeros((n_ylo, n_core) + piece.shape, piece.dtype)
     pair = lax.dynamic_update_index_in_dim(pair, line, c, 1)

time: 267 us -> 272 us (1.019)
  blocking collectives: 106 us -> 102 us
    all_to_all x1 -> x0, waiting for transfers between devices: 22.9 us -> none  [gather_rows(): lax.all_to_all(copies, 'ylo', split_axis=0, concat_axis=0, tiled=True)]
    ppermute x0 -> x6, waiting for transfers between devices: none -> 19.7 us  [the longest x3 13.7 us: gather_rows(): lax.ppermute(piece, 'ylo', line_pairs(n_ylo, -s))]
    ppermute x0 -> x6, starting transfers between devices: none -> 15.4 us  [the longest x3 11.5 us: gather_rows(): lax.ppermute(piece, 'ylo', line_pairs(n_ylo, s))]
    ppermute x1, starting transfers between devices: 9.84 us -> 2.59 us  [gather_rows(): other = lax.ppermute(line, 'core', swap_pairs(n_core))]
    all_to_all x1 -> x0, starting transfers between devices: 5.42 us -> none  [gather_rows(): lax.all_to_all(copies, 'ylo', split_axis=0, concat_axis=0, tiled=True)]
    all_to_all x1, waiting for transfers between devices: 51 us -> 55 us  [shards(): lax.all_to_all(back, 'blk', split_axis=1, concat_axis=1, tiled=True)]
    all_to_all x1, blocking collectives: 31.6 us -> 27.9 us  [scatter_rows(): lax.all_to_all(half, 'ylo', split_axis=1, concat_axis=1, tiled=True)]
    ppermute x1, starting transfers between devices: 8.32 us -> 5.2 us  [scatter_rows(): got = lax.ppermute(sent, 'core', swap_pairs(n_core))]
  transfers between devices with their start and end apart: 6 -> 11, of which waited for: 5 -> 7; matrix products, arithmetic and copies ran while one was open for 9% -> 11% of each run, Pallas kernels for 0% -> 0%
where the time goes in v11:
time: 272 us; the launch traced here: 269 us
  blocking collectives  102 us (38%)
  waiting for transfers between devices  83 us (31%)
  starting transfers between devices  32.7 us (12%)
  local copies, waits for them, and re-layouts  18.4 us (7%)
  between operations  14.3 us (5%)
  matrix products  11 us (4%)
  other arithmetic  7.96 us (3%)
    all_to_all x1, blocking collectives, shards(): lax.all_to_all(sending, 'blk', split_axis=1, concat_axis=1, tiled=True)  73.7 us
    all_to_all x1, waiting for transfers between devices, shards(): lax.all_to_all(back, 'blk', split_axis=1, concat_axis=1, tiled=True)  55 us
    all_to_all x1, blocking collectives, scatter_rows(): lax.all_to_all(half, 'ylo', split_axis=1, concat_axis=1, tiled=True)  27.9 us
    ppermute x3, waiting for transfers between devices, gather_rows(): lax.ppermute(piece, 'ylo', line_pairs(n_ylo, -s))  13.7 us
    ppermute x3, starting transfers between devices, gather_rows(): lax.ppermute(piece, 'ylo', line_pairs(n_ylo, s))  11.5 us
    all_to_all x1, starting transfers between devices, shards(): lax.all_to_all(back, 'blk', split_axis=1, concat_axis=1, tiled=True)  9.28 us
    ppermute x3, waiting for transfers between devices, gather_rows(): lax.ppermute(piece, 'ylo', line_pairs(n_ylo, s))  6.05 us
  transfers between devices with their start and end apart: 11, of which 7 were waited for; matrix products, arithmetic and copies ran while one was open for 11% of the time, Pallas kernels for 0%

profile of v11, /device:TPU:1, one launch (start us, length us, event | category | flops | bytes accessed | tf_op | source)
XLA Modules:
  0.0 268.9 jit_solution(11198812623295776813)
XLA Ops:
  7.2 0.0 copy-start
  7.2 0.0 all-gather.2.cloned.1.call-start
  7.2 6.2 %collective-permute-start = (bf16[32,16,256]{2,1,0:T(8,128)(2,1)}, bf16[32,16,256]{2,1,0:T(8,128)(2,1)S(1)}, u32[]{:S(2)}, u32[]{:S(2)}) collective-permute-start(bf16[32,16,256]{2,1,0:T(8,128)(2,1)} %param.6), channel_id=1, source_target_pairs={{0,6},{1,7},{8,14},{9,15},{16,22},{17,23},{24,30},{25,31},{32,38},... | collective-permute-start | bytes 786440 | tf_op jit(solution)/shard_map/ppermute | solution.py:47
  13.4 1.3 collective-permute-start.1
  14.8 1.3 collective-permute-start.3
  16.1 4.0 %collective-permute-start.2 = (bf16[32,16,256]{2,1,0:T(8,128)(2,1)}, bf16[32,16,256]{2,1,0:T(8,128)(2,1)S(1)}, u32[]{:S(2)}, u32[]{:S(2)}) collective-permute-start(bf16[32,16,256]{2,1,0:T(8,128)(2,1)} %param.6), channel_id=1, source_target_pairs={{0,2},{2,4},{4,6},{1,3},{3,5},{5,7},{8,10},{10,12},{12,14},{9,11},... | collective-permute-start | bytes 786440 | tf_op jit(solution)/shard_map/ppermute | solution.py:47
  20.1 1.3 collective-permute-start.5
  21.4 0.0 all-gather.2.cloned.1.call-update
  21.4 0.0 collective-permute-done
  21.4 1.3 collective-permute-start.4
  22.7 0.5 collective-permute-done.1
  23.2 5.6 %collective-permute-done.2 = bf16[32,16,256]{2,1,0:T(8,128)(2,1)S(1)} collective-permute-done((bf16[32,16,256]{2,1,0:T(8,128)(2,1)}, bf16[32,16,256]{2,1,0:T(8,128)(2,1)S(1)}, u32[]{:S(2)}, u32[]{:S(2)}) %collective-permute-start.2) | collective-permute-done | bytes 262176 | tf_op jit(solution)/shard_map/ppermute | solution.py:47
  28.8 1.0 bitcast_dynamic-update-slice_fusion.5
  29.8 0.0 collective-permute-done.3
  29.8 13.7 %collective-permute-done.4 = bf16[32,16,256]{2,1,0:T(8,128)(2,1)S(1)} collective-permute-done((bf16[32,16,256]{2,1,0:T(8,128)(2,1)}, bf16[32,16,256]{2,1,0:T(8,128)(2,1)S(1)}, u32[]{:S(2)}, u32[]{:S(2)}) %collective-permute-start.4) | collective-permute-done | bytes 262176 | tf_op jit(solution)/shard_map/ppermute | solution.py:48
  43.5 0.0 collective-permute-done.5
  43.6 1.5 broadcast_in_dim.10
  45.1 1.5 bitcast_dynamic-update-slice_fusion.1
  46.6 2.6 collective-permute-start.6
  49.2 2.5 collective-permute-done.6
  51.7 1.1 bitcast_dynamic-update-slice_fusion
  52.7 0.0 copy-done
  52.7 3.1 %fusion.11 = f32[16,256,256]{2,1,0:T(8,128)S(1)} fusion(bf16[16,256,256]{2,1,0:T(8,128)(2,1)S(1)} %bitcast.52, bf16[256,16,256]{2,1,0:T(8,128)(2,1)} %bitcast.9), kind=kOutput, calls=%fused_computation.17 | convolution fusion | flops 536870912 | bytes 8388608 | tf_op jit(solution)/shard_map/bkr,kbi->bir/dot_general | solution.py:87
  55.9 2.4 copy.22
  58.3 4.2 %fusion.13 = (bf16[4,64,16,256]{3,2,0,1:T(8,128)(2,1)}, bf16[16,64,4,256]{3,0,2,1:T(8,128)(2,1)}) fusion(f32[16,64,4,256]{3,0,2,1:T(8,128)S(1)} %bitcast.56), kind=kLoop, calls=%fused_computation.20 | loop fusion | flops 20971520 | bytes 8388608 | tf_op jit(solution)/shard_map/transpose | solution.py:90
  62.5 3.4 %all-gather.2.cloned.1.call-done = bf16[256,16,256]{2,1,0:T(8,128)(2,1)} async-done(((bf16[32,16,256]{2,1,0:T(8,128)(2,1)}), bf16[256,16,256]{2,1,0:T(8,128)(2,1)}) %all-gather.2.cloned.1.call-update) | async-done | bytes 2097168 | tf_op jit(solution)/shard_map/all_gather | solution.py:86
  65.9 73.7 %all_to_all.15 = bf16[4,64,16,256]{3,2,0,1:T(8,128)(2,1)S(1)} all-to-all(bf16[4,64,16,256]{3,2,0,1:T(8,128)(2,1)} %bitcast.62), channel_id=1, replica_groups=mesh['blk'=64,'ylo'=4,'core'=2] {'blk'}, dimensions={1} | all-to-all | bytes 4194304 | tf_op jit(solution)/shard_map/all_to_all | solution.py:94
  139.6 0.0 copy-start.3
  139.6 0.0 copy-start.4
  139.6 0.2 copy.23
  139.7 0.0 copy-start.2
  139.7 2.2 copy-done.3
  141.9 0.6 copy-done.4
  142.5 1.7 fusion.7
  144.2 0.0 copy-done.2
  144.2 0.0 copy-start.1
  144.3 0.9 convolution_convert_fusion
  145.1 0.5 copy-done.1
  145.6 1.6 copy.26
  147.3 9.3 %all-to-all-start.1 = ((bf16[4,64,16,256]{3,2,0,1:T(8,128)(2,1)}), bf16[4,64,16,256]{3,2,0,1:T(8,128)(2,1)}, u32[]{:S(2)}, u32[]{:S(2)}) async-start(bf16[4,64,16,256]{3,2,0,1:T(8,128)(2,1)} %copy.26), calls=%async_computation.1 | async-start | bytes 4194304 | tf_op jit(solution)/shard_map/all_to_all | solution.py:111
  156.5 0.2 reduce-scatter.2.cloned.1.call-start
  156.8 4.3 %convert_bitcast_fusion = bf16[256,16,256]{0,2,1:T(8,128)(2,1)} fusion(bf16[16,256,256]{2,1,0:T(8,128)(2,1)} %copy-done.1, bf16[16,256,256]{2,1,0:T(8,128)(2,1)} %bitcast.55), kind=kOutput, calls=%fused_computation.19 | convolution fusion | flops 537919488 | bytes 6291456 | tf_op jit(solution)/shard_map/qcr,qjr->cqj/dot_general | solution.py:105
  161.1 4.6 %copy.31 = bf16[256,16,256]{2,1,0:T(8,128)(2,1)} copy(bf16[256,16,256]{0,2,1:T(8,128)(2,1)} %convert_bitcast_fusion) | data formatting | bytes 4194304 | tf_op jit(solution)/shard_map/convert_element_type | solution.py:107
  165.7 0.0 reduce-scatter.2.cloned.1.call-update
  165.7 55.0 %all-to-all-done.1 = bf16[4,64,16,256]{3,2,0,1:T(8,128)(2,1)} async-done(((bf16[4,64,16,256]{3,2,0,1:T(8,128)(2,1)}), bf16[4,64,16,256]{3,2,0,1:T(8,128)(2,1)}, u32[]{:S(2)}, u32[]{:S(2)}) %all-to-all-start.1) | async-done | bytes 2097184 | tf_op jit(solution)/shard_map/all_to_all | solution.py:111
  220.7 3.2 %multiply_convert_fusion = bf16[4,64,16,256]{3,2,0,1:T(8,128)(2,1)S(1)} fusion(bf16[4,64,16,256]{3,2,0,1:T(8,128)(2,1)} %get-tuple-element.7, bf16[4,64,16,256]{3,2,0,1:T(8,128)(2,1)} %all-to-all-done.1), kind=kLoop, calls=%fused_computation.11 | loop fusion | flops 4194304 | bytes 6291456 | tf_op jit(solution)/shard_map/convert_element_type | solution.py:112
  223.9 1.0 fusion.14
  224.9 0.2 constant_dynamic-slice_fusion.1
  225.1 0.1 copy.49
  225.2 5.2 %collective-permute-start.7 = (bf16[16,4,32,256]{3,2,0,1:T(8,128)(2,1)S(1)}, bf16[16,4,32,256]{3,2,0,1:T(8,128)(2,1)S(1)}, u32[]{:S(2)}, u32[]{:S(2)}) collective-permute-start(bf16[16,4,32,256]{3,2,0,1:T(8,128)(2,1)S(1)} %bitcast.65), channel_id=1, source_target_pairs={{0,1},{1,0},{2,3},{3,2},{4,5},{5,4},{6,7},{7,6},{8,9},{9,8},{10,11... | collective-permute-start | bytes 3145736 | tf_op jit(solution)/shard_map/ppermute | solution.py:67
  230.4 2.3 collective-permute-done.7
  232.7 0.4 fusion.8
  233.1 27.9 %all_to_all.16 = bf16[16,4,32,256]{3,2,0,1:T(8,128)(2,1)S(1)} all-to-all(bf16[16,4,32,256]{3,2,0,1:T(8,128)(2,1)S(1)} %fusion.8), channel_id=1, replica_groups=mesh['blk'=64,'ylo'=4,'core'=2] {'ylo'}, dimensions={1} | all-to-all | bytes 2097152 | tf_op jit(solution)/shard_map/all_to_all | solution.py:69
  261.0 0.2 reduce_sum.12
  261.2 0.9 copy.32
  262.1 0.0 reduce-scatter.2.cloned.1.call-done
  (6 shorter events, 0.1 us)
Async XLA Ops:
  7.2 45.6 %copy-start = (bf16[4096,256]{1,0:T(8,128)(2,1)S(1)}, bf16[4096,256]{1,0:T(8,128)(2,1)}, u32[]{:S(2)}) copy-start(bf16[4096,256]{1,0:T(8,128)(2,1)} %param.4) | copy-start | bytes 6291460
  7.2 58.7 %all-gather.2.cloned.1.call-start = ((), (), s32[]{:S(2)}) async-start(), calls=%async_computation.4 | async-start | bytes 2359296 | tf_op jit(solution)/shard_map/all_gather | solution.py:86
  7.2 14.2 %collective-permute-start = (bf16[32,16,256]{2,1,0:T(8,128)(2,1)}, bf16[32,16,256]{2,1,0:T(8,128)(2,1)S(1)}, u32[]{:S(2)}, u32[]{:S(2)}) collective-permute-start(bf16[32,16,256]{2,1,0:T(8,128)(2,1)} %param.6), channel_id=1, source_target_pairs={{0,6},{1,7},{8,14},{9,15},{16,22},{17,23},{24,30},{25,31},{32,38},... | collective-permute-start | bytes 786440 | tf_op jit(solution)/shard_map/ppermute | solution.py:47
  13.4 9.7 %collective-permute-start.1 = (bf16[32,16,256]{2,1,0:T(8,128)(2,1)}, bf16[32,16,256]{2,1,0:T(8,128)(2,1)S(1)}, u32[]{:S(2)}, u32[]{:S(2)}) collective-permute-start(bf16[32,16,256]{2,1,0:T(8,128)(2,1)} %param.6), channel_id=1, source_target_pairs={{0,4},{2,6},{1,5},{3,7},{8,12},{10,14},{9,13},{11,15},{16,20},{18,... | collective-permute-start | bytes 786440 | tf_op jit(solution)/shard_map/ppermute | solution.py:47
  14.8 15.0 %collective-permute-start.3 = (bf16[32,16,256]{2,1,0:T(8,128)(2,1)}, bf16[32,16,256]{2,1,0:T(8,128)(2,1)S(1)}, u32[]{:S(2)}, u32[]{:S(2)}) collective-permute-start(bf16[32,16,256]{2,1,0:T(8,128)(2,1)} %param.6), channel_id=1, source_target_pairs={{2,0},{4,2},{6,4},{3,1},{5,3},{7,5},{10,8},{12,10},{14,12},{11,9},... | collective-permute-start | bytes 786440 | tf_op jit(solution)/shard_map/ppermute | solution.py:48
  16.1 12.8 %collective-permute-start.2 = (bf16[32,16,256]{2,1,0:T(8,128)(2,1)}, bf16[32,16,256]{2,1,0:T(8,128)(2,1)S(1)}, u32[]{:S(2)}, u32[]{:S(2)}) collective-permute-start(bf16[32,16,256]{2,1,0:T(8,128)(2,1)} %param.6), channel_id=1, source_target_pairs={{0,2},{2,4},{4,6},{1,3},{3,5},{5,7},{8,10},{10,12},{12,14},{9,11},... | collective-permute-start | bytes 786440 | tf_op jit(solution)/shard_map/ppermute | solution.py:47
  20.1 23.5 %collective-permute-start.5 = (bf16[32,16,256]{2,1,0:T(8,128)(2,1)}, bf16[32,16,256]{2,1,0:T(8,128)(2,1)S(1)}, u32[]{:S(2)}, u32[]{:S(2)}) collective-permute-start(bf16[32,16,256]{2,1,0:T(8,128)(2,1)} %param.6), channel_id=1, source_target_pairs={{6,0},{7,1},{14,8},{15,9},{22,16},{23,17},{30,24},{31,25},{38,32},... | collective-permute-start | bytes 786440 | tf_op jit(solution)/shard_map/ppermute | solution.py:48
  21.4 22.1 %collective-permute-start.4 = (bf16[32,16,256]{2,1,0:T(8,128)(2,1)}, bf16[32,16,256]{2,1,0:T(8,128)(2,1)S(1)}, u32[]{:S(2)}, u32[]{:S(2)}) collective-permute-start(bf16[32,16,256]{2,1,0:T(8,128)(2,1)} %param.6), channel_id=1, source_target_pairs={{4,0},{6,2},{5,1},{7,3},{12,8},{14,10},{13,9},{15,11},{20,16},{22,... | collective-permute-start | bytes 786440 | tf_op jit(solution)/shard_map/ppermute | solution.py:48
  46.6 5.1 %collective-permute-start.6 = (bf16[4,32,16,256]{3,2,1,0:T(8,128)(2,1)}, bf16[4,32,16,256]{3,2,1,0:T(8,128)(2,1)S(1)}, u32[]{:S(2)}, u32[]{:S(2)}) collective-permute-start(bf16[4,32,16,256]{3,2,1,0:T(8,128)(2,1)} %get-tuple-element.15), channel_id=1, source_target_pairs={{0,1},{1,0},{2,3},{3,2},{4,5},{5,4},{6,7},{7,6},{8,9},{9,8},{10,11... | collective-permute-start | bytes 3145736 | tf_op jit(solution)/shard_map/ppermute | solution.py:51
  139.6 2.3 copy-start.3
  139.6 3.0 %copy-start.4 = (bf16[4096,256]{1,0:T(8,128)(2,1)S(1)}, bf16[4096,256]{1,0:T(8,128)(2,1)}, u32[]{:S(2)}) copy-start(bf16[4096,256]{1,0:T(8,128)(2,1)} %param.5) | copy-start | bytes 6291460
  139.7 4.5 %copy-start.2 = (bf16[4,64,16,256]{3,2,1,0:T(8,128)(2,1)}, bf16[4,64,16,256]{3,2,1,0:T(8,128)(2,1)S(1)}, u32[]{:S(2)}) copy-start(bf16[4,64,16,256]{3,2,1,0:T(8,128)(2,1)S(1)} %copy.23) | copy-start | bytes 6291460
  144.2 1.4 copy-start.1
  147.3 73.5 %all-to-all-start.1 = ((bf16[4,64,16,256]{3,2,0,1:T(8,128)(2,1)}), bf16[4,64,16,256]{3,2,0,1:T(8,128)(2,1)}, u32[]{:S(2)}, u32[]{:S(2)}) async-start(bf16[4,64,16,256]{3,2,0,1:T(8,128)(2,1)} %copy.26), calls=%async_computation.1 | async-start | bytes 4194304 | tf_op jit(solution)/shard_map/all_to_all | solution.py:111
  156.5 105.5 %reduce-scatter.2.cloned.1.call-start = ((), (), s32[]{:S(2)}) async-start(), calls=%async_computation.5 | async-start | bytes 2359296 | tf_op jit(solution)/shard_map/reduce_scatter | solution.py:106
  225.2 7.5 %collective-permute-start.7 = (bf16[16,4,32,256]{3,2,0,1:T(8,128)(2,1)S(1)}, bf16[16,4,32,256]{3,2,0,1:T(8,128)(2,1)S(1)}, u32[]{:S(2)}, u32[]{:S(2)}) collective-permute-start(bf16[16,4,32,256]{3,2,0,1:T(8,128)(2,1)S(1)} %bitcast.65), channel_id=1, source_target_pairs={{0,1},{1,0},{2,3},{3,2},{4,5},{5,4},{6,7},{7,6},{8,9},{9,8},{10,11... | collective-permute-start | bytes 3145736 | tf_op jit(solution)/shard_map/ppermute | solution.py:67
Sparse Core Ops, SparseCore 0:
  21.5 44.3 all-gather.1
  165.8 58.2 reduce-scatter.1

commit v12 on v10

--- a/solution.py
+++ b/solution.py
@@ -85,17 +85,19 @@
     pre_split = pre_act.reshape(block_count, blk_count, inner_count, row_count)
     activated = gelu_value(pre_split).astype(jnp.bfloat16)
     slope = jnp.transpose(gelu_slope(pre_split).astype(jnp.bfloat16), (2, 1, 0, 3))
-    activated, second_full, slope = lax.optimization_barrier((activated, second_full, slope))
+    targets = target_field.reshape(block_count, block_size, row_count).astype(jnp.float32)
+    activated, second_full, slope, targets = lax.optimization_barrier(
+        (activated, second_full, slope, targets)
+    )
     sending = jnp.transpose(activated, (2, 1, 0, 3))
     sending = with_layout_constraint(sending, Layout((1, 0, 2, 3)))
     received = lax.all_to_all(sending, "blk", split_axis=1, concat_axis=1, tiled=True)
     permuted = received.reshape(block_count, block_size, row_count)
-    targets = target_field.reshape(block_count, block_size, row_count)
     second_t = jnp.transpose(second_full, (1, 0, 2))
     predicted = jnp.einsum(
         "qcj,qcr->qjr", second_t, permuted, preferred_element_type=jnp.float32
     )
-    residual = ((predicted - targets.astype(jnp.float32)) * scale_factor).astype(jnp.bfloat16)
+    residual = ((predicted - targets) * scale_factor).astype(jnp.bfloat16)
     permuted_grad = jnp.einsum(
         "qcj,qjr->qcr", second_t, residual, preferred_element_type=jnp.float32
     ).astype(jnp.bfloat16)

time: 267 us -> 270 us (1.011)
  other arithmetic: 7.96 us -> 12 us
    all_to_all x1, waiting for transfers between devices: 51 us -> 55.3 us  [shards(): lax.all_to_all(back, 'blk', split_axis=1, concat_axis=1, tiled=True)]
    convert_element_type x0 -> x1, other arithmetic: none -> 4.01 us  [shards(): target_field.reshape(block_count, block_size, row_count).astype(jnp.float32)]
    ppermute x1, starting transfers between devices: 8.32 us -> 4.62 us  [scatter_rows(): got = lax.ppermute(sent, 'core', swap_pairs(n_core))]
  transfers between devices with their start and end apart: 6 -> 6, of which waited for: 5 -> 3; matrix products, arithmetic and copies ran while one was open for 9% -> 11% of each run, Pallas kernels for 0% -> 0%
where the time goes in v12:
time: 270 us; the launch traced here: 269 us
  blocking collectives  106 us (39%)
  waiting for transfers between devices  81.2 us (30%)
  starting transfers between devices  29.1 us (11%)
  local copies, waits for them, and re-layouts  16.8 us (6%)
  between operations  14.2 us (5%)
  other arithmetic  12 us (4%)
  matrix products  9.43 us (3%)
    all_to_all x1, blocking collectives, shards(): lax.all_to_all(sending, 'blk', split_axis=1, concat_axis=1, tiled=True)  75 us
    all_to_all x1, waiting for transfers between devices, shards(): lax.all_to_all(back, 'blk', split_axis=1, concat_axis=1, tiled=True)  55.3 us
    all_to_all x1, blocking collectives, scatter_rows(): lax.all_to_all(half, 'ylo', split_axis=1, concat_axis=1, tiled=True)  30.8 us
    all_to_all x1, waiting for transfers between devices, gather_rows(): lax.all_to_all(copies, 'ylo', split_axis=0, concat_axis=0, tiled=True)  22.9 us
    ppermute x1, starting transfers between devices, gather_rows(): other = lax.ppermute(line, 'core', swap_pairs(n_core))  9.84 us
    all_to_all x1, starting transfers between devices, shards(): lax.all_to_all(back, 'blk', split_axis=1, concat_axis=1, tiled=True)  9.03 us
    all_to_all x1, starting transfers between devices, gather_rows(): lax.all_to_all(copies, 'ylo', split_axis=0, concat_axis=0, tiled=True)  5.42 us
  transfers between devices with their start and end apart: 6, of which 3 were waited for; matrix products, arithmetic and copies ran while one was open for 11% of the time, Pallas kernels for 0%

profile of v12, /device:TPU:1, one launch (start us, length us, event | category | flops | bytes accessed | tf_op | source)
XLA Modules:
  0.0 268.6 jit_solution(11210857098206409368)
XLA Ops:
  7.2 0.0 copy-start
  7.2 2.2 broadcast_in_dim.17
  9.3 5.4 %all-to-all-start = ((bf16[4,32,16,256]{3,2,1,0:T(8,128)(2,1)}), bf16[4,32,16,256]{3,2,1,0:T(8,128)(2,1)S(1)}, u32[]{:S(2)}, u32[]{:S(2)}) async-start(bf16[4,32,16,256]{3,2,1,0:T(8,128)(2,1)} %broadcast_in_dim.17), calls=%async_computation | async-start | bytes 2097152 | tf_op jit(solution)/shard_map/all_to_all | solution.py:47
  14.8 0.0 all-gather.2.cloned.1.call-start
  14.8 0.7 all-gather.2.cloned.1.call-update
  15.5 22.9 %all-to-all-done = bf16[4,32,16,256]{3,2,1,0:T(8,128)(2,1)S(1)} async-done(((bf16[4,32,16,256]{3,2,1,0:T(8,128)(2,1)}), bf16[4,32,16,256]{3,2,1,0:T(8,128)(2,1)S(1)}, u32[]{:S(2)}, u32[]{:S(2)}) %all-to-all-start) | async-done | bytes 1048608 | tf_op jit(solution)/shard_map/all_to_all | solution.py:47
  38.4 9.8 %collective-permute-start = (bf16[4,32,16,256]{3,2,1,0:T(8,128)(2,1)S(1)}, bf16[4,32,16,256]{3,2,1,0:T(8,128)(2,1)}, u32[]{:S(2)}, u32[]{:S(2)}) collective-permute-start(bf16[4,32,16,256]{3,2,1,0:T(8,128)(2,1)S(1)} %all-to-all-done), channel_id=1, source_target_pairs={{0,1},{1,0},{2,3},{3,2},{4,5},{5,4},{6,7},{7,6},{8,9},{9,8},{10,11... | collective-permute-start | bytes 3145736 | tf_op jit(solution)/shard_map/ppermute | solution.py:48
  48.2 4.0 %convert.3 = f32[16,256,256]{2,1,0:T(8,128)} convert(bf16[16,256,256]{2,1,0:T(8,128)(2,1)} %bitcast.54) | non-fusion elementwise | flops 1048576 | bytes 6291456 | tf_op jit(solution)/shard_map/convert_element_type | solution.py:88
  52.2 0.2 broadcast_in_dim.16
  52.4 0.1 bitcast_dynamic-update-slice_fusion.1
  52.5 0.0 collective-permute-done
  52.5 1.3 bitcast_dynamic-update-slice_fusion
  53.9 0.0 copy-done
  53.9 1.5 fusion.9
  55.4 2.4 copy.26
  57.8 4.2 %fusion.11 = (bf16[4,64,16,256]{3,2,0,1:T(8,128)(2,1)}, bf16[16,64,4,256]{3,0,2,1:T(8,128)(2,1)}) fusion(f32[16,64,4,256]{3,0,2,1:T(8,128)S(1)} %bitcast.46), kind=kLoop, calls=%fused_computation.18 | loop fusion | flops 20971520 | bytes 8388608 | tf_op jit(solution)/shard_map/transpose | solution.py:87
  62.0 0.0 all-gather.2.cloned.1.call-done
  62.0 0.0 copy-start.4
  62.0 75.0 %all_to_all.20 = bf16[4,64,16,256]{3,2,0,1:T(8,128)(2,1)S(1)} all-to-all(bf16[4,64,16,256]{3,2,0,1:T(8,128)(2,1)} %bitcast.52), channel_id=1, replica_groups=mesh['blk'=64,'ylo'=4,'core'=2] {'blk'}, dimensions={1} | all-to-all | bytes 4194304 | tf_op jit(solution)/shard_map/all_to_all | solution.py:94
  137.0 0.0 copy-start.3
  137.0 0.2 copy.27
  137.2 0.0 copy-start.2
  137.2 0.0 copy-done.4
  137.2 2.8 %copy-done.3 = f32[16,256,256]{2,1,0:T(8,128)S(1)} copy-done((f32[16,256,256]{2,1,0:T(8,128)S(1)}, f32[16,256,256]{2,1,0:T(8,128)}, u32[]{:S(2)}) %copy-start.3) | copy-done | bytes 4194328
  140.0 1.8 multiply_convert_fusion.1
  141.7 0.0 copy-done.2
  141.7 0.0 copy-start.1
  141.7 0.9 convolution_convert_fusion
  142.6 0.5 copy-done.1
  143.1 1.6 copy.30
  144.6 9.0 %all-to-all-start.2 = ((bf16[4,64,16,256]{3,2,0,1:T(8,128)(2,1)}), bf16[4,64,16,256]{3,2,0,1:T(8,128)(2,1)}, u32[]{:S(2)}, u32[]{:S(2)}) async-start(bf16[4,64,16,256]{3,2,0,1:T(8,128)(2,1)} %copy.30), calls=%async_computation.2 | async-start | bytes 4194304 | tf_op jit(solution)/shard_map/all_to_all | solution.py:110
  153.7 0.2 reduce-scatter.2.cloned.1.call-start
  153.9 4.3 %convert_bitcast_fusion = bf16[256,16,256]{0,2,1:T(8,128)(2,1)} fusion(bf16[16,256,256]{2,1,0:T(8,128)(2,1)} %copy-done.1, bf16[16,256,256]{2,1,0:T(8,128)(2,1)} %bitcast.45), kind=kOutput, calls=%fused_computation.17 | convolution fusion | flops 537919488 | bytes 6291456 | tf_op jit(solution)/shard_map/qcr,qjr->cqj/dot_general | solution.py:104
  158.2 4.6 %copy.35 = bf16[256,16,256]{2,1,0:T(8,128)(2,1)} copy(bf16[256,16,256]{0,2,1:T(8,128)(2,1)} %convert_bitcast_fusion) | data formatting | bytes 4194304 | tf_op jit(solution)/shard_map/convert_element_type | solution.py:106
  162.8 0.0 reduce-scatter.2.cloned.1.call-update
  162.8 55.3 %all-to-all-done.2 = bf16[4,64,16,256]{3,2,0,1:T(8,128)(2,1)} async-done(((bf16[4,64,16,256]{3,2,0,1:T(8,128)(2,1)}), bf16[4,64,16,256]{3,2,0,1:T(8,128)(2,1)}, u32[]{:S(2)}, u32[]{:S(2)}) %all-to-all-start.2) | async-done | bytes 2097184 | tf_op jit(solution)/shard_map/all_to_all | solution.py:110
  218.1 3.2 %multiply_convert_fusion = bf16[4,64,16,256]{3,2,0,1:T(8,128)(2,1)S(1)} fusion(bf16[4,64,16,256]{3,2,0,1:T(8,128)(2,1)} %get-tuple-element.9, bf16[4,64,16,256]{3,2,0,1:T(8,128)(2,1)} %all-to-all-done.2), kind=kLoop, calls=%fused_computation.8 | loop fusion | flops 4194304 | bytes 6291456 | tf_op jit(solution)/shard_map/convert_element_type | solution.py:111
  221.3 1.0 fusion.12
  222.3 0.2 constant_dynamic-slice_fusion.1
  222.5 0.1 copy.53
  222.6 4.6 %collective-permute-start.1 = (bf16[16,4,32,256]{3,2,0,1:T(8,128)(2,1)S(1)}, bf16[16,4,32,256]{3,2,0,1:T(8,128)(2,1)S(1)}, u32[]{:S(2)}, u32[]{:S(2)}) collective-permute-start(bf16[16,4,32,256]{3,2,0,1:T(8,128)(2,1)S(1)} %bitcast.56), channel_id=1, source_target_pairs={{0,1},{1,0},{2,3},{3,2},{4,5},{5,4},{6,7},{7,6},{8,9},{9,8},{10,11... | collective-permute-start | bytes 3145736 | tf_op jit(solution)/shard_map/ppermute | solution.py:64
  227.2 2.3 collective-permute-done.1
  229.5 0.4 fusion.6
  229.9 30.8 %all_to_all.21 = bf16[16,4,32,256]{3,2,0,1:T(8,128)(2,1)S(1)} all-to-all(bf16[16,4,32,256]{3,2,0,1:T(8,128)(2,1)S(1)} %fusion.6), channel_id=1, replica_groups=mesh['blk'=64,'ylo'=4,'core'=2] {'ylo'}, dimensions={1} | all-to-all | bytes 2097152 | tf_op jit(solution)/shard_map/all_to_all | solution.py:66
  260.7 0.2 reduce_sum.12
  260.9 0.9 copy.36
  261.8 0.0 reduce-scatter.2.cloned.1.call-done
Async XLA Ops:
  7.2 46.7 %copy-start = (bf16[4096,256]{1,0:T(8,128)(2,1)S(1)}, bf16[4096,256]{1,0:T(8,128)(2,1)}, u32[]{:S(2)}) copy-start(bf16[4096,256]{1,0:T(8,128)(2,1)} %param.4) | copy-start | bytes 6291460
  9.3 29.0 %all-to-all-start = ((bf16[4,32,16,256]{3,2,1,0:T(8,128)(2,1)}), bf16[4,32,16,256]{3,2,1,0:T(8,128)(2,1)S(1)}, u32[]{:S(2)}, u32[]{:S(2)}) async-start(bf16[4,32,16,256]{3,2,1,0:T(8,128)(2,1)} %broadcast_in_dim.17), calls=%async_computation | async-start | bytes 2097152 | tf_op jit(solution)/shard_map/all_to_all | solution.py:47
  14.8 47.3 %all-gather.2.cloned.1.call-start = ((), (), s32[]{:S(2)}) async-start(), calls=%async_computation.5 | async-start | bytes 2359296 | tf_op jit(solution)/shard_map/all_gather | solution.py:83
  38.4 14.1 %collective-permute-start = (bf16[4,32,16,256]{3,2,1,0:T(8,128)(2,1)S(1)}, bf16[4,32,16,256]{3,2,1,0:T(8,128)(2,1)}, u32[]{:S(2)}, u32[]{:S(2)}) collective-permute-start(bf16[4,32,16,256]{3,2,1,0:T(8,128)(2,1)S(1)} %all-to-all-done), channel_id=1, source_target_pairs={{0,1},{1,0},{2,3},{3,2},{4,5},{5,4},{6,7},{7,6},{8,9},{9,8},{10,11... | collective-permute-start | bytes 3145736 | tf_op jit(solution)/shard_map/ppermute | solution.py:48
  62.0 75.2 %copy-start.4 = (bf16[256,16,256]{2,1,0:T(8,128)(2,1)S(1)}, bf16[256,16,256]{2,1,0:T(8,128)(2,1)}, u32[]{:S(2)}) copy-start(bf16[256,16,256]{2,1,0:T(8,128)(2,1)} %all-gather.2.cloned.1.call-done) | copy-start | bytes 6291460
  137.0 2.9 %copy-start.3 = (f32[16,256,256]{2,1,0:T(8,128)S(1)}, f32[16,256,256]{2,1,0:T(8,128)}, u32[]{:S(2)}) copy-start(f32[16,256,256]{2,1,0:T(8,128)} %convert.3) | copy-start | bytes 12582916
  137.2 4.5 %copy-start.2 = (bf16[4,64,16,256]{3,2,1,0:T(8,128)(2,1)}, bf16[4,64,16,256]{3,2,1,0:T(8,128)(2,1)S(1)}, u32[]{:S(2)}) copy-start(bf16[4,64,16,256]{3,2,1,0:T(8,128)(2,1)S(1)} %copy.27) | copy-start | bytes 6291460
  141.7 1.3 copy-start.1
  144.6 73.5 %all-to-all-start.2 = ((bf16[4,64,16,256]{3,2,0,1:T(8,128)(2,1)}), bf16[4,64,16,256]{3,2,0,1:T(8,128)(2,1)}, u32[]{:S(2)}, u32[]{:S(2)}) async-start(bf16[4,64,16,256]{3,2,0,1:T(8,128)(2,1)} %copy.30), calls=%async_computation.2 | async-start | bytes 4194304 | tf_op jit(solution)/shard_map/all_to_all | solution.py:110
  153.7 108.1 %reduce-scatter.2.cloned.1.call-start = ((), (), s32[]{:S(2)}) async-start(), calls=%async_computation.6 | async-start | bytes 2359296 | tf_op jit(solution)/shard_map/reduce_scatter | solution.py:105
  222.6 6.9 %collective-permute-start.1 = (bf16[16,4,32,256]{3,2,0,1:T(8,128)(2,1)S(1)}, bf16[16,4,32,256]{3,2,0,1:T(8,128)(2,1)S(1)}, u32[]{:S(2)}, u32[]{:S(2)}) collective-permute-start(bf16[16,4,32,256]{3,2,0,1:T(8,128)(2,1)S(1)} %bitcast.56), channel_id=1, source_target_pairs={{0,1},{1,0},{2,3},{3,2},{4,5},{5,4},{6,7},{7,6},{8,9},{9,8},{10,11... | collective-permute-start | bytes 3145736 | tf_op jit(solution)/shard_map/ppermute | solution.py:64
Sparse Core Ops, SparseCore 0:
  17.7 44.2 all-gather.1
  163.0 57.9 reduce-scatter.1

commit v13 on v10

--- a/solution.py
+++ b/solution.py
@@ -52,17 +52,25 @@
     return pair.reshape((n_ylo * n_core * piece.shape[0],) + piece.shape[1:])
 
 
-def scatter_rows(term):
+def scatter_rows(inputs, pre_grad):
     n_core = lax.axis_size("core")
     n_ylo = lax.axis_size("ylo")
     c = lax.axis_index("core")
-    blocks, total_rows, width = term.shape
+    blocks, total_rows, width = inputs.shape
     rows = total_rows // (n_core * n_ylo)
-    split = term.reshape(blocks, n_ylo, n_core, rows, width)
-    sent = lax.dynamic_index_in_dim(split, lax.rem(c + 1, n_core), 2, keepdims=False)
-    kept = lax.dynamic_index_in_dim(split, c, 2, keepdims=False)
+    split = inputs.reshape(blocks, n_ylo, n_core, rows, width)
+    x_other = lax.dynamic_index_in_dim(split, lax.rem(c + 1, n_core), 2, keepdims=False)
+    x_mine = lax.dynamic_index_in_dim(split, c, 2, keepdims=False)
+    sent = jnp.einsum(
+        "bykr,bir->byki", x_other, pre_grad, preferred_element_type=jnp.float32
+    ).astype(jnp.bfloat16)
     got = lax.ppermute(sent, "core", swap_pairs(n_core))
+    kept = jnp.einsum(
+        "bykr,bir->byki", x_mine, pre_grad, preferred_element_type=jnp.float32
+    ).astype(jnp.bfloat16)
+    kept, got = lax.optimization_barrier((kept, got))
     half = (kept.astype(jnp.float32) + got.astype(jnp.float32)).astype(jnp.bfloat16)
+    half = with_layout_constraint(half, Layout((1, 0, 2, 3)))
     arrived = lax.all_to_all(half, "ylo", split_axis=1, concat_axis=1, tiled=True)
     total = jnp.sum(arrived.astype(jnp.float32), axis=1).astype(jnp.bfloat16)
     return jnp.transpose(total, (1, 0, 2))
@@ -108,11 +116,7 @@
     activated_grad = lax.all_to_all(back, "blk", split_axis=1, concat_axis=1, tiled=True)
     pre_grad = (activated_grad.astype(jnp.float32) * slope).astype(jnp.bfloat16)
     pre_grad = jnp.transpose(pre_grad, (2, 1, 0, 3)).reshape(block_count, block_size, row_count)
-    first_sum = scatter_rows(
-        jnp.einsum("bkr,bir->bki", inputs, pre_grad, preferred_element_type=jnp.float32).astype(
-            jnp.bfloat16
-        )
-    )
+    first_sum = scatter_rows(inputs, pre_grad)
     return (first_sum, second_out)
 
 

time: 267 us -> 270 us (1.011)
  waiting for transfers between devices: 81 us -> 66.2 us
  blocking collectives: 106 us -> 120 us
  starting transfers between devices: 31.5 us -> 34.4 us
    all_to_all x1, blocking collectives: 31.6 us -> 53.5 us  [scatter_rows(): lax.all_to_all(half, 'ylo', split_axis=1, concat_axis=1, tiled=True)]
    all_to_all x1, waiting for transfers between devices: 51 us -> 35.6 us  [shards(): lax.all_to_all(back, 'blk', split_axis=1, concat_axis=1, tiled=True)]
    all_to_all x1, blocking collectives: 73.9 us -> 66.9 us  [shards(): lax.all_to_all(sending, 'blk', split_axis=1, concat_axis=1, tiled=True)]
    all_to_all x1, starting transfers between devices: 7.73 us -> 12.8 us  [shards(): lax.all_to_all(back, 'blk', split_axis=1, concat_axis=1, tiled=True)]
where the time goes in v13:
time: 270 us
  blocking collectives  120 us (44%)
  waiting for transfers between devices  66.2 us (25%)
  starting transfers between devices  34.4 us (13%)
  local copies, waits for them, and re-layouts  17.6 us (7%)
  between operations  14.2 us (5%)
  matrix products  9.5 us (4%)
  other arithmetic  7.5 us (3%)
    all_to_all x1, blocking collectives, shards(): lax.all_to_all(sending, 'blk', split_axis=1, concat_axis=1, tiled=True)  66.9 us
    all_to_all x1, blocking collectives, scatter_rows(): lax.all_to_all(half, 'ylo', split_axis=1, concat_axis=1, tiled=True)  53.5 us
    all_to_all x1, waiting for transfers between devices, shards(): lax.all_to_all(back, 'blk', split_axis=1, concat_axis=1, tiled=True)  35.6 us
    all_to_all x1, waiting for transfers between devices, gather_rows(): lax.all_to_all(copies, 'ylo', split_axis=0, concat_axis=0, tiled=True)  22.9 us
    all_to_all x1, starting transfers between devices, shards(): lax.all_to_all(back, 'blk', split_axis=1, concat_axis=1, tiled=True)  12.8 us
    ppermute x1, starting transfers between devices, gather_rows(): other = lax.ppermute(line, 'core', swap_pairs(n_core))  9.84 us
    ppermute x1, starting transfers between devices, scatter_rows(): got = lax.ppermute(sent, 'core', swap_pairs(n_core))  6.12 us
    all_to_all x1, starting transfers between devices, gather_rows(): lax.all_to_all(copies, 'ylo', split_axis=0, concat_axis=0, tiled=True)  5.42 us
  transfers between devices with their start and end apart: 6, of which 5 were waited for; matrix products, arithmetic and copies ran while one was open for 9% of the time, Pallas kernels for 0%

profile of v13, /device:TPU:1, one launch (start us, length us, event | category | flops | bytes accessed | tf_op | source)
XLA Modules:
  0.0 269.8 jit_solution(15014780799550700285)
XLA Ops:
  7.2 2.0 broadcast_in_dim.17
  9.2 5.4 %all-to-all-start = ((bf16[4,32,16,256]{3,2,1,0:T(8,128)(2,1)}), bf16[4,32,16,256]{3,2,1,0:T(8,128)(2,1)S(1)}, u32[]{:S(2)}, u32[]{:S(2)}) async-start(bf16[4,32,16,256]{3,2,1,0:T(8,128)(2,1)} %broadcast_in_dim.17), calls=%async_computation | async-start | bytes 2097152 | tf_op jit(solution)/shard_map/all_to_all | solution.py:47
  14.6 0.0 all-gather.2.cloned.1.call-start
  14.6 0.7 all-gather.2.cloned.1.call-update
  15.3 22.9 %all-to-all-done = bf16[4,32,16,256]{3,2,1,0:T(8,128)(2,1)S(1)} async-done(((bf16[4,32,16,256]{3,2,1,0:T(8,128)(2,1)}), bf16[4,32,16,256]{3,2,1,0:T(8,128)(2,1)S(1)}, u32[]{:S(2)}, u32[]{:S(2)}) %all-to-all-start) | async-done | bytes 1048608 | tf_op jit(solution)/shard_map/all_to_all | solution.py:47
  38.2 9.8 %collective-permute-start = (bf16[4,32,16,256]{3,2,1,0:T(8,128)(2,1)S(1)}, bf16[4,32,16,256]{3,2,1,0:T(8,128)(2,1)S(1)}, u32[]{:S(2)}, u32[]{:S(2)}) collective-permute-start(bf16[4,32,16,256]{3,2,1,0:T(8,128)(2,1)S(1)} %all-to-all-done), channel_id=1, source_target_pairs={{0,1},{1,0},{2,3},{3,2},{4,5},{5,4},{6,7},{7,6},{8,9},{9,8},{10,11... | collective-permute-start | bytes 3145736 | tf_op jit(solution)/shard_map/ppermute | solution.py:48
  48.1 0.2 broadcast_in_dim.16
  48.3 0.0 copy-start.1
  48.3 0.1 bitcast_dynamic-update-slice_fusion.1
  48.4 2.0 collective-permute-done
  50.3 0.1 bitcast_dynamic-update-slice_fusion
  50.4 0.0 copy-done.1
  50.4 1.5 fusion.12
  51.9 2.4 copy.37
  54.4 3.8 %fusion.14 = (bf16[4,64,16,256]{3,2,0,1:T(8,128)(2,1)}, bf16[16,64,4,256]{3,0,2,1:T(8,128)(2,1)S(1)}) fusion(f32[16,64,4,256]{3,0,2,1:T(8,128)S(1)} %bitcast.51), kind=kLoop, calls=%fused_computation.21 | loop fusion | flops 20971520 | bytes 8388608 | tf_op jit(solution)/shard_map/transpose | solution.py:95
  58.2 3.6 %all-gather.2.cloned.1.call-done = bf16[256,16,256]{2,1,0:T(8,128)(2,1)} async-done(((bf16[32,16,256]{2,1,0:T(8,128)(2,1)}), bf16[256,16,256]{2,1,0:T(8,128)(2,1)}) %all-gather.2.cloned.1.call-update) | async-done | bytes 2097168 | tf_op jit(solution)/shard_map/all_gather | solution.py:91
  61.8 66.9 %all_to_all.20 = bf16[4,64,16,256]{3,2,0,1:T(8,128)(2,1)S(1)} all-to-all(bf16[4,64,16,256]{3,2,0,1:T(8,128)(2,1)S(1)} %bitcast.57), channel_id=1, replica_groups=mesh['blk'=64,'ylo'=4,'core'=2] {'blk'}, dimensions={1} | all-to-all | bytes 4194304 | tf_op jit(solution)/shard_map/all_to_all | solution.py:99
  128.7 0.0 copy-start.3
  128.7 0.0 copy-start.4
  128.7 0.2 copy.38
  128.9 0.0 copy-start
  128.9 2.2 copy-done.3
  131.1 0.6 copy-done.4
  131.7 1.7 fusion.7
  133.4 0.0 copy-done
  133.4 0.9 convolution_convert_fusion
  134.3 1.6 copy.41
  135.9 12.8 %all-to-all-start.2 = ((bf16[4,64,16,256]{3,2,0,1:T(8,128)(2,1)}), bf16[4,64,16,256]{3,2,0,1:T(8,128)(2,1)}, u32[]{:S(2)}, u32[]{:S(2)}) async-start(bf16[4,64,16,256]{3,2,0,1:T(8,128)(2,1)} %copy.41), calls=%async_computation.2 | async-start | bytes 4194304 | tf_op jit(solution)/shard_map/all_to_all | solution.py:116
  148.7 0.2 reduce-scatter.2.cloned.1.call-start
  148.9 3.7 %convert_bitcast_fusion = bf16[256,16,256]{0,2,1:T(8,128)(2,1)} fusion(bf16[16,256,256]{2,1,0:T(8,128)(2,1)S(1)} %fusion.7, bf16[16,256,256]{2,1,0:T(8,128)(2,1)} %bitcast.50), kind=kOutput, calls=%fused_computation.19 | convolution fusion | flops 537919488 | bytes 6291456 | tf_op jit(solution)/shard_map/qcr,qjr->cqj/dot_general | solution.py:110
  152.7 4.6 %copy.47 = bf16[256,16,256]{2,1,0:T(8,128)(2,1)} copy(bf16[256,16,256]{0,2,1:T(8,128)(2,1)} %convert_bitcast_fusion) | data formatting | bytes 4194304 | tf_op jit(solution)/shard_map/convert_element_type | solution.py:112
  157.2 0.0 copy-start.2
  157.2 0.0 reduce-scatter.2.cloned.1.call-update
  157.3 1.6 copy-done.2
  158.8 1.2 dynamic-slice_bitcast_fusion
  160.1 0.0 copy-start.5
  160.1 35.6 %all-to-all-done.2 = bf16[4,64,16,256]{3,2,0,1:T(8,128)(2,1)} async-done(((bf16[4,64,16,256]{3,2,0,1:T(8,128)(2,1)}), bf16[4,64,16,256]{3,2,0,1:T(8,128)(2,1)}, u32[]{:S(2)}, u32[]{:S(2)}) %all-to-all-start.2) | async-done | bytes 2097184 | tf_op jit(solution)/shard_map/all_to_all | solution.py:116
  195.7 3.1 %multiply_convert_fusion = bf16[4,64,16,256]{3,2,0,1:T(8,128)(2,1)S(1)} fusion(bf16[4,64,16,256]{3,2,0,1:T(8,128)(2,1)} %get-tuple-element.9, bf16[4,64,16,256]{3,2,0,1:T(8,128)(2,1)} %all-to-all-done.2), kind=kLoop, calls=%fused_computation.11 | loop fusion | flops 4194304 | bytes 6291456 | tf_op jit(solution)/shard_map/convert_element_type | solution.py:117
  198.7 0.0 copy-done.5
  198.7 0.9 fusion.22
  199.6 6.1 %collective-permute-start.1 = (bf16[16,4,32,256]{3,2,0,1:T(8,128)(2,1)S(1)}, bf16[16,4,32,256]{3,2,0,1:T(8,128)(2,1)S(1)}, u32[]{:S(2)}, u32[]{:S(2)}) collective-permute-start(bf16[16,4,32,256]{3,2,0,1:T(8,128)(2,1)S(1)} %fusion.22), channel_id=1, source_target_pairs={{0,1},{1,0},{2,3},{3,2},{4,5},{5,4},{6,7},{7,6},{8,9},{9,8},{10,11... | collective-permute-start | bytes 3145736 | tf_op jit(solution)/shard_map/ppermute | solution.py:67
  205.7 0.9 fusion.19
  206.6 1.4 collective-permute-done.1
  208.0 0.4 add_convert_fusion
  208.4 53.5 %all_to_all.21 = bf16[16,4,32,256]{3,2,0,1:T(8,128)(2,1)S(1)} all-to-all(bf16[16,4,32,256]{3,2,0,1:T(8,128)(2,1)S(1)} %add_convert_fusion), channel_id=1, replica_groups=mesh['blk'=64,'ylo'=4,'core'=2] {'ylo'}, dimensions={1} | all-to-all | bytes 2097152 | tf_op jit(solution)/shard_map/all_to_all | solution.py:74
  261.9 0.2 reduce_sum.12
  262.1 0.9 copy.48
  263.0 0.0 reduce-scatter.2.cloned.1.call-done
Async XLA Ops:
  9.2 29.0 %all-to-all-start = ((bf16[4,32,16,256]{3,2,1,0:T(8,128)(2,1)}), bf16[4,32,16,256]{3,2,1,0:T(8,128)(2,1)S(1)}, u32[]{:S(2)}, u32[]{:S(2)}) async-start(bf16[4,32,16,256]{3,2,1,0:T(8,128)(2,1)} %broadcast_in_dim.17), calls=%async_computation | async-start | bytes 2097152 | tf_op jit(solution)/shard_map/all_to_all | solution.py:47
  14.6 47.2 %all-gather.2.cloned.1.call-start = ((), (), s32[]{:S(2)}) async-start(), calls=%async_computation.5 | async-start | bytes 2359296 | tf_op jit(solution)/shard_map/all_gather | solution.py:91
  38.2 12.1 %collective-permute-start = (bf16[4,32,16,256]{3,2,1,0:T(8,128)(2,1)S(1)}, bf16[4,32,16,256]{3,2,1,0:T(8,128)(2,1)S(1)}, u32[]{:S(2)}, u32[]{:S(2)}) collective-permute-start(bf16[4,32,16,256]{3,2,1,0:T(8,128)(2,1)S(1)} %all-to-all-done), channel_id=1, source_target_pairs={{0,1},{1,0},{2,3},{3,2},{4,5},{5,4},{6,7},{7,6},{8,9},{9,8},{10,11... | collective-permute-start | bytes 3145736 | tf_op jit(solution)/shard_map/ppermute | solution.py:48
  48.3 2.2 copy-start.1
  128.7 2.3 copy-start.3
  128.7 3.0 %copy-start.4 = (bf16[4096,256]{1,0:T(8,128)(2,1)S(1)}, bf16[4096,256]{1,0:T(8,128)(2,1)}, u32[]{:S(2)}) copy-start(bf16[4096,256]{1,0:T(8,128)(2,1)} %param.5) | copy-start | bytes 6291460
  128.9 4.5 %copy-start = (bf16[4,64,16,256]{3,2,1,0:T(8,128)(2,1)}, bf16[4,64,16,256]{3,2,1,0:T(8,128)(2,1)S(1)}, u32[]{:S(2)}) copy-start(bf16[4,64,16,256]{3,2,1,0:T(8,128)(2,1)S(1)} %copy.38) | copy-start | bytes 6291460
  135.9 59.8 %all-to-all-start.2 = ((bf16[4,64,16,256]{3,2,0,1:T(8,128)(2,1)}), bf16[4,64,16,256]{3,2,0,1:T(8,128)(2,1)}, u32[]{:S(2)}, u32[]{:S(2)}) async-start(bf16[4,64,16,256]{3,2,0,1:T(8,128)(2,1)} %copy.41), calls=%async_computation.2 | async-start | bytes 4194304 | tf_op jit(solution)/shard_map/all_to_all | solution.py:116
  148.7 114.3 %reduce-scatter.2.cloned.1.call-start = ((), (), s32[]{:S(2)}) async-start(), calls=%async_computation.6 | async-start | bytes 2359296 | tf_op jit(solution)/shard_map/reduce_scatter | solution.py:111
  157.2 1.6 copy-start.2
  160.1 38.7 %copy-start.5 = (bf16[16,4,32,256]{3,2,1,0:T(8,128)(2,1)S(1)}, bf16[16,4,32,256]{3,2,1,0:T(8,128)(2,1)}, u32[]{:S(2)}) copy-start(bf16[16,4,32,256]{3,2,1,0:T(8,128)(2,1)} %get-tuple-element.20) | copy-start | bytes 3145732
  199.6 8.4 %collective-permute-start.1 = (bf16[16,4,32,256]{3,2,0,1:T(8,128)(2,1)S(1)}, bf16[16,4,32,256]{3,2,0,1:T(8,128)(2,1)S(1)}, u32[]{:S(2)}, u32[]{:S(2)}) collective-permute-start(bf16[16,4,32,256]{3,2,0,1:T(8,128)(2,1)S(1)} %fusion.22), channel_id=1, source_target_pairs={{0,1},{1,0},{2,3},{3,2},{4,5},{5,4},{6,7},{7,6},{8,9},{9,8},{10,11... | collective-permute-start | bytes 3145736 | tf_op jit(solution)/shard_map/ppermute | solution.py:67
Sparse Core Ops, SparseCore 0:
  17.5 44.2 all-gather.1
  157.4 60.2 reduce-scatter.1
